TPU v7x, 512 devices: a whole 4x4x16 slice. The times are simulated.
512 devices in a mesh: dp: 64 (over z, x), pair: 8 (over y, core).
Axes of the slice: x: 4, y: 4, z: 16, core: 2. Of those that a mesh axis runs over, the one named last changes fastest.
Arguments:
- embedding: bfloat16 [65536, 1024], P(('dp', 'pair')), may hold values from -32 to 32
- labels: int32 [65536], P(('dp', 'pair')), may hold values from 0 to 127, as said below
- order_ids: int32 [65536], P(('dp', 'pair')), may hold values from 0 to 65535, each once
Outputs:
- best_similarity: float32 [65536], P(('dp', 'pair'))
Inputs may be any that keep to these rules, and one draw needn't show every extreme that they name: `labels`: clusters 2 * g to 2 * g + 1 form owner group g. Among the 128 rows of one device (aligned blocks of the whole array) at most 4 name clusters of any one group, and in every draw some group gets exactly 4 rows from every device.
All inputs are finite; a program needn't handle non-finite values.
Results may differ from a plain program's by a relative error of at most 0.00049.
Values may be sent and summed in bfloat16 or wider, within the bound.
No kernel may reach another device: no remote copies, remote signals or barrier semaphores. Data moves between devices by JAX's collectives and lax.ppermute only.
A program may use at most 64 MiB of HBM per device.

v0:
```python
import jax
import jax.numpy as jnp
from jax import lax
from jax.sharding import PartitionSpec as P

CL_OWN = 2


def tile_best(own_rows, own_labels, own_order, other_rows, other_labels, other_order):
    scores = jnp.dot(own_rows, other_rows.T, preferred_element_type=jnp.float32)
    same_cluster = (other_labels[None, :] == own_labels[:, None]) & (own_labels[:, None] >= 0)
    earlier = same_cluster & (other_order[None, :] < own_order[:, None])
    after_own = same_cluster & (own_order[:, None] < other_order[None, :])
    ahead = jnp.max(jnp.where(earlier, scores, -1.0), axis=1)
    behind = jnp.max(jnp.where(after_own, scores, -1.0), axis=0)
    return (ahead, behind)


def on_device(embedding, labels, order_ids):
    groups = lax.axis_size("dp")
    rows_here = embedding.shape[0]
    capacity = 2 * rows_here // groups
    slot_count = groups * capacity
    values = embedding.astype(jnp.float32)
    squares = jnp.sum(values * values, axis=1, keepdims=True)
    shifted = squares + 1e-06
    unit_rows = (values * lax.rsqrt(shifted)).astype(jnp.bfloat16)
    owner_group = labels // CL_OWN
    onehot = (owner_group[:, None] == jnp.arange(groups, dtype=jnp.int32)[None, :]).astype(
        jnp.int32
    )
    before = jnp.cumsum(onehot, axis=0) - onehot
    slot_index = owner_group * capacity + jnp.sum(before * onehot, axis=1)
    send_rows = (
        jnp.zeros((slot_count, unit_rows.shape[1]), jnp.bfloat16).at[slot_index].set(unit_rows)
    )
    send_labels = jnp.full((slot_count,), -1, jnp.int32).at[slot_index].set(labels)
    send_order = jnp.zeros((slot_count,), jnp.int32).at[slot_index].set(order_ids)
    got_rows, got_labels, got_order = (
        lax.all_to_all(
            send_rows.reshape(groups, capacity, -1), "dp", split_axis=0, concat_axis=0, tiled=True
        ),
        lax.all_to_all(
            send_labels.reshape(groups, capacity), "dp", split_axis=0, concat_axis=0, tiled=True
        ),
        lax.all_to_all(
            send_order.reshape(groups, capacity), "dp", split_axis=0, concat_axis=0, tiled=True
        ),
    )
    got_rows = got_rows.reshape(slot_count, -1)
    got_labels = got_labels.reshape(slot_count)
    got_order = got_order.reshape(slot_count)
    best_seen = jnp.full((slot_count,), -1.0, jnp.float32)
    piece = (
        lax.all_gather(got_rows, "pair", axis=0, tiled=True),
        lax.all_gather(got_labels, "pair", axis=0, tiled=True),
        lax.all_gather(got_order, "pair", axis=0, tiled=True),
    )
    piece_count = piece[0].shape[0]
    for offset in range(0, piece_count, 512):
        width_now = min(512, piece_count - offset)
        found = tile_best(
            got_rows,
            got_labels,
            got_order,
            piece[0][offset : offset + width_now],
            piece[1][offset : offset + width_now],
            piece[2][offset : offset + width_now],
        )
        best_seen = jnp.maximum(best_seen, found[0])
    answered = lax.all_to_all(
        best_seen.reshape(groups, capacity), "dp", split_axis=0, concat_axis=0, tiled=True
    )
    return answered.reshape(slot_count)[slot_index]


def solution(mesh):
    in_specs = (P(("dp", "pair"), None), P(("dp", "pair")), P(("dp", "pair")))
    out_specs = P(("dp", "pair"))
    return jax.shard_map(
        on_device, mesh=mesh, in_specs=in_specs, out_specs=out_specs, check_vma=False
    )
```

profile of v0, /device:TPU:1, one launch (start us, length us, event | category | flops | bytes accessed | tf_op | source)
XLA Modules:
  0.0 161.6 jit_solution(7379392571141710078)
XLA Ops:
  7.2 1.1 fusion.8
  8.7 0.7 compare_select_fusion
  9.4 1.8 %scatter_custom_fusion.2 = bf16[256,1024]{1,0:T(8,128)(2,1)S(1)} fusion(s32[128]{0:T(128)S(1)} %compare_select_fusion, bf16[128,1024]{1,0:T(8,128)(2,1)} %param.3, f32[128]{0:T(128)S(1)} %add_rsqrt_fusion, bf16[]{:T(256)} %constant.18.clone.1), kind=kCustom, calls=%fused_computation.20 | custom fusion | flops 393216 | bytes 786946 | tf_op jit(solution)/shard_map/scatter | solution.py:35
  11.4 48.9 %all_to_all.29 = bf16[64,4,1024]{2,1,0:T(4,128)(2,1)S(1)} all-to-all(bf16[64,4,1024]{2,1,0:T(4,128)(2,1)S(1)} %reshape.107), channel_id=1, replica_groups=mesh['dp'=64,'pair'=8] {'dp'}, dimensions={0} | all-to-all | bytes 1048576 | tf_op jit(solution)/shard_map/all_to_all | solution.py:40
  60.3 0.9 reshape.108
  61.3 1.2 scatter_custom_fusion
  62.5 0.7 all_to_all.19
  63.2 7.9 %all-to-all-start = ((s32[64,1,4]{2,1,0:T(1,128)}), s32[64,1,4]{2,1,0:T(1,128)S(1)}, u32[]{:S(2)}, u32[]{:S(2)}) async-start(s32[64,1,4]{2,1,0:T(1,128)} %bitcast), calls=%async_computation | async-start | bytes 65536 | tf_op jit(solution)/shard_map/all_to_all | solution.py:43
  71.1 1.1 scatter_custom_fusion.1
  72.2 0.7 all_to_all.21
  72.9 11.8 %all-to-all-done = s32[64,1,4]{2,1,0:T(1,128)S(1)} async-done(((s32[64,1,4]{2,1,0:T(1,128)}), s32[64,1,4]{2,1,0:T(1,128)S(1)}, u32[]{:S(2)}, u32[]{:S(2)}) %all-to-all-start) | async-done | bytes 1056 | tf_op jit(solution)/shard_map/all_to_all | solution.py:43
  84.7 4.5 %all-to-all-start.1 = ((s32[64,1,4]{2,1,0:T(1,128)}), s32[64,1,4]{2,1,0:T(1,128)S(1)}, u32[]{:S(2)}, u32[]{:S(2)}) async-start(s32[64,1,4]{2,1,0:T(1,128)} %bitcast.2), calls=%async_computation.1 | async-start | bytes 65536 | tf_op jit(solution)/shard_map/all_to_all | solution.py:46
  89.3 13.5 %all-to-all-done.1 = s32[64,1,4]{2,1,0:T(1,128)S(1)} async-done(((s32[64,1,4]{2,1,0:T(1,128)}), s32[64,1,4]{2,1,0:T(1,128)S(1)}, u32[]{:S(2)}, u32[]{:S(2)}) %all-to-all-start.1) | async-done | bytes 1056 | tf_op jit(solution)/shard_map/all_to_all | solution.py:46
  103.4 0.7 reduce.13
  104.2 0.7 reduce.14
  105.1 14.6 %all-gather = s32[8,1,256]{2,1,0:T(1,128)S(1)} all-gather(s32[1,1,256]{2,1,0:T(1,128)S(1)} %reshape.146), channel_id=1, replica_groups=mesh['dp'=64,'pair'=8] {'pair'}, dimensions={0}, use_global_device_ids=true | all-gather | bytes 9216 | tf_op jit(solution)/shard_map/all_gather | solution.py:56
  119.6 8.1 %all-gather.1 = s32[8,1,256]{2,1,0:T(1,128)S(1)} all-gather(s32[1,1,256]{2,1,0:T(1,128)S(1)} %reshape.148), channel_id=1, replica_groups=mesh['dp'=64,'pair'=8] {'pair'}, dimensions={0}, use_global_device_ids=true | all-gather | bytes 9216 | tf_op jit(solution)/shard_map/all_gather | solution.py:57
  127.8 2.1 %fusion.3 = f32[256]{0:T(256)S(1)} fusion(bf16[256,1024]{1,0:T(8,128)(2,1)} %reshape.108, bf16[2048,1024]{1,0:T(8,128)(2,1)} %all-gather.4.cloned.1.call-done, s32[512]{0:T(512)S(1)} %bitcast.29, s32[512]{0:T(512)S(1)} %bitcast.26, pred[256]{0:T(512)(128)(4,1)S(1)} %broadcast_compare_fusion, s32[256]{0:T(256)S(1)} %reshape.106, s32[256]{0:T(256)S(1)} %reshape.105), kind=kOutput, calls=%fused_computation.11 | convolution fusion | flops 269221632 | bytes 1580288 | tf_op jit(solution)/shard_map/dot_general | solution.py:10
  129.9 1.8 %fusion.2 = f32[256]{0:T(256)S(1)} fusion(bf16[256,1024]{1,0:T(8,128)(2,1)S(1)} %copy-done, bf16[2048,1024]{1,0:T(8,128)(2,1)} %all-gather.4.cloned.1.call-done, s32[512]{0:T(512)S(1)} %bitcast.28, s32[512]{0:T(512)S(1)} %bitcast.25, pred[256]{0:T(512)(128)(4,1)S(1)} %broadcast_compare_fusion, s32[256]{0:T(256)S(1)} %reshape.106, s32[256]{0:T(256)S(1)} %reshape.105), kind=kOutput, calls=%fused_computation.10 | convolution fusion | flops 269221632 | bytes 1580288 | tf_op jit(solution)/shard_map/dot_general | solution.py:10
  132.9 0.7 max.41
  133.6 4.6 %all-to-all-start.3 = ((f32[64,1,4]{2,1,0:T(1,128)}), f32[64,1,4]{2,1,0:T(1,128)S(1)}, u32[]{:S(2)}, u32[]{:S(2)}) async-start(f32[64,1,4]{2,1,0:T(1,128)} %bitcast.10), calls=%async_computation.3 | async-start | bytes 65536 | tf_op jit(solution)/shard_map/all_to_all | solution.py:71
  138.3 13.4 %all-to-all-done.3 = f32[64,1,4]{2,1,0:T(1,128)S(1)} async-done(((f32[64,1,4]{2,1,0:T(1,128)}), f32[64,1,4]{2,1,0:T(1,128)S(1)}, u32[]{:S(2)}, u32[]{:S(2)}) %all-to-all-start.3) | async-done | bytes 1056 | tf_op jit(solution)/shard_map/all_to_all | solution.py:71
  152.2 0.7 reduce.15
  153.0 1.8 %gather_fusion = f32[128]{0:T(128)} fusion(f32[256]{0:T(256)S(1)} %reshape.109, s32[1024]{0:T(1024)S(1)} %pad_clamp_fusion), kind=kCustom, calls=%fused_computation | custom fusion | bytes 1536 | tf_op jit(solution)/shard_map/gather | solution.py:74
  (27 shorter events, 4.1 us)
Async XLA Ops:
  6.5 121.3 %all-gather.4.cloned.1.call-start = ((), (), s32[]{:S(2)}) async-start(), calls=%async_computation.4 | async-start | bytes 4718592 | tf_op jit(solution)/shard_map/all_gather | solution.py:55
  61.3 68.7 %copy-start = (bf16[256,1024]{1,0:T(8,128)(2,1)S(1)}, bf16[256,1024]{1,0:T(8,128)(2,1)}, u32[]{:S(2)}) copy-start(bf16[256,1024]{1,0:T(8,128)(2,1)} %reshape.108) | copy-start | bytes 1572868
  63.2 21.5 %all-to-all-start = ((s32[64,1,4]{2,1,0:T(1,128)}), s32[64,1,4]{2,1,0:T(1,128)S(1)}, u32[]{:S(2)}, u32[]{:S(2)}) async-start(s32[64,1,4]{2,1,0:T(1,128)} %bitcast), calls=%async_computation | async-start | bytes 65536 | tf_op jit(solution)/shard_map/all_to_all | solution.py:43
  84.7 18.1 %all-to-all-start.1 = ((s32[64,1,4]{2,1,0:T(1,128)}), s32[64,1,4]{2,1,0:T(1,128)S(1)}, u32[]{:S(2)}, u32[]{:S(2)}) async-start(s32[64,1,4]{2,1,0:T(1,128)} %bitcast.2), calls=%async_computation.1 | async-start | bytes 65536 | tf_op jit(solution)/shard_map/all_to_all | solution.py:46
  127.8 3.9 %copy-start.1 = (bf16[2048,1024]{1,0:T(8,128)(2,1)S(1)}, bf16[2048,1024]{1,0:T(8,128)(2,1)}, u32[]{:S(2)}) copy-start(bf16[2048,1024]{1,0:T(8,128)(2,1)} %all-gather.4.cloned.1.call-done) | copy-start | bytes 12582916
  133.6 18.0 %all-to-all-start.3 = ((f32[64,1,4]{2,1,0:T(1,128)}), f32[64,1,4]{2,1,0:T(1,128)S(1)}, u32[]{:S(2)}, u32[]{:S(2)}) async-start(f32[64,1,4]{2,1,0:T(1,128)} %bitcast.10), calls=%async_computation.3 | async-start | bytes 65536 | tf_op jit(solution)/shard_map/all_to_all | solution.py:71
Sparse Core Ops, SparseCore 0:
  61.4 35.0 all-gather.3
where the time goes:
time: 162 us
  blocking collectives  71.6 us (44%)
  waiting for transfers between devices  38.7 us (24%)
  starting transfers between devices  17 us (10%)
  between operations  13.5 us (8%)
  local copies, waits for them, and re-layouts  8.9 us (5%)
  other arithmetic  6.85 us (4%)
  matrix products  5.07 us (3%)
    all_to_all x1, blocking collectives, on_device(): lax.all_to_all(send_rows.reshape(groups, capacity, -1), 'dp', split_axis=...  48.9 us
    all_gather x1, blocking collectives, on_device(): lax.all_gather(got_labels, 'pair', axis=0, tiled=True)  14.6 us
    all_to_all x1, waiting for transfers between devices, on_device(): lax.all_to_all(send_order.reshape(groups, capacity), 'dp', split_axis=0,...  13.5 us
    all_to_all x1, waiting for transfers between devices, on_device(): lax.all_to_all(best_seen.reshape(groups, capacity), 'dp', split_axis=0, c...  13.4 us
    all_to_all x1, waiting for transfers between devices, on_device(): lax.all_to_all(send_labels.reshape(groups, capacity), 'dp', split_axis=0,...  11.8 us
    all_gather x1, blocking collectives, on_device(): lax.all_gather(got_order, 'pair', axis=0, tiled=True)  8.1 us
    all_to_all x1, starting transfers between devices, on_device(): lax.all_to_all(send_labels.reshape(groups, capacity), 'dp', split_axis=0,...  7.86 us
    dot_general x4, matrix products, tile_best(): scores = jnp.dot(own_rows, other_rows.T, preferred_element_type=jnp.float32)  5.07 us
  transfers between devices with their start and end apart: 4, of which 3 were waited for; matrix products, arithmetic and copies ran while one was open for 3% of the time, Pallas kernels for 0%

commit v1 on v0

v1 whole, which is shorter than its diff:
```python
import jax
import jax.numpy as jnp
from jax import lax
from jax.sharding import PartitionSpec as P

CL_OWN = 2
META = 128


def tile_best(own_rows, own_key, other_rows, other_key, rows_total):
    scores = jnp.dot(own_rows, other_rows.T, preferred_element_type=jnp.float32)
    same_cluster = (other_key[None, :] // rows_total) == (own_key[:, None] // rows_total)
    earlier = same_cluster & (other_key[None, :] < own_key[:, None])
    return jnp.max(jnp.where(earlier, scores, -1.0), axis=1)


def slot_keys(rows, width, rows_total):
    meta = rows[:, width : width + 3].astype(jnp.int32)
    return meta[:, 0] * rows_total + meta[:, 1] * 256 + meta[:, 2]


def on_device(embedding, labels, order_ids):
    groups = lax.axis_size("dp")
    pairs = lax.axis_size("pair")
    rows_here, width = embedding.shape
    rows_total = rows_here * groups * pairs
    capacity = 2 * rows_here // groups
    slot_count = groups * capacity
    values = embedding.astype(jnp.float32)
    squares = jnp.sum(values * values, axis=1, keepdims=True)
    shifted = squares + 1e-06
    unit_rows = (values * lax.rsqrt(shifted)).astype(jnp.bfloat16)
    owner_group = labels // CL_OWN
    onehot = (owner_group[:, None] == jnp.arange(groups, dtype=jnp.int32)[None, :]).astype(
        jnp.int32
    )
    before = jnp.cumsum(onehot, axis=0) - onehot
    slot_index = owner_group * capacity + jnp.sum(before * onehot, axis=1)
    meta = jnp.stack([labels + 1, order_ids // 256, order_ids % 256], axis=1).astype(jnp.bfloat16)
    meta = jnp.pad(meta, ((0, 0), (0, META - 3)))
    packed = jnp.concatenate([unit_rows, meta], axis=1)
    send_rows = jnp.zeros((slot_count, width + META), jnp.bfloat16).at[slot_index].set(packed)
    got_rows = lax.all_to_all(
        send_rows.reshape(groups, capacity, -1), "dp", split_axis=0, concat_axis=0, tiled=True
    ).reshape(slot_count, -1)
    piece_rows = lax.all_gather(got_rows, "pair", axis=0, tiled=True)
    got_key = slot_keys(got_rows, width, rows_total)
    piece_key = slot_keys(piece_rows, width, rows_total)
    column = lax.broadcasted_iota(jnp.int32, got_rows.shape, 1)
    query_rows = jnp.where(column < width, got_rows, jnp.zeros_like(got_rows))
    best_seen = jnp.full((slot_count,), -1.0, jnp.float32)
    piece_count = piece_rows.shape[0]
    for offset in range(0, piece_count, 512):
        width_now = min(512, piece_count - offset)
        found = tile_best(
            query_rows,
            got_key,
            piece_rows[offset : offset + width_now],
            piece_key[offset : offset + width_now],
            rows_total,
        )
        best_seen = jnp.maximum(best_seen, found)
    answered = lax.all_to_all(
        best_seen.reshape(groups, capacity), "dp", split_axis=0, concat_axis=0, tiled=True
    )
    return answered.reshape(slot_count)[slot_index]


def solution(mesh):
    in_specs = (P(("dp", "pair"), None), P(("dp", "pair")), P(("dp", "pair")))
    out_specs = P(("dp", "pair"))
    return jax.shard_map(
        on_device, mesh=mesh, in_specs=in_specs, out_specs=out_specs, check_vma=False
    )
```

time: 162 us -> 147 us (0.907)
  blocking collectives: 71.6 us -> 51.3 us
  waiting for transfers between devices: 38.7 us -> 50.3 us
  local copies, waits for them, and re-layouts: 8.9 us -> 4.9 us
  matrix products: 5.07 us -> 2.55 us
  other arithmetic: 6.85 us -> 9.14 us
  starting transfers between devices: 17 us -> 15.3 us
    all_gather x1, waiting for transfers between devices: 0.02 us -> 36.7 us  [on_device(): piece_rows = lax.all_gather(got_rows, 'pair', axis=0, tiled=True)]
    all_to_all x2 -> x0, waiting for transfers between devices: 25.2 us -> none  [the longest x1 13.5 us: on_device(): lax.all_to_all(send_order.reshape(groups, capacity), 'dp', split_axis=0,...]
    all_gather x2 -> x0, blocking collectives: 22.7 us -> none  [the longest x1 14.6 us: on_device(): lax.all_gather(got_labels, 'pair', axis=0, tiled=True)]
    all_to_all x2 -> x0, starting transfers between devices: 12.4 us -> none  [the longest x1 7.86 us: on_device(): lax.all_to_all(send_labels.reshape(groups, capacity), 'dp', split_axis=0,...]
    all_to_all x1, starting transfers between devices: 4.61 us -> 15.3 us  [on_device(): lax.all_to_all(best_seen.reshape(groups, capacity), 'dp', split_axis=0, c...]
    convert_element_type x0 -> x3, other arithmetic: none -> 3.27 us  [the longest x2 2.21 us: slot_keys(): meta = rows[:, width:width + 3].astype(jnp.int32)]
    dot_general x4, matrix products: 5.07 us -> 2.55 us  [tile_best(): scores = jnp.dot(own_rows, other_rows.T, preferred_element_type=jnp.float32)]
    scatter x2 -> x0, local copies, waits for them, and re-layouts: 2.35 us -> none  [the longest x1 1.24 us: on_device(): jnp.full((slot_count,), -1, jnp.int32).at[slot_index].set(labels)]
  transfers between devices with their start and end apart: 4 -> 2, of which waited for: 3 -> 2; matrix products, arithmetic and copies ran while one was open for 3% -> 1% of each run, Pallas kernels for 0% -> 0%
where the time goes in v1:
time: 147 us
  blocking collectives  51.3 us (35%)
  waiting for transfers between devices  50.3 us (34%)
  starting transfers between devices  15.3 us (10%)
  between operations  13.5 us (9%)
  other arithmetic  9.14 us (6%)
  local copies, waits for them, and re-layouts  4.9 us (3%)
  matrix products  2.55 us (2%)
    all_to_all x1, blocking collectives, on_device(): lax.all_to_all(send_rows.reshape(groups, capacity, -1), 'dp', split_axis=...  51.3 us
    all_gather x1, waiting for transfers between devices, on_device(): piece_rows = lax.all_gather(got_rows, 'pair', axis=0, tiled=True)  36.7 us
    all_to_all x1, starting transfers between devices, on_device(): lax.all_to_all(best_seen.reshape(groups, capacity), 'dp', split_axis=0, c...  15.3 us
    all_to_all x1, waiting for transfers between devices, on_device(): lax.all_to_all(best_seen.reshape(groups, capacity), 'dp', split_axis=0, c...  13.6 us
  transfers between devices with their start and end apart: 2, of which 2 were waited for; matrix products, arithmetic and copies ran while one was open for 1% of the time, Pallas kernels for 0%

profile of v1, /device:TPU:1, one launch (start us, length us, event | category | flops | bytes accessed | tf_op | source)
XLA Modules:
  0.0 147.0 jit_solution(5943194328745755197)
XLA Ops:
  6.5 0.7 convert_bitcast_fusion.1
  7.7 0.7 convert_bitcast_fusion
  8.5 1.1 fusion.18
  9.6 1.1 fusion.19
  10.6 1.3 scatter_custom_fusion
  12.1 51.3 %all_to_all.11 = bf16[64,4,1152]{2,1,0:T(4,128)(2,1)S(1)} all-to-all(bf16[64,4,1152]{2,1,0:T(4,128)(2,1)S(1)} %reshape.177), channel_id=1, replica_groups=mesh['dp'=64,'pair'=8] {'dp'}, dimensions={0} | all-to-all | bytes 1179648 | tf_op jit(solution)/shard_map/all_to_all | solution.py:43
  63.4 1.0 reshape.178
  64.4 0.9 slice_convert_fusion.1
  65.3 0.3 fusion.33
  65.6 36.7 %all-gather.2.cloned.1.call-done = bf16[2048,1152]{1,0:T(8,128)(2,1)} async-done(((bf16[256,1152]{1,0:T(8,128)(2,1)}), bf16[2048,1152]{1,0:T(8,128)(2,1)}) %all-gather.2.cloned.1.call-update) | async-done | bytes 4718608 | tf_op jit(solution)/shard_map/all_gather | solution.py:46
  102.3 1.3 slice_convert_fusion
  103.6 0.6 slice_add_fusion
  104.2 0.4 slice_reduce_fusion.3
  104.6 0.2 copy-done.1
  104.8 0.6 fusion.4
  105.4 0.6 fusion.7
  106.1 0.6 fusion.10
  106.7 0.6 fusion.13
  107.3 0.7 max.41
  108.1 15.3 %all-to-all-start.1 = ((f32[64,1,4]{2,1,0:T(1,128)}), f32[64,1,4]{2,1,0:T(1,128)S(1)}, u32[]{:S(2)}, u32[]{:S(2)}) async-start(f32[64,1,4]{2,1,0:T(1,128)} %bitcast.3), calls=%async_computation.1 | async-start | bytes 65536 | tf_op jit(solution)/shard_map/all_to_all | solution.py:63
  123.4 13.6 %all-to-all-done.1 = f32[64,1,4]{2,1,0:T(1,128)S(1)} async-done(((f32[64,1,4]{2,1,0:T(1,128)}), f32[64,1,4]{2,1,0:T(1,128)S(1)}, u32[]{:S(2)}, u32[]{:S(2)}) %all-to-all-start.1) | async-done | bytes 1056 | tf_op jit(solution)/shard_map/all_to_all | solution.py:63
  137.0 0.5 broadcast.218
  137.5 0.7 reduce.15
  138.3 1.8 %gather_fusion = f32[128]{0:T(128)} fusion(f32[256]{0:T(256)S(1)} %reshape.179, s32[1024]{0:T(1024)S(1)} %pad_clamp_fusion), kind=kCustom, calls=%fused_computation | custom fusion | bytes 1536 | tf_op jit(solution)/shard_map/gather | solution.py:66
  (19 shorter events, 0.9 us)
Async XLA Ops:
  6.5 95.7 %all-gather.2.cloned.1.call-start = ((), (), s32[]{:S(2)}) async-start(), calls=%async_computation.2 | async-start | bytes 5308416 | tf_op jit(solution)/shard_map/all_gather | solution.py:46
  64.4 40.2 %copy-start = (bf16[256,1152]{1,0:T(8,128)(2,1)S(1)}, bf16[256,1152]{1,0:T(8,128)(2,1)}, u32[]{:S(2)}) copy-start(bf16[256,1152]{1,0:T(8,128)(2,1)} %reshape.178) | copy-start | bytes 1769476
  102.3 2.5 %copy-start.1 = (bf16[2048,1152]{1,0:T(8,128)(2,1)S(1)}, bf16[2048,1152]{1,0:T(8,128)(2,1)}, u32[]{:S(2)}) copy-start(bf16[2048,1152]{1,0:T(8,128)(2,1)} %all-gather.2.cloned.1.call-done) | copy-start | bytes 14155780
  108.1 28.9 %all-to-all-start.1 = ((f32[64,1,4]{2,1,0:T(1,128)}), f32[64,1,4]{2,1,0:T(1,128)S(1)}, u32[]{:S(2)}, u32[]{:S(2)}) async-start(f32[64,1,4]{2,1,0:T(1,128)} %bitcast.3), calls=%async_computation.1 | async-start | bytes 65536 | tf_op jit(solution)/shard_map/all_to_all | solution.py:63
Sparse Core Ops, SparseCore 0:
  64.5 37.7 all-gather.1

commit v2 on v1

--- a/solution.py
+++ b/solution.py
@@ -5,6 +5,7 @@
 
 CL_OWN = 2
 META = 128
+PUBLISH_ROWS = 32
 
 
 def tile_best(own_rows, own_key, other_rows, other_key, rows_total):
@@ -60,8 +61,11 @@
             rows_total,
         )
         best_seen = jnp.maximum(best_seen, found)
-    answered = lax.all_to_all(
-        best_seen.reshape(groups, capacity), "dp", split_axis=0, concat_axis=0, tiled=True
+    publish = jnp.zeros((PUBLISH_ROWS * 128,), jnp.float32).at[:slot_count].set(best_seen)
+    published = lax.all_gather(publish.reshape(PUBLISH_ROWS, 128), "dp", axis=0, tiled=False)
+    me = lax.axis_index("dp")
+    answered = lax.dynamic_slice_in_dim(
+        published.reshape(groups, PUBLISH_ROWS * 128), me * capacity, capacity, axis=1
     )
     return answered.reshape(slot_count)[slot_index]
 

time: 147 us -> 257 us (1.75)
  the two profiles are of different devices: /device:TPU:1 before, /device:TPU:8 now
where the time goes in v2:
time: 257 us; the launch traced here: 256 us
  waiting for transfers between devices  172 us (67%)
  blocking collectives  54 us (21%)
  between operations  13.5 us (5%)
  other arithmetic  8.4 us (3%)
  local copies, waits for them, and re-layouts  6.2 us (2%)
    all_gather x1, waiting for transfers between devices, on_device(): lax.all_gather(publish.reshape(PUBLISH_ROWS, 128), 'dp', axis=0, tiled=Fa...  140 us
    all_to_all x1, blocking collectives, on_device(): lax.all_to_all(send_rows.reshape(groups, capacity, -1), 'dp', split_axis=...  54 us
    all_gather x1, waiting for transfers between devices, on_device(): piece_rows = lax.all_gather(got_rows, 'pair', axis=0, tiled=True)  31.6 us
  transfers between devices with their start and end apart: 2, of which 2 were waited for; matrix products, arithmetic and copies ran while one was open for 0% of the time, Pallas kernels for 0%

profile of v2, /device:TPU:8, one launch (start us, length us, event | category | flops | bytes accessed | tf_op | source)
XLA Modules:
  0.0 256.4 jit_solution(14375752796550664068)
XLA Ops:
  6.5 0.7 convert_bitcast_fusion.1
  7.3 0.2 reduce_window_sum.11
  7.5 0.2 select_reduce_fusion
  7.7 0.7 convert_bitcast_fusion
  8.5 1.1 fusion.18
  9.6 1.1 fusion.19
  10.6 1.3 scatter_custom_fusion
  12.1 54.0 %all_to_all.5 = bf16[64,4,1152]{2,1,0:T(4,128)(2,1)S(1)} all-to-all(bf16[64,4,1152]{2,1,0:T(4,128)(2,1)S(1)} %reshape.149), channel_id=1, replica_groups=mesh['dp'=64,'pair'=8] {'dp'}, dimensions={0} | all-to-all | bytes 1179648 | tf_op jit(solution)/shard_map/all_to_all | solution.py:44
  66.1 1.0 reshape.150
  67.2 0.9 slice_convert_fusion.1
  68.1 0.3 fusion.33
  68.4 31.6 %all-gather.3.cloned.1.call-done = bf16[2048,1152]{1,0:T(8,128)(2,1)} async-done(((bf16[256,1152]{1,0:T(8,128)(2,1)}), bf16[2048,1152]{1,0:T(8,128)(2,1)}) %all-gather.3.cloned.1.call-update) | async-done | bytes 4718608 | tf_op jit(solution)/shard_map/all_gather | solution.py:47
  99.9 1.3 slice_convert_fusion
  101.2 0.6 slice_add_fusion
  101.8 0.4 slice_reduce_fusion.3
  102.2 0.2 copy-done.1
  102.4 0.6 fusion.4
  103.1 0.6 fusion.7
  103.7 0.6 fusion.10
  104.4 0.6 fusion.13
  105.0 0.6 pad_bitcast_fusion
  105.7 140.1 %all-gather.5.cloned.1.call-done = f32[64,32,128]{2,1,0:T(8,128)} async-done(((f32[1,32,128]{2,1,0:T(8,128)}), f32[64,32,128]{2,1,0:T(8,128)}) %all-gather.5.cloned.1.call-update) | async-done | bytes 1048592 | tf_op jit(solution)/shard_map/all_gather | solution.py:65
  245.8 1.8 copy.10
  247.8 1.8 gather_fusion
  (20 shorter events, 0.7 us)
Async XLA Ops:
  6.5 93.4 %all-gather.3.cloned.1.call-start = ((), (), s32[]{:S(2)}) async-start(), calls=%async_computation.1 | async-start | bytes 5308416 | tf_op jit(solution)/shard_map/all_gather | solution.py:47
  67.1 35.1 %copy-start = (bf16[256,1152]{1,0:T(8,128)(2,1)S(1)}, bf16[256,1152]{1,0:T(8,128)(2,1)}, u32[]{:S(2)}) copy-start(bf16[256,1152]{1,0:T(8,128)(2,1)} %reshape.150) | copy-start | bytes 1769476
  67.1 178.7 %all-gather.5.cloned.1.call-start = ((), (), s32[]{:S(2)}) async-start(), calls=%async_computation.2 | async-start | bytes 1064960 | tf_op jit(solution)/shard_map/all_gather | solution.py:65
  99.9 2.5 copy-start.1
Sparse Core Ops, SparseCore 0:
  67.2 32.6 all-gather.2
  105.8 139.9 all-gather.4

commit v3 on v1

--- a/solution.py
+++ b/solution.py
@@ -1,7 +1,7 @@
 import jax
 import jax.numpy as jnp
 from jax import lax
-from jax.sharding import PartitionSpec as P
+from jax.sharding import Mesh, PartitionSpec as P
 
 CL_OWN = 2
 META = 128
@@ -21,7 +21,7 @@
 
 def on_device(embedding, labels, order_ids):
     groups = lax.axis_size("dp")
-    pairs = lax.axis_size("pair")
+    pairs = lax.axis_size("y") * lax.axis_size("core")
     rows_here, width = embedding.shape
     rows_total = rows_here * groups * pairs
     capacity = 2 * rows_here // groups
@@ -43,7 +43,8 @@
     got_rows = lax.all_to_all(
         send_rows.reshape(groups, capacity, -1), "dp", split_axis=0, concat_axis=0, tiled=True
     ).reshape(slot_count, -1)
-    piece_rows = lax.all_gather(got_rows, "pair", axis=0, tiled=True)
+    piece_rows = lax.all_gather(got_rows, "y", axis=0, tiled=True)
+    piece_rows = lax.all_gather(piece_rows, "core", axis=0, tiled=True)
     got_key = slot_keys(got_rows, width, rows_total)
     piece_key = slot_keys(piece_rows, width, rows_total)
     column = lax.broadcasted_iota(jnp.int32, got_rows.shape, 1)
@@ -67,8 +68,14 @@
 
 
 def solution(mesh):
-    in_specs = (P(("dp", "pair"), None), P(("dp", "pair")), P(("dp", "pair")))
-    out_specs = P(("dp", "pair"))
+    cores = 2
+    split = Mesh(
+        mesh.devices.reshape(mesh.shape["dp"], mesh.shape["pair"] // cores, cores),
+        ("dp", "y", "core"),
+    )
+    rows = ("dp", "y", "core")
+    in_specs = (P(rows, None), P(rows), P(rows))
+    out_specs = P(rows)
     return jax.shard_map(
-        on_device, mesh=mesh, in_specs=in_specs, out_specs=out_specs, check_vma=False
+        on_device, mesh=split, in_specs=in_specs, out_specs=out_specs, check_vma=False
     )

time: 147 us -> 173 us (1.18)
  waiting for transfers between devices: 50.3 us -> 77.1 us
    all_gather x1 -> x2, waiting for transfers between devices: 36.7 us -> 63.5 us  [the longest x1 36.1 us: on_device(): piece_rows = lax.all_gather(got_rows, 'y', axis=0, tiled=True)]
  transfers between devices with their start and end apart: 2 -> 3, of which waited for: 2 -> 3; matrix products, arithmetic and copies ran while one was open for 1% -> 1% of each run, Pallas kernels for 0% -> 0%
where the time goes in v3:
time: 173 us
  waiting for transfers between devices  77.1 us (45%)
  blocking collectives  51.3 us (30%)
  starting transfers between devices  14.4 us (8%)
  between operations  13.5 us (8%)
  other arithmetic  9.14 us (5%)
  local copies, waits for them, and re-layouts  4.87 us (3%)
  matrix products  2.55 us (1%)
    all_to_all x1, blocking collectives, on_device(): lax.all_to_all(send_rows.reshape(groups, capacity, -1), 'dp', split_axis=...  51.3 us
    all_gather x1, waiting for transfers between devices, on_device(): piece_rows = lax.all_gather(got_rows, 'y', axis=0, tiled=True)  36.1 us
    all_gather x1, waiting for transfers between devices, on_device(): piece_rows = lax.all_gather(piece_rows, 'core', axis=0, tiled=True)  27.4 us
    all_to_all x1, starting transfers between devices, on_device(): lax.all_to_all(best_seen.reshape(groups, capacity), 'dp', split_axis=0, c...  14.3 us
    all_to_all x1, waiting for transfers between devices, on_device(): lax.all_to_all(best_seen.reshape(groups, capacity), 'dp', split_axis=0, c...  13.6 us
  transfers between devices with their start and end apart: 3, of which 3 were waited for; matrix products, arithmetic and copies ran while one was open for 1% of the time, Pallas kernels for 0%

profile of v3, /device:TPU:1, one launch (start us, length us, event | category | flops | bytes accessed | tf_op | source)
XLA Modules:
  0.0 172.8 jit_solution(6586163521684375823)
XLA Ops:
  6.5 0.7 convert_bitcast_fusion.1
  7.7 0.7 convert_bitcast_fusion
  8.5 1.1 fusion.18
  9.6 1.1 fusion.19
  10.6 1.3 scatter_custom_fusion
  12.1 51.3 %all_to_all.11 = bf16[64,4,1152]{2,1,0:T(4,128)(2,1)S(1)} all-to-all(bf16[64,4,1152]{2,1,0:T(4,128)(2,1)S(1)} %reshape.177), channel_id=1, replica_groups=mesh['dp'=64,'y'=4,'core'=2] {'dp'}, dimensions={0} | all-to-all | bytes 1179648 | tf_op jit(solution)/shard_map/all_to_all | solution.py:43
  63.4 0.9 reshape.178
  64.4 36.1 %all-gather.3.cloned.1.call-done = bf16[1024,1152]{1,0:T(8,128)(2,1)} async-done(((bf16[256,1152]{1,0:T(8,128)(2,1)}), bf16[1024,1152]{1,0:T(8,128)(2,1)}) %all-gather.3.cloned.1.call-update) | async-done | bytes 2359312 | tf_op jit(solution)/shard_map/all_gather | solution.py:46
  100.6 0.9 slice_convert_fusion.1
  101.5 0.3 fusion.33
  101.8 27.4 %all-gather.5.cloned.1.call-done = bf16[2048,1152]{1,0:T(8,128)(2,1)} async-done(((bf16[1024,1152]{1,0:T(8,128)(2,1)}), bf16[2048,1152]{1,0:T(8,128)(2,1)}) %all-gather.5.cloned.1.call-update) | async-done | bytes 4718608 | tf_op jit(solution)/shard_map/all_gather | solution.py:47
  129.1 1.3 slice_convert_fusion
  130.4 0.6 slice_add_fusion
  131.0 0.4 slice_reduce_fusion.3
  131.7 0.6 fusion.4
  132.3 0.6 fusion.7
  132.9 0.6 fusion.10
  133.6 0.6 fusion.13
  134.2 0.7 max.41
  134.9 14.3 %all-to-all-start.1 = ((f32[64,1,4]{2,1,0:T(1,128)}), f32[64,1,4]{2,1,0:T(1,128)S(1)}, u32[]{:S(2)}, u32[]{:S(2)}) async-start(f32[64,1,4]{2,1,0:T(1,128)} %bitcast.3), calls=%async_computation.1 | async-start | bytes 65536 | tf_op jit(solution)/shard_map/all_to_all | solution.py:64
  149.3 13.6 %all-to-all-done.1 = f32[64,1,4]{2,1,0:T(1,128)S(1)} async-done(((f32[64,1,4]{2,1,0:T(1,128)}), f32[64,1,4]{2,1,0:T(1,128)S(1)}, u32[]{:S(2)}, u32[]{:S(2)}) %all-to-all-start.1) | async-done | bytes 1056 | tf_op jit(solution)/shard_map/all_to_all | solution.py:64
  162.9 0.5 broadcast.218
  163.4 0.7 reduce.15
  164.2 1.8 %gather_fusion = f32[128]{0:T(128)} fusion(f32[256]{0:T(256)S(1)} %reshape.179, s32[1024]{0:T(1024)S(1)} %pad_clamp_fusion), kind=kCustom, calls=%fused_computation | custom fusion | bytes 1536 | tf_op jit(solution)/shard_map/gather | solution.py:67
  (22 shorter events, 1.2 us)
Async XLA Ops:
  6.5 94.0 %all-gather.3.cloned.1.call-start = ((), (), s32[]{:S(2)}) async-start(), calls=%async_computation.2 | async-start | bytes 2949120 | tf_op jit(solution)/shard_map/all_gather | solution.py:46
  64.4 64.8 %all-gather.5.cloned.1.call-start = ((), (), s32[]{:S(2)}) async-start(), calls=%async_computation.3 | async-start | bytes 7077888 | tf_op jit(solution)/shard_map/all_gather | solution.py:47
  100.5 30.9 %copy-start = (bf16[256,1152]{1,0:T(8,128)(2,1)S(1)}, bf16[256,1152]{1,0:T(8,128)(2,1)}, u32[]{:S(2)}) copy-start(bf16[256,1152]{1,0:T(8,128)(2,1)} %reshape.178) | copy-start | bytes 1769476
  129.1 2.5 %copy-start.1 = (bf16[2048,1152]{1,0:T(8,128)(2,1)S(1)}, bf16[2048,1152]{1,0:T(8,128)(2,1)}, u32[]{:S(2)}) copy-start(bf16[2048,1152]{1,0:T(8,128)(2,1)} %all-gather.5.cloned.1.call-done) | copy-start | bytes 14155780
  134.9 27.9 %all-to-all-start.1 = ((f32[64,1,4]{2,1,0:T(1,128)}), f32[64,1,4]{2,1,0:T(1,128)S(1)}, u32[]{:S(2)}, u32[]{:S(2)}) async-start(f32[64,1,4]{2,1,0:T(1,128)} %bitcast.3), calls=%async_computation.1 | async-start | bytes 65536 | tf_op jit(solution)/shard_map/all_to_all | solution.py:64
Sparse Core Ops, SparseCore 0:
  64.5 35.9 all-gather.2
  102.6 26.4 all-gather.4

commit v4 on v1

v4 whole, which is shorter than its diff:
```python
import jax
import jax.numpy as jnp
from jax import lax
from jax.sharding import PartitionSpec as P

CL_OWN = 2
META = 128


def slot_best(query_rows, query_key, key_rows, key_key, rows_total):
    scores = jnp.dot(query_rows, key_rows.T, preferred_element_type=jnp.float32)
    same_cluster = (key_key[None, :] // rows_total) == (query_key[:, None] // rows_total)
    earlier = same_cluster & (key_key[None, :] < query_key[:, None])
    return jnp.max(jnp.where(earlier, scores, -1.0), axis=1)


def chunk_keys(chunks, capacity, width, rows_total):
    start = capacity * width
    meta = chunks[:, start : start + 3 * capacity].astype(jnp.int32)
    meta = meta.reshape(chunks.shape[0], capacity, 3)
    return meta[:, :, 0] * rows_total + meta[:, :, 1] * 256 + meta[:, :, 2]


def on_device(embedding, labels, order_ids):
    groups = lax.axis_size("dp")
    pairs = lax.axis_size("pair")
    rows_here, width = embedding.shape
    rows_total = rows_here * groups * pairs
    capacity = 2 * rows_here // groups
    slot_count = groups * capacity
    values = embedding.astype(jnp.float32)
    squares = jnp.sum(values * values, axis=1, keepdims=True)
    shifted = squares + 1e-06
    unit_rows = (values * lax.rsqrt(shifted)).astype(jnp.bfloat16)
    owner_group = labels // CL_OWN
    onehot = (owner_group[:, None] == jnp.arange(groups, dtype=jnp.int32)[None, :]).astype(
        jnp.int32
    )
    before = jnp.cumsum(onehot, axis=0) - onehot
    rank = jnp.sum(before * onehot, axis=1)
    slot_index = owner_group * capacity + rank
    meta = jnp.stack([labels + 1, order_ids // 256, order_ids % 256], axis=1).astype(jnp.bfloat16)
    pieces = []
    meta_pieces = []
    for k in range(capacity):
        pick = ((owner_group[None, :] == jnp.arange(groups, dtype=jnp.int32)[:, None])
                & (rank[None, :] == k)).astype(jnp.bfloat16)
        pieces.append(jnp.dot(pick, unit_rows, preferred_element_type=jnp.float32))
        meta_pieces.append(jnp.dot(pick, meta, preferred_element_type=jnp.float32))
    meta_block = jnp.concatenate(meta_pieces, axis=1)
    meta_block = jnp.pad(meta_block, ((0, 0), (0, META - meta_block.shape[1])))
    send = jnp.concatenate(pieces + [meta_block], axis=1).astype(jnp.bfloat16)
    got = lax.all_to_all(send, "dp", split_axis=0, concat_axis=0, tiled=True)
    piece = lax.all_gather(got, "pair", axis=0, tiled=True)
    got_key = chunk_keys(got, capacity, width, rows_total).reshape(slot_count)
    piece_key = chunk_keys(piece, capacity, width, rows_total)
    query_rows = got[:, : capacity * width].reshape(slot_count, width)
    best_seen = jnp.full((slot_count,), -1.0, jnp.float32)
    for k in range(capacity):
        found = slot_best(
            query_rows,
            got_key,
            piece[:, k * width : (k + 1) * width],
            piece_key[:, k],
            rows_total,
        )
        best_seen = jnp.maximum(best_seen, found)
    answered = lax.all_to_all(best_seen, "dp", split_axis=0, concat_axis=0, tiled=True)
    mine = slot_index[:, None] == jnp.arange(slot_count, dtype=jnp.int32)[None, :]
    return jnp.max(jnp.where(mine, answered[None, :], -jnp.inf), axis=1)


def solution(mesh):
    in_specs = (P(("dp", "pair"), None), P(("dp", "pair")), P(("dp", "pair")))
    out_specs = P(("dp", "pair"))
    return jax.shard_map(
        on_device, mesh=mesh, in_specs=in_specs, out_specs=out_specs, check_vma=False
    )
```

time: 147 us -> 152 us (1.034)
  matrix products: 2.55 us -> 12.6 us
  other arithmetic: 9.14 us -> 5.38 us
    dot_general x4 -> x12, matrix products: 2.55 us -> 12.6 us  [the longest x4 7.23 us: slot_best(): scores = jnp.dot(query_rows, key_rows.T, preferred_element_type=jnp.float32)]
    convert_element_type x3 -> x0, other arithmetic: 3.27 us -> none  [the longest x2 2.21 us: slot_keys(): meta = rows[:, width:width + 3].astype(jnp.int32)]
    gather x1 -> x0, local copies, waits for them, and re-layouts: 1.77 us -> none  [on_device(): return answered.reshape(slot_count)[slot_index]]
  transfers between devices with their start and end apart: 2 -> 2, of which waited for: 2 -> 2; matrix products, arithmetic and copies ran while one was open for 1% -> 0% of each run, Pallas kernels for 0% -> 0%
where the time goes in v4:
time: 152 us; the launch traced here: 151 us
  blocking collectives  50.1 us (33%)
  waiting for transfers between devices  48.8 us (32%)
  starting transfers between devices  15.3 us (10%)
  between operations  13.6 us (9%)
  matrix products  12.6 us (8%)
  local copies, waits for them, and re-layouts  5.6 us (4%)
  other arithmetic  5.38 us (4%)
    all_to_all x1, blocking collectives, on_device(): got = lax.all_to_all(send, 'dp', split_axis=0, concat_axis=0, tiled=True)  50.1 us
    all_gather x1, waiting for transfers between devices, on_device(): piece = lax.all_gather(got, 'pair', axis=0, tiled=True)  35.2 us
    all_to_all x1, starting transfers between devices, on_device(): lax.all_to_all(best_seen, 'dp', split_axis=0, concat_axis=0, tiled=True)  15.3 us
    all_to_all x1, waiting for transfers between devices, on_device(): lax.all_to_all(best_seen, 'dp', split_axis=0, concat_axis=0, tiled=True)  13.6 us
    dot_general x4, matrix products, slot_best(): scores = jnp.dot(query_rows, key_rows.T, preferred_element_type=jnp.float32)  7.23 us
    dot_general x4, matrix products, on_device(): pieces.append(jnp.dot(pick, unit_rows, preferred_element_type=jnp.float32))  4.84 us
  transfers between devices with their start and end apart: 2, of which 2 were waited for; matrix products, arithmetic and copies ran while one was open for 0% of the time, Pallas kernels for 0%

profile of v4, /device:TPU:1, one launch (start us, length us, event | category | flops | bytes accessed | tf_op | source)
XLA Modules:
  0.0 151.4 jit_solution(7625603940408909853)
XLA Ops:
  6.5 0.7 convert_bitcast_fusion.1
  7.7 1.1 fusion.16
  8.8 0.7 convert_bitcast_fusion
  9.4 1.2 fusion.5
  10.9 1.2 fusion.7
  12.3 1.2 fusion.9
  13.6 1.2 fusion.11
  15.0 0.5 broadcast.339
  15.5 1.0 reduce.4
  16.8 50.1 %all_to_all.15 = bf16[64,2,2112]{2,1,0:T(2,128)(2,1)S(1)} all-to-all(bf16[64,2,2112]{2,1,0:T(2,128)(2,1)S(1)} %reshape.539), channel_id=1, replica_groups=mesh['dp'=64,'pair'=8] {'dp'}, dimensions={0} | all-to-all | bytes 1081344 | tf_op jit(solution)/shard_map/all_to_all | solution.py:53
  67.0 0.6 reshape.540
  67.6 0.9 copy.37
  69.3 35.2 %all-gather.3.cloned.1.call-done = bf16[512,1,4224]{2,0,1:T(8,128)(2,1)} async-done(((bf16[64,1,4224]{2,0,1:T(8,128)(2,1)}), bf16[512,1,4224]{2,0,1:T(8,128)(2,1)}) %all-gather.3.cloned.1.call-update) | async-done | bytes 4325392 | tf_op jit(solution)/shard_map/all_gather | solution.py:54
  104.5 0.9 slice.68
  105.6 1.8 %fusion = f32[256]{0:T(256)S(1)} fusion(bf16[256,1024]{1,0:T(8,128)(2,1)S(1)} %reshape.524, bf16[512,4224]{1,0:T(8,128)(2,1)} %bitcast.66, s32[512]{0:T(512)S(1)} %bitcast.64, s32[512]{0:T(512)S(1)} %add_select_fusion.3, s32[256]{0:T(256)S(1)} %add.128, s32[256]{0:T(256)S(1)} %and_select_fusion), kind=kOutput, calls=%fused_computation.4 | convolution fusion | flops 269090560 | bytes 1580032 | tf_op jit(solution)/shard_map/dot_general | solution.py:11
  107.4 1.8 %fusion.1 = f32[256]{0:T(256)S(1)} fusion(bf16[256,1024]{1,0:T(8,128)(2,1)S(1)} %reshape.524, bf16[512,4224]{1,0:T(8,128)(2,1)} %bitcast.67, s32[512]{0:T(512)S(1)} %bitcast.62, s32[512]{0:T(512)S(1)} %add_select_fusion.2, s32[256]{0:T(256)S(1)} %add.128, s32[256]{0:T(256)S(1)} %and_select_fusion), kind=kOutput, calls=%fused_computation.5 | convolution fusion | flops 269090560 | bytes 1580032 | tf_op jit(solution)/shard_map/dot_general | solution.py:11
  109.2 1.8 %fusion.2 = f32[256]{0:T(256)S(1)} fusion(bf16[256,1024]{1,0:T(8,128)(2,1)S(1)} %reshape.524, bf16[512,4224]{1,0:T(8,128)(2,1)} %bitcast.68, s32[512]{0:T(512)S(1)} %bitcast.60, s32[512]{0:T(512)S(1)} %add_select_fusion.1, s32[256]{0:T(256)S(1)} %add.128, s32[256]{0:T(256)S(1)} %and_select_fusion), kind=kOutput, calls=%fused_computation.6 | convolution fusion | flops 269090560 | bytes 1580032 | tf_op jit(solution)/shard_map/dot_general | solution.py:11
  111.1 1.8 %fusion.3 = f32[256]{0:T(256)S(1)} fusion(bf16[256,1024]{1,0:T(8,128)(2,1)S(1)} %reshape.524, bf16[512,4224]{1,0:T(8,128)(2,1)} %bitcast.69, s32[512]{0:T(512)S(1)} %bitcast.58, s32[512]{0:T(512)S(1)} %add_select_fusion, s32[256]{0:T(256)S(1)} %add.128, s32[256]{0:T(256)S(1)} %and_select_fusion), kind=kOutput, calls=%fused_computation.7 | convolution fusion | flops 269090560 | bytes 1580032 | tf_op jit(solution)/shard_map/dot_general | solution.py:11
  112.9 0.7 max.38
  113.6 15.3 %all-to-all-start.1 = ((f32[64,4,1]{1,2,0:T(1,128)}), f32[64,4,1]{1,2,0:T(1,128)S(1)}, u32[]{:S(2)}, u32[]{:S(2)}) async-start(f32[64,4,1]{1,2,0:T(1,128)} %bitcast.13), calls=%async_computation.1 | async-start | bytes 65536 | tf_op jit(solution)/shard_map/all_to_all | solution.py:68
  128.9 13.6 %all-to-all-done.1 = f32[64,4,1]{1,2,0:T(1,128)S(1)} async-done(((f32[64,4,1]{1,2,0:T(1,128)}), f32[64,4,1]{1,2,0:T(1,128)S(1)}, u32[]{:S(2)}, u32[]{:S(2)}) %all-to-all-start.1) | async-done | bytes 1056 | tf_op jit(solution)/shard_map/all_to_all | solution.py:68
  142.5 0.5 broadcast.338
  143.0 0.7 reduce.3
  143.9 0.7 select_reduce_fusion
  (40 shorter events, 2.6 us)
Async XLA Ops:
  6.5 97.9 %all-gather.3.cloned.1.call-start = ((), (), s32[]{:S(2)}) async-start(), calls=%async_computation.2 | async-start | bytes 4866048 | tf_op jit(solution)/shard_map/all_gather | solution.py:54
  113.6 28.9 %all-to-all-start.1 = ((f32[64,4,1]{1,2,0:T(1,128)}), f32[64,4,1]{1,2,0:T(1,128)S(1)}, u32[]{:S(2)}, u32[]{:S(2)}) async-start(f32[64,4,1]{1,2,0:T(1,128)} %bitcast.13), calls=%async_computation.1 | async-start | bytes 65536 | tf_op jit(solution)/shard_map/all_to_all | solution.py:68
Sparse Core Ops, SparseCore 0:
  68.6 35.8 all-gather.2

commit v5 on v1

--- a/solution.py
+++ b/solution.py
@@ -5,6 +5,7 @@
 
 CL_OWN = 2
 META = 128
+KEY_TILE = 2048
 
 
 def tile_best(own_rows, own_key, other_rows, other_key, rows_total):
@@ -50,8 +51,8 @@
     query_rows = jnp.where(column < width, got_rows, jnp.zeros_like(got_rows))
     best_seen = jnp.full((slot_count,), -1.0, jnp.float32)
     piece_count = piece_rows.shape[0]
-    for offset in range(0, piece_count, 512):
-        width_now = min(512, piece_count - offset)
+    for offset in range(0, piece_count, KEY_TILE):
+        width_now = min(KEY_TILE, piece_count - offset)
         found = tile_best(
             query_rows,
             got_key,
@@ -63,7 +64,8 @@
     answered = lax.all_to_all(
         best_seen.reshape(groups, capacity), "dp", split_axis=0, concat_axis=0, tiled=True
     )
-    return answered.reshape(slot_count)[slot_index]
+    mine = slot_index[:, None] == jnp.arange(slot_count, dtype=jnp.int32)[None, :]
+    return jnp.max(jnp.where(mine, answered.reshape(1, slot_count), -jnp.inf), axis=1)
 
 
 def solution(mesh):

time: 147 us -> 146 us (level)
  blocking collectives: 51.3 us -> 79.8 us
  starting transfers between devices: 15.3 us -> 0.01 us
  waiting for transfers between devices: 50.3 us -> 36.7 us
  local copies, waits for them, and re-layouts: 4.9 us -> 1.97 us
  matrix products: 2.55 us -> 4.05 us
    all_to_all x0 -> x1, blocking collectives: none -> 28.6 us  [on_device(): lax.all_to_all(best_seen.reshape(groups, capacity), 'dp', split_axis=0, c...]
    all_to_all x1 -> x0, starting transfers between devices: 15.3 us -> none  [on_device(): lax.all_to_all(best_seen.reshape(groups, capacity), 'dp', split_axis=0, c...]
    all_to_all x1 -> x0, waiting for transfers between devices: 13.6 us -> none  [on_device(): lax.all_to_all(best_seen.reshape(groups, capacity), 'dp', split_axis=0, c...]
    gather x1 -> x0, local copies, waits for them, and re-layouts: 1.77 us -> none  [on_device(): return answered.reshape(slot_count)[slot_index]]
    dot_general x4 -> x1, matrix products: 2.55 us -> 4.05 us  [tile_best(): scores = jnp.dot(own_rows, other_rows.T, preferred_element_type=jnp.float32)]
  transfers between devices with their start and end apart: 2 -> 1, of which waited for: 2 -> 1; matrix products, arithmetic and copies ran while one was open for 1% -> 1% of each run, Pallas kernels for 0% -> 0%
where the time goes in v5:
time: 146 us
  blocking collectives  79.8 us (55%)
  waiting for transfers between devices  36.7 us (25%)
  between operations  13.5 us (9%)
  other arithmetic  9.91 us (7%)
  matrix products  4.05 us (3%)
  local copies, waits for them, and re-layouts  1.97 us (1%)
    all_to_all x1, blocking collectives, on_device(): lax.all_to_all(send_rows.reshape(groups, capacity, -1), 'dp', split_axis=...  51.3 us
    all_gather x1, waiting for transfers between devices, on_device(): piece_rows = lax.all_gather(got_rows, 'pair', axis=0, tiled=True)  36.7 us
    all_to_all x1, blocking collectives, on_device(): lax.all_to_all(best_seen.reshape(groups, capacity), 'dp', split_axis=0, c...  28.6 us
    dot_general x1, matrix products, tile_best(): scores = jnp.dot(own_rows, other_rows.T, preferred_element_type=jnp.float32)  4.05 us
  transfers between devices with their start and end apart: 1, of which 1 were waited for; matrix products, arithmetic and copies ran while one was open for 1% of the time, Pallas kernels for 0%

profile of v5, /device:TPU:1, one launch (start us, length us, event | category | flops | bytes accessed | tf_op | source)
XLA Modules:
  0.0 146.0 jit_solution(7372876934294677289)
XLA Ops:
  6.5 0.7 convert_bitcast_fusion.1
  7.2 0.1 fusion.21
  7.3 0.2 reduce_window_sum.11
  7.5 0.2 select_reduce_fusion.1
  7.7 0.7 convert_bitcast_fusion
  8.3 0.1 copy.10
  8.5 1.1 fusion.6
  9.6 1.1 fusion.7
  10.6 1.3 scatter_custom_fusion
  12.0 0.1 reshape.115
  12.1 51.3 %all_to_all.11 = bf16[64,4,1152]{2,1,0:T(4,128)(2,1)S(1)} all-to-all(bf16[64,4,1152]{2,1,0:T(4,128)(2,1)S(1)} %reshape.115), channel_id=1, replica_groups=mesh['dp'=64,'pair'=8] {'dp'}, dimensions={0} | all-to-all | bytes 1179648 | tf_op jit(solution)/shard_map/all_to_all | solution.py:44
  63.4 1.0 reshape.116
  64.4 0.9 slice_convert_fusion.1
  65.3 0.3 fusion.18
  65.6 36.7 %all-gather.2.cloned.1.call-done = bf16[2048,1152]{1,0:T(8,128)(2,1)} async-done(((bf16[256,1152]{1,0:T(8,128)(2,1)}), bf16[2048,1152]{1,0:T(8,128)(2,1)}) %all-gather.2.cloned.1.call-update) | async-done | bytes 4718608 | tf_op jit(solution)/shard_map/all_gather | solution.py:47
  102.3 1.1 slice_convert_fusion
  103.4 0.9 fusion.1
  104.4 4.0 %fusion = f32[256]{0:T(256)S(1)} fusion(bf16[2048,1152]{1,0:T(8,128)(2,1)} %all-gather.2.cloned.1.call-done, s32[2048]{0:T(1024)S(1)} %fusion.1, s32[2048]{0:T(1024)S(1)} %add_select_fusion.1, s32[256]{0:T(256)S(1)} %get-tuple-element.6, s32[256]{0:T(256)S(1)} %get-tuple-element.5, bf16[256,1152]{1,0:T(8,128)(2,1)S(1)} %copy-done, ...), kind=kOutput, calls=%fused_computation.2 | convolution fusion | flops 1210875648 | bytes 5329024 | tf_op jit(solution)/shard_map/dot_general | solution.py:12
  108.4 0.1 max_broadcast_in_dim.15
  108.5 28.6 %all_to_all.12 = f32[64,1,4]{2,1,0:T(1,128)S(1)} all-to-all(f32[64,1,4]{2,1,0:T(1,128)S(1)} %bitcast.8), channel_id=1, replica_groups=mesh['dp'=64,'pair'=8] {'dp'}, dimensions={0} | all-to-all | bytes 2048 | tf_op jit(solution)/shard_map/all_to_all | solution.py:64
  137.1 0.5 broadcast.182
  137.6 0.7 reduce.9
  138.3 0.1 broadcast_in_dim.36
  138.5 0.7 select_reduce_fusion
  (10 shorter events, 0.1 us)
Async XLA Ops:
  6.5 95.7 %all-gather.2.cloned.1.call-start = ((), (), s32[]{:S(2)}) async-start(), calls=%async_computation.2 | async-start | bytes 5308416 | tf_op jit(solution)/shard_map/all_gather | solution.py:47
  65.6 38.8 %copy-start = (bf16[256,1152]{1,0:T(8,128)(2,1)S(1)}, bf16[256,1152]{1,0:T(8,128)(2,1)}, u32[]{:S(2)}) copy-start(bf16[256,1152]{1,0:T(8,128)(2,1)} %reshape.116) | copy-start | bytes 1769476
Sparse Core Ops, SparseCore 0:
  64.5 37.7 all-gather.1

commit v6 on v5

--- a/solution.py
+++ b/solution.py
@@ -5,7 +5,6 @@
 
 CL_OWN = 2
 META = 128
-KEY_TILE = 2048
 
 
 def tile_best(own_rows, own_key, other_rows, other_key, rows_total):
@@ -18,6 +17,33 @@
 def slot_keys(rows, width, rows_total):
     meta = rows[:, width : width + 3].astype(jnp.int32)
     return meta[:, 0] * rows_total + meta[:, 1] * 256 + meta[:, 2]
+
+
+def pair_blocks(block, pairs):
+    chips = pairs // 2
+    if pairs % 2 or chips != 4:
+        gathered = lax.all_gather(block, "pair", axis=0, tiled=True)
+        return jnp.split(gathered, pairs, axis=0)
+
+    def at(y, c):
+        return (y % chips) * 2 + c
+
+    def perm(to):
+        return [(p, to(p // 2, p % 2)) for p in range(pairs)]
+
+    swap = perm(lambda y, c: at(y, 1 - c))
+    up = perm(lambda y, c: at(y + 1, c))
+    down = perm(lambda y, c: at(y - 1, c))
+    cross = perm(lambda y, c: at(y - 1, 1 - c))
+    sibling = lax.ppermute(block, "pair", swap)
+    from_below = lax.ppermute(block, "pair", up)
+    from_above = lax.ppermute(block, "pair", down)
+    two_below = lax.ppermute(from_below, "pair", up)
+    two_above = lax.ppermute(from_above, "pair", cross)
+    sibling_below = lax.ppermute(from_below, "pair", swap)
+    sibling_above = lax.ppermute(from_above, "pair", swap)
+    return [block, sibling, from_below, from_above, two_below, two_above, sibling_below,
+            sibling_above]
 
 
 def on_device(embedding, labels, order_ids):
@@ -44,21 +70,14 @@
     got_rows = lax.all_to_all(
         send_rows.reshape(groups, capacity, -1), "dp", split_axis=0, concat_axis=0, tiled=True
     ).reshape(slot_count, -1)
-    piece_rows = lax.all_gather(got_rows, "pair", axis=0, tiled=True)
+    blocks = pair_blocks(got_rows, pairs)
     got_key = slot_keys(got_rows, width, rows_total)
-    piece_key = slot_keys(piece_rows, width, rows_total)
     column = lax.broadcasted_iota(jnp.int32, got_rows.shape, 1)
     query_rows = jnp.where(column < width, got_rows, jnp.zeros_like(got_rows))
     best_seen = jnp.full((slot_count,), -1.0, jnp.float32)
-    piece_count = piece_rows.shape[0]
-    for offset in range(0, piece_count, KEY_TILE):
-        width_now = min(KEY_TILE, piece_count - offset)
+    for block in blocks:
         found = tile_best(
-            query_rows,
-            got_key,
-            piece_rows[offset : offset + width_now],
-            piece_key[offset : offset + width_now],
-            rows_total,
+            query_rows, got_key, block, slot_keys(block, width, rows_total), rows_total
         )
         best_seen = jnp.maximum(best_seen, found)
     answered = lax.all_to_all(

time: 146 us -> 132 us (0.904)
  blocking collectives: 79.8 us -> 21.6 us
  starting transfers between devices: 0.01 us -> 47 us
  between operations: 13.5 us -> 0.31 us
  waiting for transfers between devices: 36.7 us -> 47 us
  other arithmetic: 9.91 us -> 7.6 us
    all_to_all x1 -> x0, blocking collectives: 51.3 us -> none  [on_device(): lax.all_to_all(send_rows.reshape(groups, capacity, -1), 'dp', split_axis=...]
    all_gather x1 -> x0, waiting for transfers between devices: 36.7 us -> none  [on_device(): piece_rows = lax.all_gather(got_rows, 'pair', axis=0, tiled=True)]
    all_to_all x0 -> x1, waiting for transfers between devices: none -> 32.4 us  [on_device(): lax.all_to_all(send_rows.reshape(groups, capacity, -1), 'dp', split_axis=...]
    ppermute x0 -> x7, starting transfers between devices: none -> 27.9 us  [the longest x1 7.33 us: pair_blocks(): sibling_above = lax.ppermute(from_above, 'pair', swap)]
    all_to_all x0 -> x1, starting transfers between devices: none -> 19.1 us  [on_device(): lax.all_to_all(send_rows.reshape(groups, capacity, -1), 'dp', split_axis=...]
    ppermute x0 -> x7, waiting for transfers between devices: none -> 14.7 us  [the longest x1 7 us: pair_blocks(): two_above = lax.ppermute(from_above, 'pair', cross)]
    all_to_all x1, blocking collectives: 28.6 us -> 21.6 us  [on_device(): lax.all_to_all(best_seen.reshape(groups, capacity), 'dp', split_axis=0, c...]
    dot_general x1 -> x8, matrix products: 4.05 us -> 4.2 us  [tile_best(): scores = jnp.dot(own_rows, other_rows.T, preferred_element_type=jnp.float32)]
  transfers between devices with their start and end apart: 1 -> 8, of which waited for: 1 -> 4; matrix products, arithmetic and copies ran while one was open for 1% -> 3% of each run, Pallas kernels for 0% -> 0%
where the time goes in v6:
time: 132 us; the launch traced here: 131 us
  starting transfers between devices  47 us (36%)
  waiting for transfers between devices  47 us (36%)
  blocking collectives  21.6 us (16%)
  other arithmetic  7.6 us (6%)
  matrix products  4.2 us (3%)
  local copies, waits for them, and re-layouts  3.36 us (3%)
    all_to_all x1, waiting for transfers between devices, on_device(): lax.all_to_all(send_rows.reshape(groups, capacity, -1), 'dp', split_axis=...  32.4 us
    all_to_all x1, blocking collectives, on_device(): lax.all_to_all(best_seen.reshape(groups, capacity), 'dp', split_axis=0, c...  21.6 us
    all_to_all x1, starting transfers between devices, on_device(): lax.all_to_all(send_rows.reshape(groups, capacity, -1), 'dp', split_axis=...  19.1 us
    ppermute x1, starting transfers between devices, pair_blocks(): sibling_above = lax.ppermute(from_above, 'pair', swap)  7.33 us
    ppermute x1, waiting for transfers between devices, pair_blocks(): two_above = lax.ppermute(from_above, 'pair', cross)  7 us
    ppermute x1, starting transfers between devices, pair_blocks(): sibling = lax.ppermute(block, 'pair', swap)  6.41 us
    ppermute x1, starting transfers between devices, pair_blocks(): from_above = lax.ppermute(block, 'pair', down)  4.64 us
    dot_general x8, matrix products, tile_best(): scores = jnp.dot(own_rows, other_rows.T, preferred_element_type=jnp.float32)  4.2 us
  transfers between devices with their start and end apart: 8, of which 4 were waited for; matrix products, arithmetic and copies ran while one was open for 3% of the time, Pallas kernels for 0%

profile of v6, /device:TPU:1, one launch (start us, length us, event | category | flops | bytes accessed | tf_op | source)
XLA Modules:
  0.0 131.1 jit_solution(11929652485400428734)
XLA Ops:
  0.0 1.2 fusion.9
  1.2 0.6 copy-done.1
  1.8 0.6 copy-done.2
  3.2 1.3 %scatter_custom_fusion = bf16[256,1152]{1,0:T(8,128)(2,1)S(1)} fusion(s32[128]{0:T(128)S(1)} %get-tuple-element.7, s32[]{} %constant.167, bf16[128,3]{1,0:T(8,128)(2,1)S(1)} %copy.10, bf16[]{:T(256)} %constant.137.clone.1, bf16[128,1024]{1,0:T(8,128)(2,1)S(1)} %fusion.10, bf16[]{:T(256)} %constant.165), kind=kCustom, calls=%fused_computation.26 | custom fusion | flops 884736 | bytes 890880 | tf_op jit(solution)/shard_map/scatter | solution.py:69
  4.6 0.9 reshape.648
  5.5 19.1 %all-to-all-start = ((bf16[64,4,1152]{2,1,0:T(4,128)(2,1)}), bf16[64,4,1152]{2,1,0:T(4,128)(2,1)S(1)}, u32[]{:S(2)}, u32[]{:S(2)}) async-start(bf16[64,4,1152]{2,1,0:T(4,128)(2,1)} %reshape.648), calls=%async_computation | async-start | bytes 1179648 | tf_op jit(solution)/shard_map/all_to_all | solution.py:70
  24.6 32.4 %all-to-all-done = bf16[64,4,1152]{2,1,0:T(4,128)(2,1)S(1)} async-done(((bf16[64,4,1152]{2,1,0:T(4,128)(2,1)}), bf16[64,4,1152]{2,1,0:T(4,128)(2,1)S(1)}, u32[]{:S(2)}, u32[]{:S(2)}) %all-to-all-start) | async-done | bytes 589856 | tf_op jit(solution)/shard_map/all_to_all | solution.py:70
  57.2 4.6 %collective-permute-start.2 = (bf16[256,1152]{1,0:T(8,128)(2,1)S(1)}, bf16[256,1152]{1,0:T(8,128)(2,1)S(1)}, u32[]{:S(2)}, u32[]{:S(2)}) collective-permute-start(bf16[256,1152]{1,0:T(8,128)(2,1)S(1)} %reshape.649), channel_id=1, source_target_pairs={{0,6},{1,7},{2,0},{3,1},{4,2},{5,3},{6,4},{7,5},{8,14},{9,15},{10,... | collective-permute-start | bytes 1769480 | tf_op jit(solution)/shard_map/ppermute | solution.py:40
  61.8 1.9 %collective-permute-start.1 = (bf16[256,1152]{1,0:T(8,128)(2,1)S(1)}, bf16[256,1152]{1,0:T(8,128)(2,1)S(1)}, u32[]{:S(2)}, u32[]{:S(2)}) collective-permute-start(bf16[256,1152]{1,0:T(8,128)(2,1)S(1)} %reshape.649), channel_id=1, source_target_pairs={{0,2},{1,3},{2,4},{3,5},{4,6},{5,7},{6,0},{7,1},{8,10},{9,11},{10,... | collective-permute-start | bytes 1769480 | tf_op jit(solution)/shard_map/ppermute | solution.py:39
  63.7 6.4 %collective-permute-start = (bf16[256,1152]{1,0:T(8,128)(2,1)S(1)}, bf16[256,1152]{1,0:T(8,128)(2,1)}, u32[]{:S(2)}, u32[]{:S(2)}) collective-permute-start(bf16[256,1152]{1,0:T(8,128)(2,1)S(1)} %reshape.649), channel_id=1, source_target_pairs={{0,1},{1,0},{2,3},{3,2},{4,5},{5,4},{6,7},{7,6},{8,9},{9,8},{10,11... | collective-permute-start | bytes 1769480 | tf_op jit(solution)/shard_map/ppermute | solution.py:38
  71.3 4.0 %collective-permute-done.1 = bf16[256,1152]{1,0:T(8,128)(2,1)S(1)} collective-permute-done((bf16[256,1152]{1,0:T(8,128)(2,1)S(1)}, bf16[256,1152]{1,0:T(8,128)(2,1)S(1)}, u32[]{:S(2)}, u32[]{:S(2)}) %collective-permute-start.1) | collective-permute-done | bytes 589856 | tf_op jit(solution)/shard_map/ppermute | solution.py:39
  75.7 0.9 slice_convert_fusion.6
  76.8 7.3 %collective-permute-start.6 = (bf16[256,1152]{1,0:T(8,128)(2,1)S(1)}, bf16[256,1152]{1,0:T(8,128)(2,1)S(1)}, u32[]{:S(2)}, u32[]{:S(2)}) collective-permute-start(bf16[256,1152]{1,0:T(8,128)(2,1)S(1)} %collective-permute-done.2), channel_id=1, source_target_pairs={{0,1},{1,0},{2,3},{3,2},{4,5},{5,4},{6,7},{7,6},{8,9},{9,8},{10,11... | collective-permute-start | bytes 1769480 | tf_op jit(solution)/shard_map/ppermute | solution.py:44
  84.1 1.9 %collective-permute-start.4 = (bf16[256,1152]{1,0:T(8,128)(2,1)S(1)}, bf16[256,1152]{1,0:T(8,128)(2,1)S(1)}, u32[]{:S(2)}, u32[]{:S(2)}) collective-permute-start(bf16[256,1152]{1,0:T(8,128)(2,1)S(1)} %collective-permute-done.2), channel_id=1, source_target_pairs={{0,7},{1,6},{2,1},{3,0},{4,3},{5,2},{6,5},{7,4},{8,15},{9,14},{10,... | collective-permute-start | bytes 1769480 | tf_op jit(solution)/shard_map/ppermute | solution.py:42
  86.1 1.9 %collective-permute-start.5 = (bf16[256,1152]{1,0:T(8,128)(2,1)S(1)}, bf16[256,1152]{1,0:T(8,128)(2,1)S(1)}, u32[]{:S(2)}, u32[]{:S(2)}) collective-permute-start(bf16[256,1152]{1,0:T(8,128)(2,1)S(1)} %collective-permute-done.1), channel_id=1, source_target_pairs={{0,1},{1,0},{2,3},{3,2},{4,5},{5,4},{6,7},{7,6},{8,9},{9,8},{10,11... | collective-permute-start | bytes 1769480 | tf_op jit(solution)/shard_map/ppermute | solution.py:43
  88.0 3.7 %collective-permute-start.3 = (bf16[256,1152]{1,0:T(8,128)(2,1)S(1)}, bf16[256,1152]{1,0:T(8,128)(2,1)S(1)}, u32[]{:S(2)}, u32[]{:S(2)}) collective-permute-start(bf16[256,1152]{1,0:T(8,128)(2,1)S(1)} %collective-permute-done.1), channel_id=1, source_target_pairs={{0,2},{1,3},{2,4},{3,5},{4,6},{5,7},{6,0},{7,1},{8,10},{9,11},{10,... | collective-permute-start | bytes 1769480 | tf_op jit(solution)/shard_map/ppermute | solution.py:41
  92.5 1.5 %fusion.1 = f32[256]{0:T(256)S(1)} fusion(bf16[256,1152]{1,0:T(8,128)(2,1)} %collective-permute-done, bf16[256,1152]{1,0:T(8,128)(2,1)S(1)} %reshape.649, pred[1152]{0:T(1024)(128)(4,1)S(1)} %iota_compare_fusion.3, s32[256]{0:T(256)S(1)} %get-tuple-element.6, s32[256]{0:T(256)S(1)} %get-tuple-element.5, s32[256]{0:T(256)S(1)} %fusion.33, ...), kind=kOutput, calls=%fused_computation.10 | convolution fusion | flops 151617280 | bytes 1185920 | tf_op jit(solution)/shard_map/dot_general | solution.py:11
  94.3 7.0 %collective-permute-done.4 = bf16[256,1152]{1,0:T(8,128)(2,1)S(1)} collective-permute-done((bf16[256,1152]{1,0:T(8,128)(2,1)S(1)}, bf16[256,1152]{1,0:T(8,128)(2,1)S(1)}, u32[]{:S(2)}, u32[]{:S(2)}) %collective-permute-start.4) | collective-permute-done | bytes 589856 | tf_op jit(solution)/shard_map/ppermute | solution.py:42
  101.8 3.7 %collective-permute-done.3 = bf16[256,1152]{1,0:T(8,128)(2,1)S(1)} collective-permute-done((bf16[256,1152]{1,0:T(8,128)(2,1)S(1)}, bf16[256,1152]{1,0:T(8,128)(2,1)S(1)}, u32[]{:S(2)}, u32[]{:S(2)}) %collective-permute-start.3) | collective-permute-done | bytes 589856 | tf_op jit(solution)/shard_map/ppermute | solution.py:41
  105.7 0.4 fusion.7
  107.4 21.6 %all_to_all.11 = f32[64,1,4]{2,1,0:T(1,128)S(1)} all-to-all(f32[64,1,4]{2,1,0:T(1,128)S(1)} %bitcast.17), channel_id=1, replica_groups=mesh['dp'=64,'pair'=8] {'dp'}, dimensions={0} | all-to-all | bytes 2048 | tf_op jit(solution)/shard_map/all_to_all | solution.py:83
  129.0 0.5 broadcast.619
  129.5 0.7 reduce.21
  130.4 0.7 select_reduce_fusion
  (54 shorter events, 5.8 us)
Async XLA Ops:
  0.0 3.1 %copy-start = (bf16[128,1024]{1,0:T(8,128)(2,1)S(1)}, bf16[128,1024]{1,0:T(8,128)(2,1)}, u32[]{:S(2)}) copy-start(bf16[128,1024]{1,0:T(8,128)(2,1)} %param.3) | copy-start | bytes 786436
  1.2 0.7 copy-start.1
  1.8 0.7 copy-start.2
  5.5 51.5 %all-to-all-start = ((bf16[64,4,1152]{2,1,0:T(4,128)(2,1)}), bf16[64,4,1152]{2,1,0:T(4,128)(2,1)S(1)}, u32[]{:S(2)}, u32[]{:S(2)}) async-start(bf16[64,4,1152]{2,1,0:T(4,128)(2,1)} %reshape.648), calls=%async_computation | async-start | bytes 1179648 | tf_op jit(solution)/shard_map/all_to_all | solution.py:70
  57.2 14.1 %collective-permute-start.2 = (bf16[256,1152]{1,0:T(8,128)(2,1)S(1)}, bf16[256,1152]{1,0:T(8,128)(2,1)S(1)}, u32[]{:S(2)}, u32[]{:S(2)}) collective-permute-start(bf16[256,1152]{1,0:T(8,128)(2,1)S(1)} %reshape.649), channel_id=1, source_target_pairs={{0,6},{1,7},{2,0},{3,1},{4,2},{5,3},{6,4},{7,5},{8,14},{9,15},{10,... | collective-permute-start | bytes 1769480 | tf_op jit(solution)/shard_map/ppermute | solution.py:40
  61.8 13.4 %collective-permute-start.1 = (bf16[256,1152]{1,0:T(8,128)(2,1)S(1)}, bf16[256,1152]{1,0:T(8,128)(2,1)S(1)}, u32[]{:S(2)}, u32[]{:S(2)}) collective-permute-start(bf16[256,1152]{1,0:T(8,128)(2,1)S(1)} %reshape.649), channel_id=1, source_target_pairs={{0,2},{1,3},{2,4},{3,5},{4,6},{5,7},{6,0},{7,1},{8,10},{9,11},{10,... | collective-permute-start | bytes 1769480 | tf_op jit(solution)/shard_map/ppermute | solution.py:39
  63.7 12.0 %collective-permute-start = (bf16[256,1152]{1,0:T(8,128)(2,1)S(1)}, bf16[256,1152]{1,0:T(8,128)(2,1)}, u32[]{:S(2)}, u32[]{:S(2)}) collective-permute-start(bf16[256,1152]{1,0:T(8,128)(2,1)S(1)} %reshape.649), channel_id=1, source_target_pairs={{0,1},{1,0},{2,3},{3,2},{4,5},{5,4},{6,7},{7,6},{8,9},{9,8},{10,11... | collective-permute-start | bytes 1769480 | tf_op jit(solution)/shard_map/ppermute | solution.py:38
  76.8 17.2 %collective-permute-start.6 = (bf16[256,1152]{1,0:T(8,128)(2,1)S(1)}, bf16[256,1152]{1,0:T(8,128)(2,1)S(1)}, u32[]{:S(2)}, u32[]{:S(2)}) collective-permute-start(bf16[256,1152]{1,0:T(8,128)(2,1)S(1)} %collective-permute-done.2), channel_id=1, source_target_pairs={{0,1},{1,0},{2,3},{3,2},{4,5},{5,4},{6,7},{7,6},{8,9},{9,8},{10,11... | collective-permute-start | bytes 1769480 | tf_op jit(solution)/shard_map/ppermute | solution.py:44
  84.1 17.1 %collective-permute-start.4 = (bf16[256,1152]{1,0:T(8,128)(2,1)S(1)}, bf16[256,1152]{1,0:T(8,128)(2,1)S(1)}, u32[]{:S(2)}, u32[]{:S(2)}) collective-permute-start(bf16[256,1152]{1,0:T(8,128)(2,1)S(1)} %collective-permute-done.2), channel_id=1, source_target_pairs={{0,7},{1,6},{2,1},{3,0},{4,3},{5,2},{6,5},{7,4},{8,15},{9,14},{10,... | collective-permute-start | bytes 1769480 | tf_op jit(solution)/shard_map/ppermute | solution.py:42
  86.1 15.2 %collective-permute-start.5 = (bf16[256,1152]{1,0:T(8,128)(2,1)S(1)}, bf16[256,1152]{1,0:T(8,128)(2,1)S(1)}, u32[]{:S(2)}, u32[]{:S(2)}) collective-permute-start(bf16[256,1152]{1,0:T(8,128)(2,1)S(1)} %collective-permute-done.1), channel_id=1, source_target_pairs={{0,1},{1,0},{2,3},{3,2},{4,5},{5,4},{6,7},{7,6},{8,9},{9,8},{10,11... | collective-permute-start | bytes 1769480 | tf_op jit(solution)/shard_map/ppermute | solution.py:43
  88.0 17.5 %collective-permute-start.3 = (bf16[256,1152]{1,0:T(8,128)(2,1)S(1)}, bf16[256,1152]{1,0:T(8,128)(2,1)S(1)}, u32[]{:S(2)}, u32[]{:S(2)}) collective-permute-start(bf16[256,1152]{1,0:T(8,128)(2,1)S(1)} %collective-permute-done.1), channel_id=1, source_target_pairs={{0,2},{1,3},{2,4},{3,5},{4,6},{5,7},{6,0},{7,1},{8,10},{9,11},{10,... | collective-permute-start | bytes 1769480 | tf_op jit(solution)/shard_map/ppermute | solution.py:41

commit v7 on v6

--- a/solution.py
+++ b/solution.py
@@ -40,10 +40,10 @@
     from_above = lax.ppermute(block, "pair", down)
     two_below = lax.ppermute(from_below, "pair", up)
     two_above = lax.ppermute(from_above, "pair", cross)
-    sibling_below = lax.ppermute(from_below, "pair", swap)
-    sibling_above = lax.ppermute(from_above, "pair", swap)
-    return [block, sibling, from_below, from_above, two_below, two_above, sibling_below,
-            sibling_above]
+    rows = block.shape[0]
+    siblings = lax.ppermute(jnp.concatenate([from_below, from_above]), "pair", swap)
+    return [block, sibling, from_below, from_above, two_below, two_above, siblings[:rows],
+            siblings[rows:]]
 
 
 def on_device(embedding, labels, order_ids):
@@ -66,9 +66,10 @@
     meta = jnp.stack([labels + 1, order_ids // 256, order_ids % 256], axis=1).astype(jnp.bfloat16)
     meta = jnp.pad(meta, ((0, 0), (0, META - 3)))
     packed = jnp.concatenate([unit_rows, meta], axis=1)
-    send_rows = jnp.zeros((slot_count, width + META), jnp.bfloat16).at[slot_index].set(packed)
+    send_rows = jnp.zeros((groups, capacity, width + META), jnp.bfloat16)
+    send_rows = send_rows.at[owner_group, slot_index - owner_group * capacity].set(packed)
     got_rows = lax.all_to_all(
-        send_rows.reshape(groups, capacity, -1), "dp", split_axis=0, concat_axis=0, tiled=True
+        send_rows, "dp", split_axis=0, concat_axis=0, tiled=True
     ).reshape(slot_count, -1)
     blocks = pair_blocks(got_rows, pairs)
     got_key = slot_keys(got_rows, width, rows_total)

time: 132 us -> 150 us (1.14)
  blocking collectives: 21.6 us -> 0 us
  waiting for transfers between devices: 47 us -> 68.4 us
  local copies, waits for them, and re-layouts: 3.36 us -> 21.6 us
    all_to_all x1 -> x0, blocking collectives: 21.6 us -> none  [on_device(): lax.all_to_all(best_seen.reshape(groups, capacity), 'dp', split_axis=0, c...]
    scatter x0 -> x1, local copies, waits for them, and re-layouts: none -> 18.6 us  [on_device(): send_rows.at[owner_group, slot_index - owner_group * capacity].set(packed)]
    all_to_all x1 -> x2, waiting for transfers between devices: 32.4 us -> 45.9 us  [the longest x1 32.3 us: on_device(): lax.all_to_all(send_rows, 'dp', split_axis=0, concat_axis=0, tiled=True)]
    ppermute x2 -> x1, starting transfers between devices: 9.25 us -> 3.02 us  [pair_blocks(): lax.ppermute(jnp.concatenate([from_below, from_above]), 'pair', swap)]
    ppermute x1, waiting for transfers between devices: 3.96 us -> 10.1 us  [pair_blocks(): from_below = lax.ppermute(block, 'pair', up)]
    all_to_all x1 -> x2, starting transfers between devices: 19.1 us -> 24.7 us  [the longest x1 19.1 us: on_device(): lax.all_to_all(send_rows, 'dp', split_axis=0, concat_axis=0, tiled=True)]
    ppermute x1, waiting for transfers between devices: 3.7 us -> 9.06 us  [pair_blocks(): two_below = lax.ppermute(from_below, 'pair', up)]
    ppermute x1, waiting for transfers between devices: 7 us -> 1.81 us  [pair_blocks(): two_above = lax.ppermute(from_above, 'pair', cross)]
  transfers between devices with their start and end apart: 8 -> 8, of which waited for: 4 -> 6; matrix products, arithmetic and copies ran while one was open for 3% -> 3% of each run, Pallas kernels for 0% -> 0%
where the time goes in v7:
time: 150 us; the launch traced here: 148 us
  waiting for transfers between devices  68.4 us (46%)
  starting transfers between devices  47 us (31%)
  local copies, waits for them, and re-layouts  21.6 us (14%)
  other arithmetic  6.62 us (4%)
  matrix products  4.29 us (3%)
    all_to_all x1, waiting for transfers between devices, on_device(): lax.all_to_all(send_rows, 'dp', split_axis=0, concat_axis=0, tiled=True)  32.3 us
    all_to_all x1, starting transfers between devices, on_device(): lax.all_to_all(send_rows, 'dp', split_axis=0, concat_axis=0, tiled=True)  19.1 us
    scatter x1, local copies, waits for them, and re-layouts, on_device(): send_rows.at[owner_group, slot_index - owner_group * capacity].set(packed)  18.6 us
    all_to_all x1, waiting for transfers between devices, on_device(): lax.all_to_all(best_seen.reshape(groups, capacity), 'dp', split_axis=0, c...  13.6 us
    ppermute x1, waiting for transfers between devices, pair_blocks(): from_below = lax.ppermute(block, 'pair', up)  10.1 us
    ppermute x1, waiting for transfers between devices, pair_blocks(): two_below = lax.ppermute(from_below, 'pair', up)  9.06 us
    ppermute x1, starting transfers between devices, pair_blocks(): sibling = lax.ppermute(block, 'pair', swap)  6.14 us
    all_to_all x1, starting transfers between devices, on_device(): lax.all_to_all(best_seen.reshape(groups, capacity), 'dp', split_axis=0, c...  5.55 us
  transfers between devices with their start and end apart: 8, of which 6 were waited for; matrix products, arithmetic and copies ran while one was open for 3% of the time, Pallas kernels for 0%

profile of v7, /device:TPU:1, one launch (start us, length us, event | category | flops | bytes accessed | tf_op | source)
XLA Modules:
  0.0 148.3 jit_solution(3361215641407314391)
XLA Ops:
  1.1 0.7 convert_bitcast_fusion
  1.9 1.1 fusion.11
  3.0 1.1 fusion.12
  4.1 1.0 broadcast_in_dim.29
  5.1 18.6 %scatter_fusion = bf16[64,4,1152]{2,1,0:T(4,128)(2,1)} fusion(bf16[64,4,1152]{2,1,0:T(4,128)(2,1)} %broadcast_in_dim.29, s32[128]{0:T(128)S(1)} %fusion.27, bf16[128,1152]{1,0:T(8,128)(2,1)S(1)} %fusion.13), kind=kCustom, calls=%fused_computation | custom fusion | bytes 885760 | tf_op jit(solution)/shard_map/scatter | solution.py:70
  23.7 19.1 %all-to-all-start = ((bf16[64,4,1152]{2,1,0:T(4,128)(2,1)}), bf16[64,4,1152]{2,1,0:T(4,128)(2,1)S(1)}, u32[]{:S(2)}, u32[]{:S(2)}) async-start(bf16[64,4,1152]{2,1,0:T(4,128)(2,1)} %scatter_fusion), calls=%async_computation | async-start | bytes 1179648 | tf_op jit(solution)/shard_map/all_to_all | solution.py:71
  42.9 32.3 %all-to-all-done = bf16[64,4,1152]{2,1,0:T(4,128)(2,1)S(1)} async-done(((bf16[64,4,1152]{2,1,0:T(4,128)(2,1)}), bf16[64,4,1152]{2,1,0:T(4,128)(2,1)S(1)}, u32[]{:S(2)}, u32[]{:S(2)}) %all-to-all-start) | async-done | bytes 589856 | tf_op jit(solution)/shard_map/all_to_all | solution.py:71
  75.6 6.1 %collective-permute-start = (bf16[256,1152]{0,1:T(8,128)(2,1)S(1)}, bf16[256,1152]{0,1:T(8,128)(2,1)}, u32[]{:S(2)}, u32[]{:S(2)}) collective-permute-start(bf16[256,1152]{0,1:T(8,128)(2,1)S(1)} %copy.17), channel_id=1, source_target_pairs={{0,1},{1,0},{2,3},{3,2},{4,5},{5,4},{6,7},{7,6},{8,9},{9,8},{10,11... | collective-permute-start | bytes 1769480 | tf_op jit(solution)/shard_map/ppermute | solution.py:38
  81.8 3.3 %collective-permute-start.1 = (bf16[256,1152]{0,1:T(8,128)(2,1)S(1)}, bf16[256,1152]{0,1:T(8,128)(2,1)S(1)}, u32[]{:S(2)}, u32[]{:S(2)}) collective-permute-start(bf16[256,1152]{0,1:T(8,128)(2,1)S(1)} %copy.17), channel_id=1, source_target_pairs={{0,2},{1,3},{2,4},{3,5},{4,6},{5,7},{6,0},{7,1},{8,10},{9,11},{10,... | collective-permute-start | bytes 1769480 | tf_op jit(solution)/shard_map/ppermute | solution.py:39
  85.0 3.3 %collective-permute-start.2 = (bf16[256,1152]{0,1:T(8,128)(2,1)S(1)}, bf16[256,1152]{0,1:T(8,128)(2,1)S(1)}, u32[]{:S(2)}, u32[]{:S(2)}) collective-permute-start(bf16[256,1152]{0,1:T(8,128)(2,1)S(1)} %copy.17), channel_id=1, source_target_pairs={{0,6},{1,7},{2,0},{3,1},{4,2},{5,3},{6,4},{7,5},{8,14},{9,15},{10,... | collective-permute-start | bytes 1769480 | tf_op jit(solution)/shard_map/ppermute | solution.py:40
  89.2 0.7 slice_convert_fusion.6
  89.9 10.1 %collective-permute-done.1 = bf16[256,1152]{0,1:T(8,128)(2,1)S(1)} collective-permute-done((bf16[256,1152]{0,1:T(8,128)(2,1)S(1)}, bf16[256,1152]{0,1:T(8,128)(2,1)S(1)}, u32[]{:S(2)}, u32[]{:S(2)}) %collective-permute-start.1) | collective-permute-done | bytes 589856 | tf_op jit(solution)/shard_map/ppermute | solution.py:39
  100.0 1.6 %collective-permute-done.2 = bf16[256,1152]{0,1:T(8,128)(2,1)S(1)} collective-permute-done((bf16[256,1152]{0,1:T(8,128)(2,1)S(1)}, bf16[256,1152]{0,1:T(8,128)(2,1)S(1)}, u32[]{:S(2)}, u32[]{:S(2)}) %collective-permute-start.2) | collective-permute-done | bytes 589856 | tf_op jit(solution)/shard_map/ppermute | solution.py:40
  101.7 3.0 %collective-permute-start.5 = (bf16[512,1152]{0,1:T(8,128)(2,1)S(1)}, bf16[512,1152]{0,1:T(8,128)(2,1)S(1)}, u32[]{:S(2)}, u32[]{:S(2)}) collective-permute-start(bf16[512,1152]{0,1:T(8,128)(2,1)S(1)} %pad_maximum_fusion), channel_id=1, source_target_pairs={{0,1},{1,0},{2,3},{3,2},{4,5},{5,4},{6,7},{7,6},{8,9},{9,8},{10,11... | collective-permute-start | bytes 3538952 | tf_op jit(solution)/shard_map/ppermute | solution.py:44
  104.7 3.2 %collective-permute-start.3 = (bf16[256,1152]{0,1:T(8,128)(2,1)S(1)}, bf16[256,1152]{0,1:T(8,128)(2,1)S(1)}, u32[]{:S(2)}, u32[]{:S(2)}) collective-permute-start(bf16[256,1152]{0,1:T(8,128)(2,1)S(1)} %collective-permute-done.1), channel_id=1, source_target_pairs={{0,2},{1,3},{2,4},{3,5},{4,6},{5,7},{6,0},{7,1},{8,10},{9,11},{10,... | collective-permute-start | bytes 1769480 | tf_op jit(solution)/shard_map/ppermute | solution.py:41
  107.9 3.5 %collective-permute-start.4 = (bf16[256,1152]{0,1:T(8,128)(2,1)S(1)}, bf16[256,1152]{0,1:T(8,128)(2,1)S(1)}, u32[]{:S(2)}, u32[]{:S(2)}) collective-permute-start(bf16[256,1152]{0,1:T(8,128)(2,1)S(1)} %collective-permute-done.2), channel_id=1, source_target_pairs={{0,7},{1,6},{2,1},{3,0},{4,3},{5,2},{6,5},{7,4},{8,15},{9,14},{10,... | collective-permute-start | bytes 1769480 | tf_op jit(solution)/shard_map/ppermute | solution.py:42
  111.4 1.5 fusion.1
  113.7 9.1 %collective-permute-done.3 = bf16[256,1152]{0,1:T(8,128)(2,1)S(1)} collective-permute-done((bf16[256,1152]{0,1:T(8,128)(2,1)S(1)}, bf16[256,1152]{0,1:T(8,128)(2,1)S(1)}, u32[]{:S(2)}, u32[]{:S(2)}) %collective-permute-start.3) | collective-permute-done | bytes 589856 | tf_op jit(solution)/shard_map/ppermute | solution.py:41
  123.2 1.8 %collective-permute-done.4 = bf16[256,1152]{0,1:T(8,128)(2,1)S(1)} collective-permute-done((bf16[256,1152]{0,1:T(8,128)(2,1)S(1)}, bf16[256,1152]{0,1:T(8,128)(2,1)S(1)}, u32[]{:S(2)}, u32[]{:S(2)}) %collective-permute-start.4) | collective-permute-done | bytes 589856 | tf_op jit(solution)/shard_map/ppermute | solution.py:42
  126.3 0.7 reshape.662
  127.1 5.5 %all-to-all-start.1 = ((f32[64,1,4]{2,1,0:T(1,128)}), f32[64,1,4]{2,1,0:T(1,128)S(1)}, u32[]{:S(2)}, u32[]{:S(2)}) async-start(f32[64,1,4]{2,1,0:T(1,128)} %bitcast.15), calls=%async_computation.1 | async-start | bytes 65536 | tf_op jit(solution)/shard_map/all_to_all | solution.py:84
  132.6 13.6 %all-to-all-done.1 = f32[64,1,4]{2,1,0:T(1,128)S(1)} async-done(((f32[64,1,4]{2,1,0:T(1,128)}), f32[64,1,4]{2,1,0:T(1,128)S(1)}, u32[]{:S(2)}, u32[]{:S(2)}) %all-to-all-start.1) | async-done | bytes 1056 | tf_op jit(solution)/shard_map/all_to_all | solution.py:84
  146.7 0.7 reduce.3
  147.6 0.7 select_reduce_fusion
  (49 shorter events, 5.8 us)
Async XLA Ops:
  23.7 51.5 %all-to-all-start = ((bf16[64,4,1152]{2,1,0:T(4,128)(2,1)}), bf16[64,4,1152]{2,1,0:T(4,128)(2,1)S(1)}, u32[]{:S(2)}, u32[]{:S(2)}) async-start(bf16[64,4,1152]{2,1,0:T(4,128)(2,1)} %scatter_fusion), calls=%async_computation | async-start | bytes 1179648 | tf_op jit(solution)/shard_map/all_to_all | solution.py:71
  75.6 13.5 %collective-permute-start = (bf16[256,1152]{0,1:T(8,128)(2,1)S(1)}, bf16[256,1152]{0,1:T(8,128)(2,1)}, u32[]{:S(2)}, u32[]{:S(2)}) collective-permute-start(bf16[256,1152]{0,1:T(8,128)(2,1)S(1)} %copy.17), channel_id=1, source_target_pairs={{0,1},{1,0},{2,3},{3,2},{4,5},{5,4},{6,7},{7,6},{8,9},{9,8},{10,11... | collective-permute-start | bytes 1769480 | tf_op jit(solution)/shard_map/ppermute | solution.py:38
  81.8 18.2 %collective-permute-start.1 = (bf16[256,1152]{0,1:T(8,128)(2,1)S(1)}, bf16[256,1152]{0,1:T(8,128)(2,1)S(1)}, u32[]{:S(2)}, u32[]{:S(2)}) collective-permute-start(bf16[256,1152]{0,1:T(8,128)(2,1)S(1)} %copy.17), channel_id=1, source_target_pairs={{0,2},{1,3},{2,4},{3,5},{4,6},{5,7},{6,0},{7,1},{8,10},{9,11},{10,... | collective-permute-start | bytes 1769480 | tf_op jit(solution)/shard_map/ppermute | solution.py:39
  85.0 16.5 %collective-permute-start.2 = (bf16[256,1152]{0,1:T(8,128)(2,1)S(1)}, bf16[256,1152]{0,1:T(8,128)(2,1)S(1)}, u32[]{:S(2)}, u32[]{:S(2)}) collective-permute-start(bf16[256,1152]{0,1:T(8,128)(2,1)S(1)} %copy.17), channel_id=1, source_target_pairs={{0,6},{1,7},{2,0},{3,1},{4,2},{5,3},{6,4},{7,5},{8,14},{9,15},{10,... | collective-permute-start | bytes 1769480 | tf_op jit(solution)/shard_map/ppermute | solution.py:40
  101.7 23.8 %collective-permute-start.5 = (bf16[512,1152]{0,1:T(8,128)(2,1)S(1)}, bf16[512,1152]{0,1:T(8,128)(2,1)S(1)}, u32[]{:S(2)}, u32[]{:S(2)}) collective-permute-start(bf16[512,1152]{0,1:T(8,128)(2,1)S(1)} %pad_maximum_fusion), channel_id=1, source_target_pairs={{0,1},{1,0},{2,3},{3,2},{4,5},{5,4},{6,7},{7,6},{8,9},{9,8},{10,11... | collective-permute-start | bytes 3538952 | tf_op jit(solution)/shard_map/ppermute | solution.py:44
  104.7 18.1 %collective-permute-start.3 = (bf16[256,1152]{0,1:T(8,128)(2,1)S(1)}, bf16[256,1152]{0,1:T(8,128)(2,1)S(1)}, u32[]{:S(2)}, u32[]{:S(2)}) collective-permute-start(bf16[256,1152]{0,1:T(8,128)(2,1)S(1)} %collective-permute-done.1), channel_id=1, source_target_pairs={{0,2},{1,3},{2,4},{3,5},{4,6},{5,7},{6,0},{7,1},{8,10},{9,11},{10,... | collective-permute-start | bytes 1769480 | tf_op jit(solution)/shard_map/ppermute | solution.py:41
  107.9 17.1 %collective-permute-start.4 = (bf16[256,1152]{0,1:T(8,128)(2,1)S(1)}, bf16[256,1152]{0,1:T(8,128)(2,1)S(1)}, u32[]{:S(2)}, u32[]{:S(2)}) collective-permute-start(bf16[256,1152]{0,1:T(8,128)(2,1)S(1)} %collective-permute-done.2), channel_id=1, source_target_pairs={{0,7},{1,6},{2,1},{3,0},{4,3},{5,2},{6,5},{7,4},{8,15},{9,14},{10,... | collective-permute-start | bytes 1769480 | tf_op jit(solution)/shard_map/ppermute | solution.py:42
  127.1 19.2 %all-to-all-start.1 = ((f32[64,1,4]{2,1,0:T(1,128)}), f32[64,1,4]{2,1,0:T(1,128)S(1)}, u32[]{:S(2)}, u32[]{:S(2)}) async-start(f32[64,1,4]{2,1,0:T(1,128)} %bitcast.15), calls=%async_computation.1 | async-start | bytes 65536 | tf_op jit(solution)/shard_map/all_to_all | solution.py:84

commit v8 on v7

--- a/solution.py
+++ b/solution.py
@@ -66,10 +66,9 @@
     meta = jnp.stack([labels + 1, order_ids // 256, order_ids % 256], axis=1).astype(jnp.bfloat16)
     meta = jnp.pad(meta, ((0, 0), (0, META - 3)))
     packed = jnp.concatenate([unit_rows, meta], axis=1)
-    send_rows = jnp.zeros((groups, capacity, width + META), jnp.bfloat16)
-    send_rows = send_rows.at[owner_group, slot_index - owner_group * capacity].set(packed)
+    send_rows = jnp.zeros((slot_count, width + META), jnp.bfloat16).at[slot_index].set(packed)
     got_rows = lax.all_to_all(
-        send_rows, "dp", split_axis=0, concat_axis=0, tiled=True
+        send_rows.reshape(groups, capacity, -1), "dp", split_axis=0, concat_axis=0, tiled=True
     ).reshape(slot_count, -1)
     blocks = pair_blocks(got_rows, pairs)
     got_key = slot_keys(got_rows, width, rows_total)

time: 150 us -> 132 us (0.88)
  local copies, waits for them, and re-layouts: 21.6 us -> 2.07 us
  blocking collectives: 0 us -> 18.8 us
  waiting for transfers between devices: 68.4 us -> 54.3 us
  starting transfers between devices: 47 us -> 41.5 us
  other arithmetic: 6.62 us -> 9.77 us
    all_to_all x0 -> x1, blocking collectives: none -> 18.8 us  [on_device(): lax.all_to_all(best_seen.reshape(groups, capacity), 'dp', split_axis=0, c...]
    scatter x1 -> x0, local copies, waits for them, and re-layouts: 18.6 us -> none  [on_device(): send_rows.at[owner_group, slot_index - owner_group * capacity].set(packed)]
    all_to_all x2 -> x1, waiting for transfers between devices: 45.9 us -> 32.4 us  [on_device(): lax.all_to_all(send_rows.reshape(groups, capacity, -1), 'dp', split_axis=...]
    all_to_all x2 -> x1, starting transfers between devices: 24.7 us -> 19.1 us  [on_device(): lax.all_to_all(send_rows.reshape(groups, capacity, -1), 'dp', split_axis=...]
  transfers between devices with their start and end apart: 8 -> 7, of which waited for: 6 -> 5; matrix products, arithmetic and copies ran while one was open for 3% -> 5% of each run, Pallas kernels for 0% -> 0%
where the time goes in v8:
time: 132 us; the launch traced here: 131 us
  waiting for transfers between devices  54.3 us (41%)
  starting transfers between devices  41.5 us (31%)
  blocking collectives  18.8 us (14%)
  other arithmetic  9.77 us (7%)
  matrix products  4.2 us (3%)
  local copies, waits for them, and re-layouts  2.07 us (2%)
    all_to_all x1, waiting for transfers between devices, on_device(): lax.all_to_all(send_rows.reshape(groups, capacity, -1), 'dp', split_axis=...  32.4 us
    all_to_all x1, starting transfers between devices, on_device(): lax.all_to_all(send_rows.reshape(groups, capacity, -1), 'dp', split_axis=...  19.1 us
    all_to_all x1, blocking collectives, on_device(): lax.all_to_all(best_seen.reshape(groups, capacity), 'dp', split_axis=0, c...  18.8 us
    ppermute x1, waiting for transfers between devices, pair_blocks(): from_below = lax.ppermute(block, 'pair', up)  9.68 us
    ppermute x1, waiting for transfers between devices, pair_blocks(): two_below = lax.ppermute(from_below, 'pair', up)  9.12 us
    ppermute x1, starting transfers between devices, pair_blocks(): sibling = lax.ppermute(block, 'pair', swap)  6.13 us
    dot_general x8, matrix products, tile_best(): scores = jnp.dot(own_rows, other_rows.T, preferred_element_type=jnp.float32)  4.2 us
    ppermute x1, starting transfers between devices, pair_blocks(): two_above = lax.ppermute(from_above, 'pair', cross)  3.47 us
  transfers between devices with their start and end apart: 7, of which 5 were waited for; matrix products, arithmetic and copies ran while one was open for 5% of the time, Pallas kernels for 0%

profile of v8, /device:TPU:1, one launch (start us, length us, event | category | flops | bytes accessed | tf_op | source)
XLA Modules:
  0.0 130.9 jit_solution(4607232910641259490)
XLA Ops:
  0.0 0.7 convert_bitcast_fusion.1
  1.1 0.7 convert_bitcast_fusion
  1.9 1.1 fusion.11
  3.0 1.1 fusion.12
  4.1 1.3 %scatter_custom_fusion = bf16[256,1152]{1,0:T(8,128)(2,1)S(1)} fusion(s32[128]{0:T(128)S(1)} %get-tuple-element.7, s32[]{} %constant.168, bf16[128,3]{1,0:T(8,128)(2,1)S(1)} %copy.10, bf16[]{:T(256)} %constant.137.clone.1, bf16[128,1024]{1,0:T(8,128)(2,1)S(1)} %fusion.12, bf16[]{:T(256)} %constant.165), kind=kCustom, calls=%fused_computation.29 | custom fusion | flops 884736 | bytes 890880 | tf_op jit(solution)/shard_map/scatter | solution.py:69
  5.5 0.9 reshape.648
  6.4 19.1 %all-to-all-start = ((bf16[64,4,1152]{2,1,0:T(4,128)(2,1)}), bf16[64,4,1152]{2,1,0:T(4,128)(2,1)S(1)}, u32[]{:S(2)}, u32[]{:S(2)}) async-start(bf16[64,4,1152]{2,1,0:T(4,128)(2,1)} %reshape.648), calls=%async_computation | async-start | bytes 1179648 | tf_op jit(solution)/shard_map/all_to_all | solution.py:70
  25.5 32.4 %all-to-all-done = bf16[64,4,1152]{2,1,0:T(4,128)(2,1)S(1)} async-done(((bf16[64,4,1152]{2,1,0:T(4,128)(2,1)}), bf16[64,4,1152]{2,1,0:T(4,128)(2,1)S(1)}, u32[]{:S(2)}, u32[]{:S(2)}) %all-to-all-start) | async-done | bytes 589856 | tf_op jit(solution)/shard_map/all_to_all | solution.py:70
  58.0 6.1 %collective-permute-start = (bf16[256,1152]{1,0:T(8,128)(2,1)S(1)}, bf16[256,1152]{1,0:T(8,128)(2,1)}, u32[]{:S(2)}, u32[]{:S(2)}) collective-permute-start(bf16[256,1152]{1,0:T(8,128)(2,1)S(1)} %reshape.649), channel_id=1, source_target_pairs={{0,1},{1,0},{2,3},{3,2},{4,5},{5,4},{6,7},{7,6},{8,9},{9,8},{10,11... | collective-permute-start | bytes 1769480 | tf_op jit(solution)/shard_map/ppermute | solution.py:38
  64.2 3.2 %collective-permute-start.1 = (bf16[256,1152]{1,0:T(8,128)(2,1)S(1)}, bf16[256,1152]{1,0:T(8,128)(2,1)S(1)}, u32[]{:S(2)}, u32[]{:S(2)}) collective-permute-start(bf16[256,1152]{1,0:T(8,128)(2,1)S(1)} %reshape.649), channel_id=1, source_target_pairs={{0,2},{1,3},{2,4},{3,5},{4,6},{5,7},{6,0},{7,1},{8,10},{9,11},{10,... | collective-permute-start | bytes 1769480 | tf_op jit(solution)/shard_map/ppermute | solution.py:39
  67.4 3.4 %collective-permute-start.2 = (bf16[256,1152]{1,0:T(8,128)(2,1)S(1)}, bf16[256,1152]{1,0:T(8,128)(2,1)S(1)}, u32[]{:S(2)}, u32[]{:S(2)}) collective-permute-start(bf16[256,1152]{1,0:T(8,128)(2,1)S(1)} %reshape.649), channel_id=1, source_target_pairs={{0,6},{1,7},{2,0},{3,1},{4,2},{5,3},{6,4},{7,5},{8,14},{9,15},{10,... | collective-permute-start | bytes 1769480 | tf_op jit(solution)/shard_map/ppermute | solution.py:40
  71.9 0.9 slice_convert_fusion.6
  72.7 9.7 %collective-permute-done.1 = bf16[256,1152]{1,0:T(8,128)(2,1)S(1)} collective-permute-done((bf16[256,1152]{1,0:T(8,128)(2,1)S(1)}, bf16[256,1152]{1,0:T(8,128)(2,1)S(1)}, u32[]{:S(2)}, u32[]{:S(2)}) %collective-permute-start.1) | collective-permute-done | bytes 589856 | tf_op jit(solution)/shard_map/ppermute | solution.py:39
  82.9 1.1 collective-permute-done.2
  84.3 3.0 %collective-permute-start.5 = (bf16[512,1152]{1,0:T(8,128)(2,1)S(1)}, bf16[512,1152]{1,0:T(8,128)(2,1)S(1)}, u32[]{:S(2)}, u32[]{:S(2)}) collective-permute-start(bf16[512,1152]{1,0:T(8,128)(2,1)S(1)} %pad_maximum_fusion), channel_id=1, source_target_pairs={{0,1},{1,0},{2,3},{3,2},{4,5},{5,4},{6,7},{7,6},{8,9},{9,8},{10,11... | collective-permute-start | bytes 3538952 | tf_op jit(solution)/shard_map/ppermute | solution.py:44
  87.3 3.2 %collective-permute-start.3 = (bf16[256,1152]{1,0:T(8,128)(2,1)S(1)}, bf16[256,1152]{1,0:T(8,128)(2,1)S(1)}, u32[]{:S(2)}, u32[]{:S(2)}) collective-permute-start(bf16[256,1152]{1,0:T(8,128)(2,1)S(1)} %collective-permute-done.1), channel_id=1, source_target_pairs={{0,2},{1,3},{2,4},{3,5},{4,6},{5,7},{6,0},{7,1},{8,10},{9,11},{10,... | collective-permute-start | bytes 1769480 | tf_op jit(solution)/shard_map/ppermute | solution.py:41
  90.5 3.5 %collective-permute-start.4 = (bf16[256,1152]{1,0:T(8,128)(2,1)S(1)}, bf16[256,1152]{1,0:T(8,128)(2,1)S(1)}, u32[]{:S(2)}, u32[]{:S(2)}) collective-permute-start(bf16[256,1152]{1,0:T(8,128)(2,1)S(1)} %collective-permute-done.2), channel_id=1, source_target_pairs={{0,7},{1,6},{2,1},{3,0},{4,3},{5,2},{6,5},{7,4},{8,15},{9,14},{10,... | collective-permute-start | bytes 1769480 | tf_op jit(solution)/shard_map/ppermute | solution.py:42
  94.0 1.5 %fusion.1 = f32[256]{0:T(256)S(1)} fusion(bf16[256,1152]{1,0:T(8,128)(2,1)} %collective-permute-done, bf16[256,1152]{1,0:T(8,128)(2,1)S(1)} %reshape.649, pred[1152]{0:T(1024)(128)(4,1)S(1)} %iota_compare_fusion.3, s32[256]{0:T(256)S(1)} %get-tuple-element.6, s32[256]{0:T(256)S(1)} %get-tuple-element.5, s32[256]{0:T(256)S(1)} %fusion.35, ...), kind=kOutput, calls=%fused_computation.11 | convolution fusion | flops 151617280 | bytes 1185920 | tf_op jit(solution)/shard_map/dot_general | solution.py:11
  96.2 9.1 %collective-permute-done.3 = bf16[256,1152]{1,0:T(8,128)(2,1)S(1)} collective-permute-done((bf16[256,1152]{1,0:T(8,128)(2,1)S(1)}, bf16[256,1152]{1,0:T(8,128)(2,1)S(1)}, u32[]{:S(2)}, u32[]{:S(2)}) %collective-permute-start.3) | collective-permute-done | bytes 589856 | tf_op jit(solution)/shard_map/ppermute | solution.py:41
  105.6 2.1 %collective-permute-done.4 = bf16[256,1152]{1,0:T(8,128)(2,1)S(1)} collective-permute-done((bf16[256,1152]{1,0:T(8,128)(2,1)S(1)}, bf16[256,1152]{1,0:T(8,128)(2,1)S(1)}, u32[]{:S(2)}, u32[]{:S(2)}) %collective-permute-start.4) | collective-permute-done | bytes 589856 | tf_op jit(solution)/shard_map/ppermute | solution.py:42
  110.0 18.8 %all_to_all.11 = f32[64,1,4]{2,1,0:T(1,128)S(1)} all-to-all(f32[64,1,4]{2,1,0:T(1,128)S(1)} %bitcast.14), channel_id=1, replica_groups=mesh['dp'=64,'pair'=8] {'dp'}, dimensions={0} | all-to-all | bytes 2048 | tf_op jit(solution)/shard_map/all_to_all | solution.py:83
  128.8 0.5 broadcast.619
  129.3 0.7 reduce.21
  130.2 0.7 select_reduce_fusion
  (45 shorter events, 6.0 us)
Async XLA Ops:
  6.4 51.5 %all-to-all-start = ((bf16[64,4,1152]{2,1,0:T(4,128)(2,1)}), bf16[64,4,1152]{2,1,0:T(4,128)(2,1)S(1)}, u32[]{:S(2)}, u32[]{:S(2)}) async-start(bf16[64,4,1152]{2,1,0:T(4,128)(2,1)} %reshape.648), calls=%async_computation | async-start | bytes 1179648 | tf_op jit(solution)/shard_map/all_to_all | solution.py:70
  58.0 13.8 %collective-permute-start = (bf16[256,1152]{1,0:T(8,128)(2,1)S(1)}, bf16[256,1152]{1,0:T(8,128)(2,1)}, u32[]{:S(2)}, u32[]{:S(2)}) collective-permute-start(bf16[256,1152]{1,0:T(8,128)(2,1)S(1)} %reshape.649), channel_id=1, source_target_pairs={{0,1},{1,0},{2,3},{3,2},{4,5},{5,4},{6,7},{7,6},{8,9},{9,8},{10,11... | collective-permute-start | bytes 1769480 | tf_op jit(solution)/shard_map/ppermute | solution.py:38
  64.2 18.2 %collective-permute-start.1 = (bf16[256,1152]{1,0:T(8,128)(2,1)S(1)}, bf16[256,1152]{1,0:T(8,128)(2,1)S(1)}, u32[]{:S(2)}, u32[]{:S(2)}) collective-permute-start(bf16[256,1152]{1,0:T(8,128)(2,1)S(1)} %reshape.649), channel_id=1, source_target_pairs={{0,2},{1,3},{2,4},{3,5},{4,6},{5,7},{6,0},{7,1},{8,10},{9,11},{10,... | collective-permute-start | bytes 1769480 | tf_op jit(solution)/shard_map/ppermute | solution.py:39
  67.4 16.5 %collective-permute-start.2 = (bf16[256,1152]{1,0:T(8,128)(2,1)S(1)}, bf16[256,1152]{1,0:T(8,128)(2,1)S(1)}, u32[]{:S(2)}, u32[]{:S(2)}) collective-permute-start(bf16[256,1152]{1,0:T(8,128)(2,1)S(1)} %reshape.649), channel_id=1, source_target_pairs={{0,6},{1,7},{2,0},{3,1},{4,2},{5,3},{6,4},{7,5},{8,14},{9,15},{10,... | collective-permute-start | bytes 1769480 | tf_op jit(solution)/shard_map/ppermute | solution.py:40
  84.3 24.4 %collective-permute-start.5 = (bf16[512,1152]{1,0:T(8,128)(2,1)S(1)}, bf16[512,1152]{1,0:T(8,128)(2,1)S(1)}, u32[]{:S(2)}, u32[]{:S(2)}) collective-permute-start(bf16[512,1152]{1,0:T(8,128)(2,1)S(1)} %pad_maximum_fusion), channel_id=1, source_target_pairs={{0,1},{1,0},{2,3},{3,2},{4,5},{5,4},{6,7},{7,6},{8,9},{9,8},{10,11... | collective-permute-start | bytes 3538952 | tf_op jit(solution)/shard_map/ppermute | solution.py:44
  87.3 18.1 %collective-permute-start.3 = (bf16[256,1152]{1,0:T(8,128)(2,1)S(1)}, bf16[256,1152]{1,0:T(8,128)(2,1)S(1)}, u32[]{:S(2)}, u32[]{:S(2)}) collective-permute-start(bf16[256,1152]{1,0:T(8,128)(2,1)S(1)} %collective-permute-done.1), channel_id=1, source_target_pairs={{0,2},{1,3},{2,4},{3,5},{4,6},{5,7},{6,0},{7,1},{8,10},{9,11},{10,... | collective-permute-start | bytes 1769480 | tf_op jit(solution)/shard_map/ppermute | solution.py:41
  90.5 17.1 %collective-permute-start.4 = (bf16[256,1152]{1,0:T(8,128)(2,1)S(1)}, bf16[256,1152]{1,0:T(8,128)(2,1)S(1)}, u32[]{:S(2)}, u32[]{:S(2)}) collective-permute-start(bf16[256,1152]{1,0:T(8,128)(2,1)S(1)} %collective-permute-done.2), channel_id=1, source_target_pairs={{0,7},{1,6},{2,1},{3,0},{4,3},{5,2},{6,5},{7,4},{8,15},{9,14},{10,... | collective-permute-start | bytes 1769480 | tf_op jit(solution)/shard_map/ppermute | solution.py:42

commit v9 on v8

--- a/solution.py
+++ b/solution.py
@@ -34,15 +34,17 @@
     swap = perm(lambda y, c: at(y, 1 - c))
     up = perm(lambda y, c: at(y + 1, c))
     down = perm(lambda y, c: at(y - 1, c))
-    cross = perm(lambda y, c: at(y - 1, 1 - c))
+    rows = block.shape[0]
+    half = rows // 2
     sibling = lax.ppermute(block, "pair", swap)
     from_below = lax.ppermute(block, "pair", up)
     from_above = lax.ppermute(block, "pair", down)
-    two_below = lax.ppermute(from_below, "pair", up)
-    two_above = lax.ppermute(from_above, "pair", cross)
-    rows = block.shape[0]
+    far_low = lax.ppermute(from_below[:half], "pair", up)
+    far_high = lax.ppermute(from_above[half:], "pair", down)
     siblings = lax.ppermute(jnp.concatenate([from_below, from_above]), "pair", swap)
-    return [block, sibling, from_below, from_above, two_below, two_above, siblings[:rows],
+    far = jnp.concatenate([far_low, far_high])
+    far_sibling = lax.ppermute(far, "pair", swap)
+    return [block, sibling, from_below, from_above, far, far_sibling, siblings[:rows],
             siblings[rows:]]
 
 

time: 132 us -> 126 us (0.955)
  waiting for transfers between devices: 54.3 us -> 44 us
  starting transfers between devices: 41.5 us -> 45.8 us
    ppermute x2 -> x3, waiting for transfers between devices: 11.2 us -> 0.96 us  [the longest x1 0.96 us: pair_blocks(): far_sibling = lax.ppermute(far, 'pair', swap)]
    ppermute x2 -> x3, starting transfers between devices: 6.67 us -> 10.5 us  [the longest x1 3.93 us: pair_blocks(): far_sibling = lax.ppermute(far, 'pair', swap)]
  transfers between devices with their start and end apart: 7 -> 8, of which waited for: 5 -> 4; matrix products, arithmetic and copies ran while one was open for 5% -> 5% of each run, Pallas kernels for 0% -> 0%
where the time goes in v9:
time: 126 us; the launch traced here: 125 us
  starting transfers between devices  45.8 us (36%)
  waiting for transfers between devices  44 us (35%)
  blocking collectives  18.8 us (15%)
  other arithmetic  9.78 us (8%)
  matrix products  4.2 us (3%)
  local copies, waits for them, and re-layouts  2.17 us (2%)
    all_to_all x1, waiting for transfers between devices, on_device(): lax.all_to_all(send_rows.reshape(groups, capacity, -1), 'dp', split_axis=...  32.4 us
    all_to_all x1, starting transfers between devices, on_device(): lax.all_to_all(send_rows.reshape(groups, capacity, -1), 'dp', split_axis=...  19.1 us
    all_to_all x1, blocking collectives, on_device(): lax.all_to_all(best_seen.reshape(groups, capacity), 'dp', split_axis=0, c...  18.8 us
    ppermute x1, waiting for transfers between devices, pair_blocks(): from_below = lax.ppermute(block, 'pair', up)  9.68 us
    ppermute x1, starting transfers between devices, pair_blocks(): sibling = lax.ppermute(block, 'pair', swap)  6.13 us
    dot_general x8, matrix products, tile_best(): scores = jnp.dot(own_rows, other_rows.T, preferred_element_type=jnp.float32)  4.2 us
    ppermute x1, starting transfers between devices, pair_blocks(): far_sibling = lax.ppermute(far, 'pair', swap)  3.93 us
    ppermute x1, starting transfers between devices, pair_blocks(): lax.ppermute(jnp.concatenate([from_below, from_above]), 'pair', swap)  3.5 us
  transfers between devices with their start and end apart: 8, of which 4 were waited for; matrix products, arithmetic and copies ran while one was open for 5% of the time, Pallas kernels for 0%

profile of v9, /device:TPU:1, one launch (start us, length us, event | category | flops | bytes accessed | tf_op | source)
XLA Modules:
  0.0 125.1 jit_solution(11111622993461525192)
XLA Ops:
  0.0 0.7 convert_bitcast_fusion.1
  1.1 0.7 convert_bitcast_fusion
  1.9 1.1 fusion.11
  3.0 1.1 fusion.12
  4.1 1.3 %scatter_custom_fusion = bf16[256,1152]{1,0:T(8,128)(2,1)S(1)} fusion(s32[128]{0:T(128)S(1)} %get-tuple-element.7, s32[]{} %constant.170, bf16[128,3]{1,0:T(8,128)(2,1)S(1)} %copy.10, bf16[]{:T(256)} %constant.137.clone.1, bf16[128,1024]{1,0:T(8,128)(2,1)S(1)} %fusion.12, bf16[]{:T(256)} %constant.165), kind=kCustom, calls=%fused_computation.29 | custom fusion | flops 884736 | bytes 890880 | tf_op jit(solution)/shard_map/scatter | solution.py:71
  5.5 0.9 reshape.648
  6.4 19.1 %all-to-all-start = ((bf16[64,4,1152]{2,1,0:T(4,128)(2,1)}), bf16[64,4,1152]{2,1,0:T(4,128)(2,1)S(1)}, u32[]{:S(2)}, u32[]{:S(2)}) async-start(bf16[64,4,1152]{2,1,0:T(4,128)(2,1)} %reshape.648), calls=%async_computation | async-start | bytes 1179648 | tf_op jit(solution)/shard_map/all_to_all | solution.py:72
  25.5 32.4 %all-to-all-done = bf16[64,4,1152]{2,1,0:T(4,128)(2,1)S(1)} async-done(((bf16[64,4,1152]{2,1,0:T(4,128)(2,1)}), bf16[64,4,1152]{2,1,0:T(4,128)(2,1)S(1)}, u32[]{:S(2)}, u32[]{:S(2)}) %all-to-all-start) | async-done | bytes 589856 | tf_op jit(solution)/shard_map/all_to_all | solution.py:72
  58.0 6.1 %collective-permute-start = (bf16[256,1152]{1,0:T(8,128)(2,1)S(1)}, bf16[256,1152]{1,0:T(8,128)(2,1)}, u32[]{:S(2)}, u32[]{:S(2)}) collective-permute-start(bf16[256,1152]{1,0:T(8,128)(2,1)S(1)} %reshape.649), channel_id=1, source_target_pairs={{0,1},{1,0},{2,3},{3,2},{4,5},{5,4},{6,7},{7,6},{8,9},{9,8},{10,11... | collective-permute-start | bytes 1769480 | tf_op jit(solution)/shard_map/ppermute | solution.py:39
  64.2 3.2 %collective-permute-start.1 = (bf16[256,1152]{1,0:T(8,128)(2,1)S(1)}, bf16[256,1152]{1,0:T(8,128)(2,1)S(1)}, u32[]{:S(2)}, u32[]{:S(2)}) collective-permute-start(bf16[256,1152]{1,0:T(8,128)(2,1)S(1)} %reshape.649), channel_id=1, source_target_pairs={{0,2},{1,3},{2,4},{3,5},{4,6},{5,7},{6,0},{7,1},{8,10},{9,11},{10,... | collective-permute-start | bytes 1769480 | tf_op jit(solution)/shard_map/ppermute | solution.py:40
  67.4 3.4 %collective-permute-start.2 = (bf16[256,1152]{1,0:T(8,128)(2,1)S(1)}, bf16[256,1152]{1,0:T(8,128)(2,1)S(1)}, u32[]{:S(2)}, u32[]{:S(2)}) collective-permute-start(bf16[256,1152]{1,0:T(8,128)(2,1)S(1)} %reshape.649), channel_id=1, source_target_pairs={{0,6},{1,7},{2,0},{3,1},{4,2},{5,3},{6,4},{7,5},{8,14},{9,15},{10,... | collective-permute-start | bytes 1769480 | tf_op jit(solution)/shard_map/ppermute | solution.py:41
  71.9 0.9 slice_convert_fusion.6
  72.7 9.7 %collective-permute-done.1 = bf16[256,1152]{1,0:T(8,128)(2,1)S(1)} collective-permute-done((bf16[256,1152]{1,0:T(8,128)(2,1)S(1)}, bf16[256,1152]{1,0:T(8,128)(2,1)S(1)}, u32[]{:S(2)}, u32[]{:S(2)}) %collective-permute-start.1) | collective-permute-done | bytes 589856 | tf_op jit(solution)/shard_map/ppermute | solution.py:40
  82.9 1.1 collective-permute-done.2
  84.2 3.2 %collective-permute-start.3 = (bf16[128,1152]{1,0:T(8,128)(2,1)S(1)}, bf16[128,1152]{1,0:T(8,128)(2,1)S(1)}, u32[]{:S(2)}, u32[]{:S(2)}) collective-permute-start(bf16[128,1152]{1,0:T(8,128)(2,1)S(1)} %slice.166), channel_id=1, source_target_pairs={{0,2},{1,3},{2,4},{3,5},{4,6},{5,7},{6,0},{7,1},{8,10},{9,11},{10,... | collective-permute-start | bytes 884744 | tf_op jit(solution)/shard_map/ppermute | solution.py:42
  87.4 3.4 %collective-permute-start.4 = (bf16[128,1152]{1,0:T(8,128)(2,1)S(1)}, bf16[128,1152]{1,0:T(8,128)(2,1)S(1)}, u32[]{:S(2)}, u32[]{:S(2)}) collective-permute-start(bf16[128,1152]{1,0:T(8,128)(2,1)S(1)} %slice.167), channel_id=1, source_target_pairs={{0,6},{1,7},{2,0},{3,1},{4,2},{5,3},{6,4},{7,5},{8,14},{9,15},{10,... | collective-permute-start | bytes 884744 | tf_op jit(solution)/shard_map/ppermute | solution.py:43
  90.9 3.5 %collective-permute-start.6 = (bf16[512,1152]{1,0:T(8,128)(2,1)S(1)}, bf16[512,1152]{1,0:T(8,128)(2,1)S(1)}, u32[]{:S(2)}, u32[]{:S(2)}) collective-permute-start(bf16[512,1152]{1,0:T(8,128)(2,1)S(1)} %pad_maximum_fusion), channel_id=1, source_target_pairs={{0,1},{1,0},{2,3},{3,2},{4,5},{5,4},{6,7},{7,6},{8,9},{9,8},{10,11... | collective-permute-start | bytes 3538952 | tf_op jit(solution)/shard_map/ppermute | solution.py:44
  94.4 1.5 %fusion.1 = f32[256]{0:T(256)S(1)} fusion(bf16[256,1152]{1,0:T(8,128)(2,1)} %collective-permute-done, bf16[256,1152]{1,0:T(8,128)(2,1)S(1)} %reshape.649, pred[1152]{0:T(1024)(128)(4,1)S(1)} %iota_compare_fusion.3, s32[256]{0:T(256)S(1)} %get-tuple-element.6, s32[256]{0:T(256)S(1)} %get-tuple-element.5, s32[256]{0:T(256)S(1)} %fusion.35, ...), kind=kOutput, calls=%fused_computation.11 | convolution fusion | flops 151617280 | bytes 1185920 | tf_op jit(solution)/shard_map/dot_general | solution.py:11
  96.8 3.9 %collective-permute-start.5 = (bf16[256,1152]{1,0:T(8,128)(2,1)S(1)}, bf16[256,1152]{1,0:T(8,128)(2,1)S(1)}, u32[]{:S(2)}, u32[]{:S(2)}) collective-permute-start(bf16[256,1152]{1,0:T(8,128)(2,1)S(1)} %constant_dynamic-update-slice_fusion), channel_id=1, source_target_pairs={{0,1},{1,0},{2,3},{3,2},{4,5},{5,4},{6,7},{7,6},{8,9},{9,8},{10,11... | collective-permute-start | bytes 1769480 | tf_op jit(solution)/shard_map/ppermute | solution.py:46
  101.4 1.0 collective-permute-done.5
  104.3 18.8 %all_to_all.11 = f32[64,1,4]{2,1,0:T(1,128)S(1)} all-to-all(f32[64,1,4]{2,1,0:T(1,128)S(1)} %bitcast.14), channel_id=1, replica_groups=mesh['dp'=64,'pair'=8] {'dp'}, dimensions={0} | all-to-all | bytes 2048 | tf_op jit(solution)/shard_map/all_to_all | solution.py:85
  123.1 0.5 broadcast.619
  123.6 0.7 reduce.21
  124.4 0.7 select_reduce_fusion
  (51 shorter events, 6.2 us)
Async XLA Ops:
  6.4 51.5 %all-to-all-start = ((bf16[64,4,1152]{2,1,0:T(4,128)(2,1)}), bf16[64,4,1152]{2,1,0:T(4,128)(2,1)S(1)}, u32[]{:S(2)}, u32[]{:S(2)}) async-start(bf16[64,4,1152]{2,1,0:T(4,128)(2,1)} %reshape.648), calls=%async_computation | async-start | bytes 1179648 | tf_op jit(solution)/shard_map/all_to_all | solution.py:72
  58.0 13.8 %collective-permute-start = (bf16[256,1152]{1,0:T(8,128)(2,1)S(1)}, bf16[256,1152]{1,0:T(8,128)(2,1)}, u32[]{:S(2)}, u32[]{:S(2)}) collective-permute-start(bf16[256,1152]{1,0:T(8,128)(2,1)S(1)} %reshape.649), channel_id=1, source_target_pairs={{0,1},{1,0},{2,3},{3,2},{4,5},{5,4},{6,7},{7,6},{8,9},{9,8},{10,11... | collective-permute-start | bytes 1769480 | tf_op jit(solution)/shard_map/ppermute | solution.py:39
  64.2 18.2 %collective-permute-start.1 = (bf16[256,1152]{1,0:T(8,128)(2,1)S(1)}, bf16[256,1152]{1,0:T(8,128)(2,1)S(1)}, u32[]{:S(2)}, u32[]{:S(2)}) collective-permute-start(bf16[256,1152]{1,0:T(8,128)(2,1)S(1)} %reshape.649), channel_id=1, source_target_pairs={{0,2},{1,3},{2,4},{3,5},{4,6},{5,7},{6,0},{7,1},{8,10},{9,11},{10,... | collective-permute-start | bytes 1769480 | tf_op jit(solution)/shard_map/ppermute | solution.py:40
  67.4 16.5 %collective-permute-start.2 = (bf16[256,1152]{1,0:T(8,128)(2,1)S(1)}, bf16[256,1152]{1,0:T(8,128)(2,1)S(1)}, u32[]{:S(2)}, u32[]{:S(2)}) collective-permute-start(bf16[256,1152]{1,0:T(8,128)(2,1)S(1)} %reshape.649), channel_id=1, source_target_pairs={{0,6},{1,7},{2,0},{3,1},{4,2},{5,3},{6,4},{7,5},{8,14},{9,15},{10,... | collective-permute-start | bytes 1769480 | tf_op jit(solution)/shard_map/ppermute | solution.py:41
  84.2 12.5 %collective-permute-start.3 = (bf16[128,1152]{1,0:T(8,128)(2,1)S(1)}, bf16[128,1152]{1,0:T(8,128)(2,1)S(1)}, u32[]{:S(2)}, u32[]{:S(2)}) collective-permute-start(bf16[128,1152]{1,0:T(8,128)(2,1)S(1)} %slice.166), channel_id=1, source_target_pairs={{0,2},{1,3},{2,4},{3,5},{4,6},{5,7},{6,0},{7,1},{8,10},{9,11},{10,... | collective-permute-start | bytes 884744 | tf_op jit(solution)/shard_map/ppermute | solution.py:42
  87.4 9.3 %collective-permute-start.4 = (bf16[128,1152]{1,0:T(8,128)(2,1)S(1)}, bf16[128,1152]{1,0:T(8,128)(2,1)S(1)}, u32[]{:S(2)}, u32[]{:S(2)}) collective-permute-start(bf16[128,1152]{1,0:T(8,128)(2,1)S(1)} %slice.167), channel_id=1, source_target_pairs={{0,6},{1,7},{2,0},{3,1},{4,2},{5,3},{6,4},{7,5},{8,14},{9,15},{10,... | collective-permute-start | bytes 884744 | tf_op jit(solution)/shard_map/ppermute | solution.py:43
  90.9 12.0 %collective-permute-start.6 = (bf16[512,1152]{1,0:T(8,128)(2,1)S(1)}, bf16[512,1152]{1,0:T(8,128)(2,1)S(1)}, u32[]{:S(2)}, u32[]{:S(2)}) collective-permute-start(bf16[512,1152]{1,0:T(8,128)(2,1)S(1)} %pad_maximum_fusion), channel_id=1, source_target_pairs={{0,1},{1,0},{2,3},{3,2},{4,5},{5,4},{6,7},{7,6},{8,9},{9,8},{10,11... | collective-permute-start | bytes 3538952 | tf_op jit(solution)/shard_map/ppermute | solution.py:44
  96.8 5.5 %collective-permute-start.5 = (bf16[256,1152]{1,0:T(8,128)(2,1)S(1)}, bf16[256,1152]{1,0:T(8,128)(2,1)S(1)}, u32[]{:S(2)}, u32[]{:S(2)}) collective-permute-start(bf16[256,1152]{1,0:T(8,128)(2,1)S(1)} %constant_dynamic-update-slice_fusion), channel_id=1, source_target_pairs={{0,1},{1,0},{2,3},{3,2},{4,5},{5,4},{6,7},{7,6},{8,9},{9,8},{10,11... | collective-permute-start | bytes 1769480 | tf_op jit(solution)/shard_map/ppermute | solution.py:46

commit v10 on v9

--- a/solution.py
+++ b/solution.py
@@ -5,6 +5,7 @@
 
 CL_OWN = 2
 META = 128
+LANES = 128
 
 
 def tile_best(own_rows, own_key, other_rows, other_key, rows_total):
@@ -36,16 +37,15 @@
     down = perm(lambda y, c: at(y - 1, c))
     rows = block.shape[0]
     half = rows // 2
-    sibling = lax.ppermute(block, "pair", swap)
     from_below = lax.ppermute(block, "pair", up)
     from_above = lax.ppermute(block, "pair", down)
     far_low = lax.ppermute(from_below[:half], "pair", up)
     far_high = lax.ppermute(from_above[half:], "pair", down)
-    siblings = lax.ppermute(jnp.concatenate([from_below, from_above]), "pair", swap)
+    siblings = lax.ppermute(jnp.concatenate([block, from_below, from_above]), "pair", swap)
     far = jnp.concatenate([far_low, far_high])
     far_sibling = lax.ppermute(far, "pair", swap)
-    return [block, sibling, from_below, from_above, far, far_sibling, siblings[:rows],
-            siblings[rows:]]
+    return [block, from_below, from_above, far, far_sibling, siblings[:rows],
+            siblings[rows : 2 * rows], siblings[2 * rows :]]
 
 
 def on_device(embedding, labels, order_ids):
@@ -82,11 +82,11 @@
             query_rows, got_key, block, slot_keys(block, width, rows_total), rows_total
         )
         best_seen = jnp.maximum(best_seen, found)
-    answered = lax.all_to_all(
-        best_seen.reshape(groups, capacity), "dp", split_axis=0, concat_axis=0, tiled=True
-    )
+    lanes = jnp.pad(best_seen.reshape(groups, capacity), ((0, 0), (0, LANES - capacity)))
+    answered = lax.all_to_all(lanes, "dp", split_axis=0, concat_axis=0, tiled=True)
+    answered = answered[:, :capacity].reshape(1, slot_count)
     mine = slot_index[:, None] == jnp.arange(slot_count, dtype=jnp.int32)[None, :]
-    return jnp.max(jnp.where(mine, answered.reshape(1, slot_count), -jnp.inf), axis=1)
+    return jnp.max(jnp.where(mine, answered, -jnp.inf), axis=1)
 
 
 def solution(mesh):

time: 126 us -> 122 us (0.968)
  waiting for transfers between devices: 44 us -> 38.7 us
  blocking collectives: 18.8 us -> 22.2 us
  other arithmetic: 9.78 us -> 8.26 us
  starting transfers between devices: 45.8 us -> 47.2 us
    ppermute x1, waiting for transfers between devices: 9.68 us -> 0.01 us  [pair_blocks(): from_below = lax.ppermute(block, 'pair', up)]
    ppermute x1, waiting for transfers between devices: 1.05 us -> 5.37 us  [pair_blocks(): from_above = lax.ppermute(block, 'pair', down)]
    all_to_all x1, blocking collectives: 18.8 us -> 22.2 us  [on_device(): lax.all_to_all(lanes, 'dp', split_axis=0, concat_axis=0, tiled=True)]
    ppermute x1, starting transfers between devices: 3.93 us -> 6.94 us  [pair_blocks(): far_sibling = lax.ppermute(far, 'pair', swap)]
    ppermute x2 -> x1, starting transfers between devices: 9.64 us -> 7.33 us  [pair_blocks(): lax.ppermute(jnp.concatenate([block, from_below, from_above]), 'pair', swap)]
    ppermute x1, starting transfers between devices: 3.37 us -> 5.32 us  [pair_blocks(): far_high = lax.ppermute(from_above[half:], 'pair', down)]
    ppermute x1, starting transfers between devices: 3.2 us -> 1.92 us  [pair_blocks(): far_low = lax.ppermute(from_below[:half], 'pair', up)]
    ppermute x1, starting transfers between devices: 3.2 us -> 1.92 us  [pair_blocks(): from_below = lax.ppermute(block, 'pair', up)]
  transfers between devices with their start and end apart: 8 -> 7, of which waited for: 4 -> 3; matrix products, arithmetic and copies ran while one was open for 5% -> 3% of each run, Pallas kernels for 0% -> 0%
where the time goes in v10:
time: 122 us; the launch traced here: 121 us
  starting transfers between devices  47.2 us (39%)
  waiting for transfers between devices  38.7 us (32%)
  blocking collectives  22.2 us (18%)
  other arithmetic  8.26 us (7%)
  matrix products  3.13 us (3%)
  local copies, waits for them, and re-layouts  1.67 us (1%)
    all_to_all x1, waiting for transfers between devices, on_device(): lax.all_to_all(send_rows.reshape(groups, capacity, -1), 'dp', split_axis=...  32.4 us
    all_to_all x1, blocking collectives, on_device(): lax.all_to_all(lanes, 'dp', split_axis=0, concat_axis=0, tiled=True)  22.2 us
    all_to_all x1, starting transfers between devices, on_device(): lax.all_to_all(send_rows.reshape(groups, capacity, -1), 'dp', split_axis=...  19.1 us
    ppermute x1, starting transfers between devices, pair_blocks(): lax.ppermute(jnp.concatenate([block, from_below, from_above]), 'pair', swap)  7.33 us
    ppermute x1, starting transfers between devices, pair_blocks(): far_sibling = lax.ppermute(far, 'pair', swap)  6.94 us
    ppermute x1, waiting for transfers between devices, pair_blocks(): from_above = lax.ppermute(block, 'pair', down)  5.37 us
    ppermute x1, starting transfers between devices, pair_blocks(): far_high = lax.ppermute(from_above[half:], 'pair', down)  5.32 us
    ppermute x1, starting transfers between devices, pair_blocks(): from_above = lax.ppermute(block, 'pair', down)  4.64 us
  transfers between devices with their start and end apart: 7, of which 3 were waited for; matrix products, arithmetic and copies ran while one was open for 3% of the time, Pallas kernels for 0%

profile of v10, /device:TPU:1, one launch (start us, length us, event | category | flops | bytes accessed | tf_op | source)
XLA Modules:
  0.0 121.4 jit_solution(5813008059365602646)
XLA Ops:
  0.0 1.1 fusion.12
  1.1 0.7 convert_bitcast_fusion.1
  1.8 0.7 convert_bitcast_fusion
  3.0 1.1 fusion.13
  4.1 1.3 %scatter_custom_fusion = bf16[256,1152]{1,0:T(8,128)(2,1)S(1)} fusion(s32[128]{0:T(128)S(1)} %get-tuple-element.7, s32[]{} %constant.171, bf16[128,3]{1,0:T(8,128)(2,1)S(1)} %copy.10, bf16[]{:T(256)} %constant.138.clone.1, bf16[128,1024]{1,0:T(8,128)(2,1)S(1)} %fusion.13, bf16[]{:T(256)} %constant.166), kind=kCustom, calls=%fused_computation.30 | custom fusion | flops 884736 | bytes 890880 | tf_op jit(solution)/shard_map/scatter | solution.py:71
  5.5 0.9 reshape.567
  6.4 19.1 %all-to-all-start = ((bf16[64,4,1152]{2,1,0:T(4,128)(2,1)}), bf16[64,4,1152]{2,1,0:T(4,128)(2,1)S(1)}, u32[]{:S(2)}, u32[]{:S(2)}) async-start(bf16[64,4,1152]{2,1,0:T(4,128)(2,1)} %reshape.567), calls=%async_computation | async-start | bytes 1179648 | tf_op jit(solution)/shard_map/all_to_all | solution.py:72
  25.5 32.4 %all-to-all-done = bf16[64,4,1152]{2,1,0:T(4,128)(2,1)S(1)} async-done(((bf16[64,4,1152]{2,1,0:T(4,128)(2,1)}), bf16[64,4,1152]{2,1,0:T(4,128)(2,1)S(1)}, u32[]{:S(2)}, u32[]{:S(2)}) %all-to-all-start) | async-done | bytes 589856 | tf_op jit(solution)/shard_map/all_to_all | solution.py:72
  58.0 4.6 %collective-permute-start.1 = (bf16[256,1152]{1,0:T(8,128)(2,1)S(1)}, bf16[256,1152]{1,0:T(8,128)(2,1)S(1)}, u32[]{:S(2)}, u32[]{:S(2)}) collective-permute-start(bf16[256,1152]{1,0:T(8,128)(2,1)S(1)} %reshape.568), channel_id=1, source_target_pairs={{0,6},{1,7},{2,0},{3,1},{4,2},{5,3},{6,4},{7,5},{8,14},{9,15},{10,... | collective-permute-start | bytes 1769480 | tf_op jit(solution)/shard_map/ppermute | solution.py:41
  62.7 1.9 %collective-permute-start = (bf16[256,1152]{1,0:T(8,128)(2,1)S(1)}, bf16[256,1152]{1,0:T(8,128)(2,1)S(1)}, u32[]{:S(2)}, u32[]{:S(2)}) collective-permute-start(bf16[256,1152]{1,0:T(8,128)(2,1)S(1)} %reshape.568), channel_id=1, source_target_pairs={{0,2},{1,3},{2,4},{3,5},{4,6},{5,7},{6,0},{7,1},{8,10},{9,11},{10,... | collective-permute-start | bytes 1769480 | tf_op jit(solution)/shard_map/ppermute | solution.py:40
  65.7 5.4 %collective-permute-done.1 = bf16[256,1152]{1,0:T(8,128)(2,1)S(1)} collective-permute-done((bf16[256,1152]{1,0:T(8,128)(2,1)S(1)}, bf16[256,1152]{1,0:T(8,128)(2,1)S(1)}, u32[]{:S(2)}, u32[]{:S(2)}) %collective-permute-start.1) | collective-permute-done | bytes 589856 | tf_op jit(solution)/shard_map/ppermute | solution.py:41
  71.1 5.3 %collective-permute-start.3 = (bf16[128,1152]{1,0:T(8,128)(2,1)S(1)}, bf16[128,1152]{1,0:T(8,128)(2,1)S(1)}, u32[]{:S(2)}, u32[]{:S(2)}) collective-permute-start(bf16[128,1152]{1,0:T(8,128)(2,1)S(1)} %slice.172), channel_id=1, source_target_pairs={{0,6},{1,7},{2,0},{3,1},{4,2},{5,3},{6,4},{7,5},{8,14},{9,15},{10,... | collective-permute-start | bytes 884744 | tf_op jit(solution)/shard_map/ppermute | solution.py:43
  77.0 1.9 %collective-permute-start.2 = (bf16[128,1152]{1,0:T(8,128)(2,1)S(1)}, bf16[128,1152]{1,0:T(8,128)(2,1)S(1)}, u32[]{:S(2)}, u32[]{:S(2)}) collective-permute-start(bf16[128,1152]{1,0:T(8,128)(2,1)S(1)} %slice.171), channel_id=1, source_target_pairs={{0,2},{1,3},{2,4},{3,5},{4,6},{5,7},{6,0},{7,1},{8,10},{9,11},{10,... | collective-permute-start | bytes 884744 | tf_op jit(solution)/shard_map/ppermute | solution.py:42
  79.0 7.3 %collective-permute-start.5 = (bf16[768,1152]{1,0:T(8,128)(2,1)S(1)}, bf16[768,1152]{1,0:T(8,128)(2,1)S(1)}, u32[]{:S(2)}, u32[]{:S(2)}) collective-permute-start(bf16[768,1152]{1,0:T(8,128)(2,1)S(1)} %pad_maximum_fusion), channel_id=1, source_target_pairs={{0,1},{1,0},{2,3},{3,2},{4,5},{5,4},{6,7},{7,6},{8,9},{9,8},{10,11... | collective-permute-start | bytes 5308424 | tf_op jit(solution)/shard_map/ppermute | solution.py:44
  86.4 0.4 fusion.2
  86.8 0.4 fusion.1
  87.3 6.9 %collective-permute-start.4 = (bf16[256,1152]{1,0:T(8,128)(2,1)S(1)}, bf16[256,1152]{1,0:T(8,128)(2,1)S(1)}, u32[]{:S(2)}, u32[]{:S(2)}) collective-permute-start(bf16[256,1152]{1,0:T(8,128)(2,1)S(1)} %constant_dynamic-update-slice_fusion), channel_id=1, source_target_pairs={{0,1},{1,0},{2,3},{3,2},{4,5},{5,4},{6,7},{7,6},{8,9},{9,8},{10,11... | collective-permute-start | bytes 1769480 | tf_op jit(solution)/shard_map/ppermute | solution.py:46
  94.5 0.4 fusion.3
  94.9 1.0 collective-permute-done.4
  96.1 0.4 fusion.4
  97.1 0.4 fusion.5
  97.9 0.4 fusion.6
  98.4 22.2 %all_to_all.17 = f32[64,1,128]{2,1,0:T(1,128)S(1)} all-to-all(f32[64,1,128]{2,1,0:T(1,128)S(1)} %bitcast.18), channel_id=1, replica_groups=mesh['dp'=64,'pair'=8] {'dp'}, dimensions={0} | all-to-all | bytes 65536 | tf_op jit(solution)/shard_map/all_to_all | solution.py:86
  120.7 0.7 select_reduce_fusion
  (47 shorter events, 4.2 us)
Async XLA Ops:
  6.4 51.5 %all-to-all-start = ((bf16[64,4,1152]{2,1,0:T(4,128)(2,1)}), bf16[64,4,1152]{2,1,0:T(4,128)(2,1)S(1)}, u32[]{:S(2)}, u32[]{:S(2)}) async-start(bf16[64,4,1152]{2,1,0:T(4,128)(2,1)} %reshape.567), calls=%async_computation | async-start | bytes 1179648 | tf_op jit(solution)/shard_map/all_to_all | solution.py:72
  58.0 13.0 %collective-permute-start.1 = (bf16[256,1152]{1,0:T(8,128)(2,1)S(1)}, bf16[256,1152]{1,0:T(8,128)(2,1)S(1)}, u32[]{:S(2)}, u32[]{:S(2)}) collective-permute-start(bf16[256,1152]{1,0:T(8,128)(2,1)S(1)} %reshape.568), channel_id=1, source_target_pairs={{0,6},{1,7},{2,0},{3,1},{4,2},{5,3},{6,4},{7,5},{8,14},{9,15},{10,... | collective-permute-start | bytes 1769480 | tf_op jit(solution)/shard_map/ppermute | solution.py:41
  62.7 14.0 %collective-permute-start = (bf16[256,1152]{1,0:T(8,128)(2,1)S(1)}, bf16[256,1152]{1,0:T(8,128)(2,1)S(1)}, u32[]{:S(2)}, u32[]{:S(2)}) collective-permute-start(bf16[256,1152]{1,0:T(8,128)(2,1)S(1)} %reshape.568), channel_id=1, source_target_pairs={{0,2},{1,3},{2,4},{3,5},{4,6},{5,7},{6,0},{7,1},{8,10},{9,11},{10,... | collective-permute-start | bytes 1769480 | tf_op jit(solution)/shard_map/ppermute | solution.py:40
  71.1 16.1 %collective-permute-start.3 = (bf16[128,1152]{1,0:T(8,128)(2,1)S(1)}, bf16[128,1152]{1,0:T(8,128)(2,1)S(1)}, u32[]{:S(2)}, u32[]{:S(2)}) collective-permute-start(bf16[128,1152]{1,0:T(8,128)(2,1)S(1)} %slice.172), channel_id=1, source_target_pairs={{0,6},{1,7},{2,0},{3,1},{4,2},{5,3},{6,4},{7,5},{8,14},{9,15},{10,... | collective-permute-start | bytes 884744 | tf_op jit(solution)/shard_map/ppermute | solution.py:43
  77.0 10.2 %collective-permute-start.2 = (bf16[128,1152]{1,0:T(8,128)(2,1)S(1)}, bf16[128,1152]{1,0:T(8,128)(2,1)S(1)}, u32[]{:S(2)}, u32[]{:S(2)}) collective-permute-start(bf16[128,1152]{1,0:T(8,128)(2,1)S(1)} %slice.171), channel_id=1, source_target_pairs={{0,2},{1,3},{2,4},{3,5},{4,6},{5,7},{6,0},{7,1},{8,10},{9,11},{10,... | collective-permute-start | bytes 884744 | tf_op jit(solution)/shard_map/ppermute | solution.py:42
  79.0 17.4 %collective-permute-start.5 = (bf16[768,1152]{1,0:T(8,128)(2,1)S(1)}, bf16[768,1152]{1,0:T(8,128)(2,1)S(1)}, u32[]{:S(2)}, u32[]{:S(2)}) collective-permute-start(bf16[768,1152]{1,0:T(8,128)(2,1)S(1)} %pad_maximum_fusion), channel_id=1, source_target_pairs={{0,1},{1,0},{2,3},{3,2},{4,5},{5,4},{6,7},{7,6},{8,9},{9,8},{10,11... | collective-permute-start | bytes 5308424 | tf_op jit(solution)/shard_map/ppermute | solution.py:44
  87.3 8.6 %collective-permute-start.4 = (bf16[256,1152]{1,0:T(8,128)(2,1)S(1)}, bf16[256,1152]{1,0:T(8,128)(2,1)S(1)}, u32[]{:S(2)}, u32[]{:S(2)}) collective-permute-start(bf16[256,1152]{1,0:T(8,128)(2,1)S(1)} %constant_dynamic-update-slice_fusion), channel_id=1, source_target_pairs={{0,1},{1,0},{2,3},{3,2},{4,5},{5,4},{6,7},{7,6},{8,9},{9,8},{10,11... | collective-permute-start | bytes 1769480 | tf_op jit(solution)/shard_map/ppermute | solution.py:46

commit v11 on v9

--- a/solution.py
+++ b/solution.py
@@ -36,16 +36,15 @@
     down = perm(lambda y, c: at(y - 1, c))
     rows = block.shape[0]
     half = rows // 2
-    sibling = lax.ppermute(block, "pair", swap)
     from_below = lax.ppermute(block, "pair", up)
     from_above = lax.ppermute(block, "pair", down)
     far_low = lax.ppermute(from_below[:half], "pair", up)
     far_high = lax.ppermute(from_above[half:], "pair", down)
-    siblings = lax.ppermute(jnp.concatenate([from_below, from_above]), "pair", swap)
+    siblings = lax.ppermute(jnp.concatenate([block, from_below, from_above]), "pair", swap)
     far = jnp.concatenate([far_low, far_high])
     far_sibling = lax.ppermute(far, "pair", swap)
-    return [block, sibling, from_below, from_above, far, far_sibling, siblings[:rows],
-            siblings[rows:]]
+    return [block, from_below, from_above, far, far_sibling, siblings[:rows],
+            siblings[rows : 2 * rows], siblings[2 * rows :]]
 
 
 def on_device(embedding, labels, order_ids):

time: 126 us -> 122 us (0.968)
  waiting for transfers between devices: 44 us -> 40.8 us
  blocking collectives: 18.8 us -> 21.9 us
  starting transfers between devices: 45.8 us -> 44.1 us
    ppermute x1, waiting for transfers between devices: 9.68 us -> 6.18 us  [pair_blocks(): from_below = lax.ppermute(block, 'pair', up)]
    all_to_all x1, blocking collectives: 18.8 us -> 21.9 us  [on_device(): lax.all_to_all(best_seen.reshape(groups, capacity), 'dp', split_axis=0, c...]
    ppermute x2 -> x1, starting transfers between devices: 9.64 us -> 7.83 us  [pair_blocks(): lax.ppermute(jnp.concatenate([block, from_below, from_above]), 'pair', swap)]
  transfers between devices with their start and end apart: 8 -> 7, of which waited for: 4 -> 4; matrix products, arithmetic and copies ran while one was open for 5% -> 3% of each run, Pallas kernels for 0% -> 0%
where the time goes in v11:
time: 122 us; the launch traced here: 121 us
  starting transfers between devices  44.1 us (36%)
  waiting for transfers between devices  40.8 us (33%)
  blocking collectives  21.9 us (18%)
  other arithmetic  8.99 us (7%)
  matrix products  3.15 us (3%)
  local copies, waits for them, and re-layouts  2.17 us (2%)
    all_to_all x1, waiting for transfers between devices, on_device(): lax.all_to_all(send_rows.reshape(groups, capacity, -1), 'dp', split_axis=...  32.4 us
    all_to_all x1, blocking collectives, on_device(): lax.all_to_all(best_seen.reshape(groups, capacity), 'dp', split_axis=0, c...  21.9 us
    all_to_all x1, starting transfers between devices, on_device(): lax.all_to_all(send_rows.reshape(groups, capacity, -1), 'dp', split_axis=...  19.1 us
    ppermute x1, starting transfers between devices, pair_blocks(): lax.ppermute(jnp.concatenate([block, from_below, from_above]), 'pair', swap)  7.83 us
    ppermute x1, waiting for transfers between devices, pair_blocks(): from_below = lax.ppermute(block, 'pair', up)  6.18 us
    ppermute x1, starting transfers between devices, pair_blocks(): far_sibling = lax.ppermute(far, 'pair', swap)  4.04 us
    ppermute x1, starting transfers between devices, pair_blocks(): from_above = lax.ppermute(block, 'pair', down)  3.36 us
    ppermute x1, starting transfers between devices, pair_blocks(): far_high = lax.ppermute(from_above[half:], 'pair', down)  3.36 us
  transfers between devices with their start and end apart: 7, of which 4 were waited for; matrix products, arithmetic and copies ran while one was open for 3% of the time, Pallas kernels for 0%

profile of v11, /device:TPU:1, one launch (start us, length us, event | category | flops | bytes accessed | tf_op | source)
XLA Modules:
  0.0 121.4 jit_solution(1683171127189897043)
XLA Ops:
  0.0 0.7 convert_bitcast_fusion.1
  1.1 0.7 convert_bitcast_fusion
  1.9 1.1 fusion.12
  3.0 1.1 fusion.13
  4.1 1.3 %scatter_custom_fusion = bf16[256,1152]{1,0:T(8,128)(2,1)S(1)} fusion(s32[128]{0:T(128)S(1)} %get-tuple-element.7, s32[]{} %constant.170, bf16[128,3]{1,0:T(8,128)(2,1)S(1)} %copy.10, bf16[]{:T(256)} %constant.137.clone.1, bf16[128,1024]{1,0:T(8,128)(2,1)S(1)} %fusion.13, bf16[]{:T(256)} %constant.165), kind=kCustom, calls=%fused_computation.30 | custom fusion | flops 884736 | bytes 890880 | tf_op jit(solution)/shard_map/scatter | solution.py:70
  5.5 0.9 reshape.648
  6.4 19.1 %all-to-all-start = ((bf16[64,4,1152]{2,1,0:T(4,128)(2,1)}), bf16[64,4,1152]{2,1,0:T(4,128)(2,1)S(1)}, u32[]{:S(2)}, u32[]{:S(2)}) async-start(bf16[64,4,1152]{2,1,0:T(4,128)(2,1)} %reshape.648), calls=%async_computation | async-start | bytes 1179648 | tf_op jit(solution)/shard_map/all_to_all | solution.py:71
  25.5 32.4 %all-to-all-done = bf16[64,4,1152]{2,1,0:T(4,128)(2,1)S(1)} async-done(((bf16[64,4,1152]{2,1,0:T(4,128)(2,1)}), bf16[64,4,1152]{2,1,0:T(4,128)(2,1)S(1)}, u32[]{:S(2)}, u32[]{:S(2)}) %all-to-all-start) | async-done | bytes 589856 | tf_op jit(solution)/shard_map/all_to_all | solution.py:71
  58.0 3.2 %collective-permute-start = (bf16[256,1152]{1,0:T(8,128)(2,1)S(1)}, bf16[256,1152]{1,0:T(8,128)(2,1)S(1)}, u32[]{:S(2)}, u32[]{:S(2)}) collective-permute-start(bf16[256,1152]{1,0:T(8,128)(2,1)S(1)} %reshape.649), channel_id=1, source_target_pairs={{0,2},{1,3},{2,4},{3,5},{4,6},{5,7},{6,0},{7,1},{8,10},{9,11},{10,... | collective-permute-start | bytes 1769480 | tf_op jit(solution)/shard_map/ppermute | solution.py:39
  61.3 3.4 %collective-permute-start.1 = (bf16[256,1152]{1,0:T(8,128)(2,1)S(1)}, bf16[256,1152]{1,0:T(8,128)(2,1)S(1)}, u32[]{:S(2)}, u32[]{:S(2)}) collective-permute-start(bf16[256,1152]{1,0:T(8,128)(2,1)S(1)} %reshape.649), channel_id=1, source_target_pairs={{0,6},{1,7},{2,0},{3,1},{4,2},{5,3},{6,4},{7,5},{8,14},{9,15},{10,... | collective-permute-start | bytes 1769480 | tf_op jit(solution)/shard_map/ppermute | solution.py:40
  65.7 6.2 %collective-permute-done = bf16[256,1152]{1,0:T(8,128)(2,1)S(1)} collective-permute-done((bf16[256,1152]{1,0:T(8,128)(2,1)S(1)}, bf16[256,1152]{1,0:T(8,128)(2,1)S(1)}, u32[]{:S(2)}, u32[]{:S(2)}) %collective-permute-start) | collective-permute-done | bytes 589856 | tf_op jit(solution)/shard_map/ppermute | solution.py:39
  72.1 1.3 %collective-permute-done.1 = bf16[256,1152]{1,0:T(8,128)(2,1)S(1)} collective-permute-done((bf16[256,1152]{1,0:T(8,128)(2,1)S(1)}, bf16[256,1152]{1,0:T(8,128)(2,1)S(1)}, u32[]{:S(2)}, u32[]{:S(2)}) %collective-permute-start.1) | collective-permute-done | bytes 589856 | tf_op jit(solution)/shard_map/ppermute | solution.py:40
  73.7 3.2 %collective-permute-start.2 = (bf16[128,1152]{1,0:T(8,128)(2,1)S(1)}, bf16[128,1152]{1,0:T(8,128)(2,1)S(1)}, u32[]{:S(2)}, u32[]{:S(2)}) collective-permute-start(bf16[128,1152]{1,0:T(8,128)(2,1)S(1)} %slice.167), channel_id=1, source_target_pairs={{0,2},{1,3},{2,4},{3,5},{4,6},{5,7},{6,0},{7,1},{8,10},{9,11},{10,... | collective-permute-start | bytes 884744 | tf_op jit(solution)/shard_map/ppermute | solution.py:41
  77.0 3.4 %collective-permute-start.3 = (bf16[128,1152]{1,0:T(8,128)(2,1)S(1)}, bf16[128,1152]{1,0:T(8,128)(2,1)S(1)}, u32[]{:S(2)}, u32[]{:S(2)}) collective-permute-start(bf16[128,1152]{1,0:T(8,128)(2,1)S(1)} %slice.168), channel_id=1, source_target_pairs={{0,6},{1,7},{2,0},{3,1},{4,2},{5,3},{6,4},{7,5},{8,14},{9,15},{10,... | collective-permute-start | bytes 884744 | tf_op jit(solution)/shard_map/ppermute | solution.py:42
  80.5 7.8 %collective-permute-start.5 = (bf16[768,1152]{1,0:T(8,128)(2,1)S(1)}, bf16[768,1152]{1,0:T(8,128)(2,1)S(1)}, u32[]{:S(2)}, u32[]{:S(2)}) collective-permute-start(bf16[768,1152]{1,0:T(8,128)(2,1)S(1)} %pad_maximum_fusion), channel_id=1, source_target_pairs={{0,1},{1,0},{2,3},{3,2},{4,5},{5,4},{6,7},{7,6},{8,9},{9,8},{10,11... | collective-permute-start | bytes 5308424 | tf_op jit(solution)/shard_map/ppermute | solution.py:43
  89.2 4.0 %collective-permute-start.4 = (bf16[256,1152]{1,0:T(8,128)(2,1)S(1)}, bf16[256,1152]{1,0:T(8,128)(2,1)S(1)}, u32[]{:S(2)}, u32[]{:S(2)}) collective-permute-start(bf16[256,1152]{1,0:T(8,128)(2,1)S(1)} %constant_dynamic-update-slice_fusion), channel_id=1, source_target_pairs={{0,1},{1,0},{2,3},{3,2},{4,5},{5,4},{6,7},{7,6},{8,9},{9,8},{10,11... | collective-permute-start | bytes 1769480 | tf_op jit(solution)/shard_map/ppermute | solution.py:45
  93.5 0.4 fusion.3
  93.9 1.0 collective-permute-done.4
  95.1 0.4 fusion.4
  96.2 0.4 fusion.5
  97.5 21.9 %all_to_all.11 = f32[64,1,4]{2,1,0:T(1,128)S(1)} all-to-all(f32[64,1,4]{2,1,0:T(1,128)S(1)} %bitcast.13), channel_id=1, replica_groups=mesh['dp'=64,'pair'=8] {'dp'}, dimensions={0} | all-to-all | bytes 2048 | tf_op jit(solution)/shard_map/all_to_all | solution.py:84
  119.3 0.5 broadcast.619
  119.8 0.7 reduce.21
  120.7 0.7 select_reduce_fusion
  (48 shorter events, 5.4 us)
Async XLA Ops:
  6.4 51.5 %all-to-all-start = ((bf16[64,4,1152]{2,1,0:T(4,128)(2,1)}), bf16[64,4,1152]{2,1,0:T(4,128)(2,1)S(1)}, u32[]{:S(2)}, u32[]{:S(2)}) async-start(bf16[64,4,1152]{2,1,0:T(4,128)(2,1)} %reshape.648), calls=%async_computation | async-start | bytes 1179648 | tf_op jit(solution)/shard_map/all_to_all | solution.py:71
  58.0 13.8 %collective-permute-start = (bf16[256,1152]{1,0:T(8,128)(2,1)S(1)}, bf16[256,1152]{1,0:T(8,128)(2,1)S(1)}, u32[]{:S(2)}, u32[]{:S(2)}) collective-permute-start(bf16[256,1152]{1,0:T(8,128)(2,1)S(1)} %reshape.649), channel_id=1, source_target_pairs={{0,2},{1,3},{2,4},{3,5},{4,6},{5,7},{6,0},{7,1},{8,10},{9,11},{10,... | collective-permute-start | bytes 1769480 | tf_op jit(solution)/shard_map/ppermute | solution.py:39
  61.3 12.2 %collective-permute-start.1 = (bf16[256,1152]{1,0:T(8,128)(2,1)S(1)}, bf16[256,1152]{1,0:T(8,128)(2,1)S(1)}, u32[]{:S(2)}, u32[]{:S(2)}) collective-permute-start(bf16[256,1152]{1,0:T(8,128)(2,1)S(1)} %reshape.649), channel_id=1, source_target_pairs={{0,6},{1,7},{2,0},{3,1},{4,2},{5,3},{6,4},{7,5},{8,14},{9,15},{10,... | collective-permute-start | bytes 1769480 | tf_op jit(solution)/shard_map/ppermute | solution.py:40
  73.7 15.4 %collective-permute-start.2 = (bf16[128,1152]{1,0:T(8,128)(2,1)S(1)}, bf16[128,1152]{1,0:T(8,128)(2,1)S(1)}, u32[]{:S(2)}, u32[]{:S(2)}) collective-permute-start(bf16[128,1152]{1,0:T(8,128)(2,1)S(1)} %slice.167), channel_id=1, source_target_pairs={{0,2},{1,3},{2,4},{3,5},{4,6},{5,7},{6,0},{7,1},{8,10},{9,11},{10,... | collective-permute-start | bytes 884744 | tf_op jit(solution)/shard_map/ppermute | solution.py:41
  77.0 12.2 %collective-permute-start.3 = (bf16[128,1152]{1,0:T(8,128)(2,1)S(1)}, bf16[128,1152]{1,0:T(8,128)(2,1)S(1)}, u32[]{:S(2)}, u32[]{:S(2)}) collective-permute-start(bf16[128,1152]{1,0:T(8,128)(2,1)S(1)} %slice.168), channel_id=1, source_target_pairs={{0,6},{1,7},{2,0},{3,1},{4,2},{5,3},{6,4},{7,5},{8,14},{9,15},{10,... | collective-permute-start | bytes 884744 | tf_op jit(solution)/shard_map/ppermute | solution.py:42
  80.5 15.0 %collective-permute-start.5 = (bf16[768,1152]{1,0:T(8,128)(2,1)S(1)}, bf16[768,1152]{1,0:T(8,128)(2,1)S(1)}, u32[]{:S(2)}, u32[]{:S(2)}) collective-permute-start(bf16[768,1152]{1,0:T(8,128)(2,1)S(1)} %pad_maximum_fusion), channel_id=1, source_target_pairs={{0,1},{1,0},{2,3},{3,2},{4,5},{5,4},{6,7},{7,6},{8,9},{9,8},{10,11... | collective-permute-start | bytes 5308424 | tf_op jit(solution)/shard_map/ppermute | solution.py:43
  89.2 5.7 %collective-permute-start.4 = (bf16[256,1152]{1,0:T(8,128)(2,1)S(1)}, bf16[256,1152]{1,0:T(8,128)(2,1)S(1)}, u32[]{:S(2)}, u32[]{:S(2)}) collective-permute-start(bf16[256,1152]{1,0:T(8,128)(2,1)S(1)} %constant_dynamic-update-slice_fusion), channel_id=1, source_target_pairs={{0,1},{1,0},{2,3},{3,2},{4,5},{5,4},{6,7},{7,6},{8,9},{9,8},{10,11... | collective-permute-start | bytes 1769480 | tf_op jit(solution)/shard_map/ppermute | solution.py:45

commit v12 on v11

--- a/solution.py
+++ b/solution.py
@@ -34,14 +34,13 @@
     swap = perm(lambda y, c: at(y, 1 - c))
     up = perm(lambda y, c: at(y + 1, c))
     down = perm(lambda y, c: at(y - 1, c))
+    relay = perm(lambda y, c: at(y + 1, c) if c == 0 else at(y - 1, c))
     rows = block.shape[0]
-    half = rows // 2
     from_below = lax.ppermute(block, "pair", up)
     from_above = lax.ppermute(block, "pair", down)
-    far_low = lax.ppermute(from_below[:half], "pair", up)
-    far_high = lax.ppermute(from_above[half:], "pair", down)
+    core = lax.axis_index("pair") % 2
+    far = lax.ppermute(jnp.where(core == 0, from_below, from_above), "pair", relay)
     siblings = lax.ppermute(jnp.concatenate([block, from_below, from_above]), "pair", swap)
-    far = jnp.concatenate([far_low, far_high])
     far_sibling = lax.ppermute(far, "pair", swap)
     return [block, from_below, from_above, far, far_sibling, siblings[:rows],
             siblings[rows : 2 * rows], siblings[2 * rows :]]

time: 122 us -> 122 us (level)
    ppermute x1, starting transfers between devices: 4.04 us -> 8.51 us  [pair_blocks(): far_sibling = lax.ppermute(far, 'pair', swap)]
    ppermute x2 -> x1, starting transfers between devices: 6.56 us -> 4.64 us  [pair_blocks(): lax.ppermute(jnp.where(core == 0, from_below, from_above), 'pair', relay)]
    ppermute x1, starting transfers between devices: 7.83 us -> 6.23 us  [pair_blocks(): lax.ppermute(jnp.concatenate([block, from_below, from_above]), 'pair', swap)]
  transfers between devices with their start and end apart: 7 -> 6, of which waited for: 4 -> 4; matrix products, arithmetic and copies ran while one was open for 3% -> 3% of each run, Pallas kernels for 0% -> 0%
where the time goes in v12:
time: 122 us
  starting transfers between devices  45.1 us (37%)
  waiting for transfers between devices  40.8 us (33%)
  blocking collectives  21.5 us (18%)
  other arithmetic  9.06 us (7%)
  matrix products  3.14 us (3%)
  local copies, waits for them, and re-layouts  2.07 us (2%)
    all_to_all x1, waiting for transfers between devices, on_device(): lax.all_to_all(send_rows.reshape(groups, capacity, -1), 'dp', split_axis=...  32.3 us
    all_to_all x1, blocking collectives, on_device(): lax.all_to_all(best_seen.reshape(groups, capacity), 'dp', split_axis=0, c...  21.5 us
    all_to_all x1, starting transfers between devices, on_device(): lax.all_to_all(send_rows.reshape(groups, capacity, -1), 'dp', split_axis=...  19.1 us
    ppermute x1, starting transfers between devices, pair_blocks(): far_sibling = lax.ppermute(far, 'pair', swap)  8.51 us
    ppermute x1, starting transfers between devices, pair_blocks(): lax.ppermute(jnp.concatenate([block, from_below, from_above]), 'pair', swap)  6.23 us
    ppermute x1, waiting for transfers between devices, pair_blocks(): from_below = lax.ppermute(block, 'pair', up)  6.18 us
    ppermute x1, starting transfers between devices, pair_blocks(): lax.ppermute(jnp.where(core == 0, from_below, from_above), 'pair', relay)  4.64 us
    ppermute x1, starting transfers between devices, pair_blocks(): from_above = lax.ppermute(block, 'pair', down)  3.36 us
  transfers between devices with their start and end apart: 6, of which 4 were waited for; matrix products, arithmetic and copies ran while one was open for 3% of the time, Pallas kernels for 0%

profile of v12, /device:TPU:1, one launch (start us, length us, event | category | flops | bytes accessed | tf_op | source)
XLA Modules:
  0.0 121.9 jit_solution(11469189019943352696)
XLA Ops:
  0.0 0.7 convert_bitcast_fusion.1
  1.1 0.7 convert_bitcast_fusion
  1.9 1.1 fusion.12
  3.0 1.1 fusion.13
  4.1 1.3 %scatter_custom_fusion = bf16[256,1152]{1,0:T(8,128)(2,1)S(1)} fusion(s32[128]{0:T(128)S(1)} %get-tuple-element.7, s32[]{} %constant.182, bf16[128,3]{1,0:T(8,128)(2,1)S(1)} %copy.10, bf16[]{:T(256)} %constant.149.clone.1, bf16[128,1024]{1,0:T(8,128)(2,1)S(1)} %fusion.13, bf16[]{:T(256)} %constant.179), kind=kCustom, calls=%fused_computation.31 | custom fusion | flops 884736 | bytes 890880 | tf_op jit(solution)/shard_map/scatter | solution.py:69
  5.5 0.9 reshape.648
  6.4 19.1 %all-to-all-start = ((bf16[64,4,1152]{2,1,0:T(4,128)(2,1)}), bf16[64,4,1152]{2,1,0:T(4,128)(2,1)S(1)}, u32[]{:S(2)}, u32[]{:S(2)}) async-start(bf16[64,4,1152]{2,1,0:T(4,128)(2,1)} %reshape.648), calls=%async_computation | async-start | bytes 1179648 | tf_op jit(solution)/shard_map/all_to_all | solution.py:70
  25.5 32.3 %all-to-all-done = bf16[64,4,1152]{2,1,0:T(4,128)(2,1)S(1)} async-done(((bf16[64,4,1152]{2,1,0:T(4,128)(2,1)}), bf16[64,4,1152]{2,1,0:T(4,128)(2,1)S(1)}, u32[]{:S(2)}, u32[]{:S(2)}) %all-to-all-start) | async-done | bytes 589856 | tf_op jit(solution)/shard_map/all_to_all | solution.py:70
  58.0 3.2 %collective-permute-start = (bf16[256,1152]{1,0:T(8,128)(2,1)S(1)}, bf16[256,1152]{1,0:T(8,128)(2,1)S(1)}, u32[]{:S(2)}, u32[]{:S(2)}) collective-permute-start(bf16[256,1152]{1,0:T(8,128)(2,1)S(1)} %reshape.649), channel_id=1, source_target_pairs={{0,2},{1,3},{2,4},{3,5},{4,6},{5,7},{6,0},{7,1},{8,10},{9,11},{10,... | collective-permute-start | bytes 1769480 | tf_op jit(solution)/shard_map/ppermute | solution.py:39
  61.3 3.4 %collective-permute-start.1 = (bf16[256,1152]{1,0:T(8,128)(2,1)S(1)}, bf16[256,1152]{1,0:T(8,128)(2,1)S(1)}, u32[]{:S(2)}, u32[]{:S(2)}) collective-permute-start(bf16[256,1152]{1,0:T(8,128)(2,1)S(1)} %reshape.649), channel_id=1, source_target_pairs={{0,6},{1,7},{2,0},{3,1},{4,2},{5,3},{6,4},{7,5},{8,14},{9,15},{10,... | collective-permute-start | bytes 1769480 | tf_op jit(solution)/shard_map/ppermute | solution.py:40
  65.7 6.2 %collective-permute-done = bf16[256,1152]{1,0:T(8,128)(2,1)S(1)} collective-permute-done((bf16[256,1152]{1,0:T(8,128)(2,1)S(1)}, bf16[256,1152]{1,0:T(8,128)(2,1)S(1)}, u32[]{:S(2)}, u32[]{:S(2)}) %collective-permute-start) | collective-permute-done | bytes 589856 | tf_op jit(solution)/shard_map/ppermute | solution.py:39
  72.1 1.3 %collective-permute-done.1 = bf16[256,1152]{1,0:T(8,128)(2,1)S(1)} collective-permute-done((bf16[256,1152]{1,0:T(8,128)(2,1)S(1)}, bf16[256,1152]{1,0:T(8,128)(2,1)S(1)}, u32[]{:S(2)}, u32[]{:S(2)}) %collective-permute-start.1) | collective-permute-done | bytes 589856 | tf_op jit(solution)/shard_map/ppermute | solution.py:40
  73.8 4.6 %collective-permute-start.2 = (bf16[256,1152]{1,0:T(8,128)(2,1)S(1)}, bf16[256,1152]{1,0:T(8,128)(2,1)S(1)}, u32[]{:S(2)}, u32[]{:S(2)}) collective-permute-start(bf16[256,1152]{1,0:T(8,128)(2,1)S(1)} %broadcast_select_fusion), channel_id=1, source_target_pairs={{0,2},{1,7},{2,4},{3,1},{4,6},{5,3},{6,0},{7,5},{8,10},{9,15},{10,... | collective-permute-start | bytes 1769480 | tf_op jit(solution)/shard_map/ppermute | solution.py:42
  78.6 6.2 %collective-permute-start.4 = (bf16[768,1152]{1,0:T(8,128)(2,1)S(1)}, bf16[768,1152]{1,0:T(8,128)(2,1)S(1)}, u32[]{:S(2)}, u32[]{:S(2)}) collective-permute-start(bf16[768,1152]{1,0:T(8,128)(2,1)S(1)} %pad_maximum_fusion), channel_id=1, source_target_pairs={{0,1},{1,0},{2,3},{3,2},{4,5},{5,4},{6,7},{7,6},{8,9},{9,8},{10,11... | collective-permute-start | bytes 5308424 | tf_op jit(solution)/shard_map/ppermute | solution.py:43
  84.8 0.4 fusion.1
  85.6 8.5 %collective-permute-start.3 = (bf16[256,1152]{1,0:T(8,128)(2,1)S(1)}, bf16[256,1152]{1,0:T(8,128)(2,1)S(1)}, u32[]{:S(2)}, u32[]{:S(2)}) collective-permute-start(bf16[256,1152]{1,0:T(8,128)(2,1)S(1)} %collective-permute-done.2), channel_id=1, source_target_pairs={{0,1},{1,0},{2,3},{3,2},{4,5},{5,4},{6,7},{7,6},{8,9},{9,8},{10,11... | collective-permute-start | bytes 1769480 | tf_op jit(solution)/shard_map/ppermute | solution.py:44
  94.4 0.4 fusion.3
  94.8 1.0 collective-permute-done.3
  96.0 0.4 fusion.4
  97.0 0.4 fusion.5
  98.3 21.5 %all_to_all.11 = f32[64,1,4]{2,1,0:T(1,128)S(1)} all-to-all(f32[64,1,4]{2,1,0:T(1,128)S(1)} %bitcast.13), channel_id=1, replica_groups=mesh['dp'=64,'pair'=8] {'dp'}, dimensions={0} | all-to-all | bytes 2048 | tf_op jit(solution)/shard_map/all_to_all | solution.py:83
  119.9 0.5 broadcast.620
  120.4 0.7 reduce.21
  121.2 0.7 select_reduce_fusion
  (43 shorter events, 5.0 us)
Async XLA Ops:
  6.4 51.5 %all-to-all-start = ((bf16[64,4,1152]{2,1,0:T(4,128)(2,1)}), bf16[64,4,1152]{2,1,0:T(4,128)(2,1)S(1)}, u32[]{:S(2)}, u32[]{:S(2)}) async-start(bf16[64,4,1152]{2,1,0:T(4,128)(2,1)} %reshape.648), calls=%async_computation | async-start | bytes 1179648 | tf_op jit(solution)/shard_map/all_to_all | solution.py:70
  58.0 13.8 %collective-permute-start = (bf16[256,1152]{1,0:T(8,128)(2,1)S(1)}, bf16[256,1152]{1,0:T(8,128)(2,1)S(1)}, u32[]{:S(2)}, u32[]{:S(2)}) collective-permute-start(bf16[256,1152]{1,0:T(8,128)(2,1)S(1)} %reshape.649), channel_id=1, source_target_pairs={{0,2},{1,3},{2,4},{3,5},{4,6},{5,7},{6,0},{7,1},{8,10},{9,11},{10,... | collective-permute-start | bytes 1769480 | tf_op jit(solution)/shard_map/ppermute | solution.py:39
  61.3 12.2 %collective-permute-start.1 = (bf16[256,1152]{1,0:T(8,128)(2,1)S(1)}, bf16[256,1152]{1,0:T(8,128)(2,1)S(1)}, u32[]{:S(2)}, u32[]{:S(2)}) collective-permute-start(bf16[256,1152]{1,0:T(8,128)(2,1)S(1)} %reshape.649), channel_id=1, source_target_pairs={{0,6},{1,7},{2,0},{3,1},{4,2},{5,3},{6,4},{7,5},{8,14},{9,15},{10,... | collective-permute-start | bytes 1769480 | tf_op jit(solution)/shard_map/ppermute | solution.py:40
  73.8 11.8 %collective-permute-start.2 = (bf16[256,1152]{1,0:T(8,128)(2,1)S(1)}, bf16[256,1152]{1,0:T(8,128)(2,1)S(1)}, u32[]{:S(2)}, u32[]{:S(2)}) collective-permute-start(bf16[256,1152]{1,0:T(8,128)(2,1)S(1)} %broadcast_select_fusion), channel_id=1, source_target_pairs={{0,2},{1,7},{2,4},{3,1},{4,6},{5,3},{6,0},{7,5},{8,10},{9,15},{10,... | collective-permute-start | bytes 1769480 | tf_op jit(solution)/shard_map/ppermute | solution.py:42
  78.6 17.8 %collective-permute-start.4 = (bf16[768,1152]{1,0:T(8,128)(2,1)S(1)}, bf16[768,1152]{1,0:T(8,128)(2,1)S(1)}, u32[]{:S(2)}, u32[]{:S(2)}) collective-permute-start(bf16[768,1152]{1,0:T(8,128)(2,1)S(1)} %pad_maximum_fusion), channel_id=1, source_target_pairs={{0,1},{1,0},{2,3},{3,2},{4,5},{5,4},{6,7},{7,6},{8,9},{9,8},{10,11... | collective-permute-start | bytes 5308424 | tf_op jit(solution)/shard_map/ppermute | solution.py:43
  85.6 10.1 %collective-permute-start.3 = (bf16[256,1152]{1,0:T(8,128)(2,1)S(1)}, bf16[256,1152]{1,0:T(8,128)(2,1)S(1)}, u32[]{:S(2)}, u32[]{:S(2)}) collective-permute-start(bf16[256,1152]{1,0:T(8,128)(2,1)S(1)} %collective-permute-done.2), channel_id=1, source_target_pairs={{0,1},{1,0},{2,3},{3,2},{4,5},{5,4},{6,7},{7,6},{8,9},{9,8},{10,11... | collective-permute-start | bytes 1769480 | tf_op jit(solution)/shard_map/ppermute | solution.py:44

commit v13 on v10

--- a/solution.py
+++ b/solution.py
@@ -44,8 +44,7 @@
     siblings = lax.ppermute(jnp.concatenate([block, from_below, from_above]), "pair", swap)
     far = jnp.concatenate([far_low, far_high])
     far_sibling = lax.ppermute(far, "pair", swap)
-    return [block, from_below, from_above, far, far_sibling, siblings[:rows],
-            siblings[rows : 2 * rows], siblings[2 * rows :]]
+    return [block, from_below, from_above, far, far_sibling, siblings]
 
 
 def on_device(embedding, labels, order_ids):
@@ -65,8 +64,10 @@
     )
     before = jnp.cumsum(onehot, axis=0) - onehot
     slot_index = owner_group * capacity + jnp.sum(before * onehot, axis=1)
-    meta = jnp.stack([labels + 1, order_ids // 256, order_ids % 256], axis=1).astype(jnp.bfloat16)
-    meta = jnp.pad(meta, ((0, 0), (0, META - 3)))
+    meta_column = lax.broadcasted_iota(jnp.int32, (rows_here, META), 1)
+    meta = jnp.where(meta_column == 0, labels[:, None] + 1, 0)
+    meta = jnp.where(meta_column == 1, order_ids[:, None] // 256, meta)
+    meta = jnp.where(meta_column == 2, order_ids[:, None] % 256, meta).astype(jnp.bfloat16)
     packed = jnp.concatenate([unit_rows, meta], axis=1)
     send_rows = jnp.zeros((slot_count, width + META), jnp.bfloat16).at[slot_index].set(packed)
     got_rows = lax.all_to_all(

time: 122 us -> 121 us (level)
    another operation x3 -> x0, other arithmetic: 1.35 us -> none  [on_device(): jnp.stack([labels + 1, order_ids // 256, order_ids % 256], axis=1)]
    dot_general x8 -> x6, matrix products: 3.13 us -> 2.78 us  [tile_best(): scores = jnp.dot(own_rows, other_rows.T, preferred_element_type=jnp.float32)]
where the time goes in v13:
time: 121 us; the launch traced here: 120 us
  starting transfers between devices  47.2 us (39%)
  waiting for transfers between devices  38.7 us (32%)
  blocking collectives  22.2 us (18%)
  other arithmetic  7.56 us (6%)
  matrix products  2.78 us (2%)
  local copies, waits for them, and re-layouts  1.53 us (1%)
    all_to_all x1, waiting for transfers between devices, on_device(): lax.all_to_all(send_rows.reshape(groups, capacity, -1), 'dp', split_axis=...  32.4 us
    all_to_all x1, blocking collectives, on_device(): lax.all_to_all(lanes, 'dp', split_axis=0, concat_axis=0, tiled=True)  22.2 us
    all_to_all x1, starting transfers between devices, on_device(): lax.all_to_all(send_rows.reshape(groups, capacity, -1), 'dp', split_axis=...  19.1 us
    ppermute x1, starting transfers between devices, pair_blocks(): lax.ppermute(jnp.concatenate([block, from_below, from_above]), 'pair', swap)  7.33 us
    ppermute x1, starting transfers between devices, pair_blocks(): far_sibling = lax.ppermute(far, 'pair', swap)  6.94 us
    ppermute x1, waiting for transfers between devices, pair_blocks(): from_above = lax.ppermute(block, 'pair', down)  5.38 us
    ppermute x1, starting transfers between devices, pair_blocks(): far_high = lax.ppermute(from_above[half:], 'pair', down)  5.32 us
    ppermute x1, starting transfers between devices, pair_blocks(): from_above = lax.ppermute(block, 'pair', down)  4.64 us
  transfers between devices with their start and end apart: 7, of which 3 were waited for; matrix products, arithmetic and copies ran while one was open for 3% of the time, Pallas kernels for 0%

profile of v13, /device:TPU:1, one launch (start us, length us, event | category | flops | bytes accessed | tf_op | source)
XLA Modules:
  0.0 120.2 jit_solution(4905598729732638719)
XLA Ops:
  0.0 1.1 fusion.6
  1.1 0.7 and_select_fusion.6
  2.2 1.1 fusion.7
  3.4 1.3 %scatter_custom_fusion = bf16[256,1152]{1,0:T(8,128)(2,1)S(1)} fusion(s32[128]{0:T(128)S(1)} %get-tuple-element.7, bf16[128,128]{1,0:T(8,128)(2,1)S(1)} %select_convert_fusion, bf16[]{:T(256)} %constant.153, bf16[128,1024]{1,0:T(8,128)(2,1)S(1)} %fusion.7, bf16[]{:T(256)} %constant.128.clone.1), kind=kCustom, calls=%fused_computation.25 | custom fusion | flops 589824 | bytes 884740 | tf_op jit(solution)/shard_map/scatter | solution.py:72
  4.8 0.9 reshape.465
  5.7 19.1 %all-to-all-start = ((bf16[64,4,1152]{2,1,0:T(4,128)(2,1)}), bf16[64,4,1152]{2,1,0:T(4,128)(2,1)S(1)}, u32[]{:S(2)}, u32[]{:S(2)}) async-start(bf16[64,4,1152]{2,1,0:T(4,128)(2,1)} %reshape.465), calls=%async_computation | async-start | bytes 1179648 | tf_op jit(solution)/shard_map/all_to_all | solution.py:73
  24.9 32.4 %all-to-all-done = bf16[64,4,1152]{2,1,0:T(4,128)(2,1)S(1)} async-done(((bf16[64,4,1152]{2,1,0:T(4,128)(2,1)}), bf16[64,4,1152]{2,1,0:T(4,128)(2,1)S(1)}, u32[]{:S(2)}, u32[]{:S(2)}) %all-to-all-start) | async-done | bytes 589856 | tf_op jit(solution)/shard_map/all_to_all | solution.py:73
  57.4 4.6 %collective-permute-start.1 = (bf16[256,1152]{1,0:T(8,128)(2,1)S(1)}, bf16[256,1152]{1,0:T(8,128)(2,1)S(1)}, u32[]{:S(2)}, u32[]{:S(2)}) collective-permute-start(bf16[256,1152]{1,0:T(8,128)(2,1)S(1)} %reshape.466), channel_id=1, source_target_pairs={{0,6},{1,7},{2,0},{3,1},{4,2},{5,3},{6,4},{7,5},{8,14},{9,15},{10,... | collective-permute-start | bytes 1769480 | tf_op jit(solution)/shard_map/ppermute | solution.py:41
  62.0 1.9 %collective-permute-start = (bf16[256,1152]{1,0:T(8,128)(2,1)S(1)}, bf16[256,1152]{1,0:T(8,128)(2,1)S(1)}, u32[]{:S(2)}, u32[]{:S(2)}) collective-permute-start(bf16[256,1152]{1,0:T(8,128)(2,1)S(1)} %reshape.466), channel_id=1, source_target_pairs={{0,2},{1,3},{2,4},{3,5},{4,6},{5,7},{6,0},{7,1},{8,10},{9,11},{10,... | collective-permute-start | bytes 1769480 | tf_op jit(solution)/shard_map/ppermute | solution.py:40
  64.6 0.4 fusion.1
  65.0 5.4 %collective-permute-done.1 = bf16[256,1152]{1,0:T(8,128)(2,1)S(1)} collective-permute-done((bf16[256,1152]{1,0:T(8,128)(2,1)S(1)}, bf16[256,1152]{1,0:T(8,128)(2,1)S(1)}, u32[]{:S(2)}, u32[]{:S(2)}) %collective-permute-start.1) | collective-permute-done | bytes 589856 | tf_op jit(solution)/shard_map/ppermute | solution.py:41
  70.4 5.3 %collective-permute-start.3 = (bf16[128,1152]{1,0:T(8,128)(2,1)S(1)}, bf16[128,1152]{1,0:T(8,128)(2,1)S(1)}, u32[]{:S(2)}, u32[]{:S(2)}) collective-permute-start(bf16[128,1152]{1,0:T(8,128)(2,1)S(1)} %slice.125), channel_id=1, source_target_pairs={{0,6},{1,7},{2,0},{3,1},{4,2},{5,3},{6,4},{7,5},{8,14},{9,15},{10,... | collective-permute-start | bytes 884744 | tf_op jit(solution)/shard_map/ppermute | solution.py:43
  76.3 1.9 %collective-permute-start.2 = (bf16[128,1152]{1,0:T(8,128)(2,1)S(1)}, bf16[128,1152]{1,0:T(8,128)(2,1)S(1)}, u32[]{:S(2)}, u32[]{:S(2)}) collective-permute-start(bf16[128,1152]{1,0:T(8,128)(2,1)S(1)} %slice.124), channel_id=1, source_target_pairs={{0,2},{1,3},{2,4},{3,5},{4,6},{5,7},{6,0},{7,1},{8,10},{9,11},{10,... | collective-permute-start | bytes 884744 | tf_op jit(solution)/shard_map/ppermute | solution.py:42
  78.4 7.3 %collective-permute-start.5 = (bf16[768,1152]{1,0:T(8,128)(2,1)S(1)}, bf16[768,1152]{1,0:T(8,128)(2,1)S(1)}, u32[]{:S(2)}, u32[]{:S(2)}) collective-permute-start(bf16[768,1152]{1,0:T(8,128)(2,1)S(1)} %pad_maximum_fusion), channel_id=1, source_target_pairs={{0,1},{1,0},{2,3},{3,2},{4,5},{5,4},{6,7},{7,6},{8,9},{9,8},{10,11... | collective-permute-start | bytes 5308424 | tf_op jit(solution)/shard_map/ppermute | solution.py:44
  85.7 0.4 fusion.3
  86.1 0.4 fusion.2
  86.6 6.9 %collective-permute-start.4 = (bf16[256,1152]{1,0:T(8,128)(2,1)S(1)}, bf16[256,1152]{1,0:T(8,128)(2,1)S(1)}, u32[]{:S(2)}, u32[]{:S(2)}) collective-permute-start(bf16[256,1152]{1,0:T(8,128)(2,1)S(1)} %constant_dynamic-update-slice_fusion), channel_id=1, source_target_pairs={{0,1},{1,0},{2,3},{3,2},{4,5},{5,4},{6,7},{7,6},{8,9},{9,8},{10,11... | collective-permute-start | bytes 1769480 | tf_op jit(solution)/shard_map/ppermute | solution.py:46
  93.8 0.4 fusion.4
  94.2 1.0 collective-permute-done.4
  95.4 0.4 fusion.5
  95.9 0.4 fusion.8
  96.3 0.8 fusion
  97.2 22.2 %all_to_all.17 = f32[64,1,128]{2,1,0:T(1,128)S(1)} all-to-all(f32[64,1,128]{2,1,0:T(1,128)S(1)} %bitcast.13), channel_id=1, replica_groups=mesh['dp'=64,'pair'=8] {'dp'}, dimensions={0} | all-to-all | bytes 65536 | tf_op jit(solution)/shard_map/all_to_all | solution.py:87
  119.5 0.7 select_reduce_fusion
  (42 shorter events, 2.9 us)
Async XLA Ops:
  5.7 51.5 %all-to-all-start = ((bf16[64,4,1152]{2,1,0:T(4,128)(2,1)}), bf16[64,4,1152]{2,1,0:T(4,128)(2,1)S(1)}, u32[]{:S(2)}, u32[]{:S(2)}) async-start(bf16[64,4,1152]{2,1,0:T(4,128)(2,1)} %reshape.465), calls=%async_computation | async-start | bytes 1179648 | tf_op jit(solution)/shard_map/all_to_all | solution.py:73
  57.4 13.0 %collective-permute-start.1 = (bf16[256,1152]{1,0:T(8,128)(2,1)S(1)}, bf16[256,1152]{1,0:T(8,128)(2,1)S(1)}, u32[]{:S(2)}, u32[]{:S(2)}) collective-permute-start(bf16[256,1152]{1,0:T(8,128)(2,1)S(1)} %reshape.466), channel_id=1, source_target_pairs={{0,6},{1,7},{2,0},{3,1},{4,2},{5,3},{6,4},{7,5},{8,14},{9,15},{10,... | collective-permute-start | bytes 1769480 | tf_op jit(solution)/shard_map/ppermute | solution.py:41
  62.0 14.0 %collective-permute-start = (bf16[256,1152]{1,0:T(8,128)(2,1)S(1)}, bf16[256,1152]{1,0:T(8,128)(2,1)S(1)}, u32[]{:S(2)}, u32[]{:S(2)}) collective-permute-start(bf16[256,1152]{1,0:T(8,128)(2,1)S(1)} %reshape.466), channel_id=1, source_target_pairs={{0,2},{1,3},{2,4},{3,5},{4,6},{5,7},{6,0},{7,1},{8,10},{9,11},{10,... | collective-permute-start | bytes 1769480 | tf_op jit(solution)/shard_map/ppermute | solution.py:40
  70.4 16.1 %collective-permute-start.3 = (bf16[128,1152]{1,0:T(8,128)(2,1)S(1)}, bf16[128,1152]{1,0:T(8,128)(2,1)S(1)}, u32[]{:S(2)}, u32[]{:S(2)}) collective-permute-start(bf16[128,1152]{1,0:T(8,128)(2,1)S(1)} %slice.125), channel_id=1, source_target_pairs={{0,6},{1,7},{2,0},{3,1},{4,2},{5,3},{6,4},{7,5},{8,14},{9,15},{10,... | collective-permute-start | bytes 884744 | tf_op jit(solution)/shard_map/ppermute | solution.py:43
  76.3 10.2 %collective-permute-start.2 = (bf16[128,1152]{1,0:T(8,128)(2,1)S(1)}, bf16[128,1152]{1,0:T(8,128)(2,1)S(1)}, u32[]{:S(2)}, u32[]{:S(2)}) collective-permute-start(bf16[128,1152]{1,0:T(8,128)(2,1)S(1)} %slice.124), channel_id=1, source_target_pairs={{0,2},{1,3},{2,4},{3,5},{4,6},{5,7},{6,0},{7,1},{8,10},{9,11},{10,... | collective-permute-start | bytes 884744 | tf_op jit(solution)/shard_map/ppermute | solution.py:42
  78.4 17.4 %collective-permute-start.5 = (bf16[768,1152]{1,0:T(8,128)(2,1)S(1)}, bf16[768,1152]{1,0:T(8,128)(2,1)S(1)}, u32[]{:S(2)}, u32[]{:S(2)}) collective-permute-start(bf16[768,1152]{1,0:T(8,128)(2,1)S(1)} %pad_maximum_fusion), channel_id=1, source_target_pairs={{0,1},{1,0},{2,3},{3,2},{4,5},{5,4},{6,7},{7,6},{8,9},{9,8},{10,11... | collective-permute-start | bytes 5308424 | tf_op jit(solution)/shard_map/ppermute | solution.py:44
  86.6 8.6 %collective-permute-start.4 = (bf16[256,1152]{1,0:T(8,128)(2,1)S(1)}, bf16[256,1152]{1,0:T(8,128)(2,1)S(1)}, u32[]{:S(2)}, u32[]{:S(2)}) collective-permute-start(bf16[256,1152]{1,0:T(8,128)(2,1)S(1)} %constant_dynamic-update-slice_fusion), channel_id=1, source_target_pairs={{0,1},{1,0},{2,3},{3,2},{4,5},{5,4},{6,7},{7,6},{8,9},{9,8},{10,11... | collective-permute-start | bytes 1769480 | tf_op jit(solution)/shard_map/ppermute | solution.py:46

commit v14 on v13

--- a/solution.py
+++ b/solution.py
@@ -1,3 +1,5 @@
+import functools
+
 import jax
 import jax.numpy as jnp
 from jax import lax
@@ -20,11 +22,19 @@
     return meta[:, 0] * rows_total + meta[:, 1] * 256 + meta[:, 2]
 
 
-def pair_blocks(block, pairs):
+def query_view(rows, width):
+    column = lax.broadcasted_iota(jnp.int32, rows.shape, 1)
+    return jnp.where(column < width, rows, jnp.zeros_like(rows))
+
+
+def pair_best(block, width, rows_total, pairs):
+    own_key = slot_keys(block, width, rows_total)
+    own_query = query_view(block, width)
     chips = pairs // 2
     if pairs % 2 or chips != 4:
         gathered = lax.all_gather(block, "pair", axis=0, tiled=True)
-        return jnp.split(gathered, pairs, axis=0)
+        return tile_best(own_query, own_key, gathered, slot_keys(gathered, width, rows_total),
+                         rows_total)
 
     def at(y, c):
         return (y % chips) * 2 + c
@@ -36,15 +46,25 @@
     up = perm(lambda y, c: at(y + 1, c))
     down = perm(lambda y, c: at(y - 1, c))
     rows = block.shape[0]
-    half = rows // 2
     from_below = lax.ppermute(block, "pair", up)
     from_above = lax.ppermute(block, "pair", down)
-    far_low = lax.ppermute(from_below[:half], "pair", up)
-    far_high = lax.ppermute(from_above[half:], "pair", down)
-    siblings = lax.ppermute(jnp.concatenate([block, from_below, from_above]), "pair", swap)
-    far = jnp.concatenate([far_low, far_high])
-    far_sibling = lax.ppermute(far, "pair", swap)
-    return [block, from_below, from_above, far, far_sibling, siblings]
+    swapped = lax.ppermute(jnp.concatenate([block, from_above]), "pair", swap)
+    sibling, sibling_above = swapped[:rows], swapped[rows:]
+
+    def best_over(query, query_key, keys):
+        found = [tile_best(query, query_key, k, slot_keys(k, width, rows_total), rows_total)
+                 for k in keys]
+        return functools.reduce(jnp.maximum, found)
+
+    best = best_over(own_query, own_key, [block, from_below, from_above, sibling])
+    for_sibling = best_over(query_view(sibling, width), slot_keys(sibling, width, rows_total),
+                            [from_below, from_above])
+    for_below = best_over(query_view(from_below, width),
+                          slot_keys(from_below, width, rows_total),
+                          [from_above, sibling_above])
+    from_sibling = lax.ppermute(for_sibling, "pair", swap)
+    from_chip_above = lax.ppermute(for_below, "pair", down)
+    return jnp.maximum(best, jnp.maximum(from_sibling, from_chip_above))
 
 
 def on_device(embedding, labels, order_ids):
@@ -73,16 +93,7 @@
     got_rows = lax.all_to_all(
         send_rows.reshape(groups, capacity, -1), "dp", split_axis=0, concat_axis=0, tiled=True
     ).reshape(slot_count, -1)
-    blocks = pair_blocks(got_rows, pairs)
-    got_key = slot_keys(got_rows, width, rows_total)
-    column = lax.broadcasted_iota(jnp.int32, got_rows.shape, 1)
-    query_rows = jnp.where(column < width, got_rows, jnp.zeros_like(got_rows))
-    best_seen = jnp.full((slot_count,), -1.0, jnp.float32)
-    for block in blocks:
-        found = tile_best(
-            query_rows, got_key, block, slot_keys(block, width, rows_total), rows_total
-        )
-        best_seen = jnp.maximum(best_seen, found)
+    best_seen = pair_best(got_rows, width, rows_total, pairs)
     lanes = jnp.pad(best_seen.reshape(groups, capacity), ((0, 0), (0, LANES - capacity)))
     answered = lax.all_to_all(lanes, "dp", split_axis=0, concat_axis=0, tiled=True)
     answered = answered[:, :capacity].reshape(1, slot_count)

time: 121 us -> 115 us (0.950)
  starting transfers between devices: 47.2 us -> 40.1 us
  waiting for transfers between devices: 38.7 us -> 41.2 us
    ppermute x6 -> x5, starting transfers between devices: 28.1 us -> 21 us  [the longest x1 7.33 us: pair_best(): swapped = lax.ppermute(jnp.concatenate([block, from_above]), 'pair', swap)]
    ppermute x6 -> x5, waiting for transfers between devices: 6.34 us -> 8.81 us  [the longest x1 7.74 us: pair_best(): from_above = lax.ppermute(block, 'pair', down)]
    dot_general x6 -> x8, matrix products: 2.78 us -> 3.15 us  [tile_best(): scores = jnp.dot(own_rows, other_rows.T, preferred_element_type=jnp.float32)]
  transfers between devices with their start and end apart: 7 -> 6, of which waited for: 3 -> 4; matrix products, arithmetic and copies ran while one was open for 3% -> 4% of each run, Pallas kernels for 0% -> 0%
where the time goes in v14:
time: 115 us
  waiting for transfers between devices  41.2 us (36%)
  starting transfers between devices  40.1 us (35%)
  blocking collectives  21.6 us (19%)
  other arithmetic  7.21 us (6%)
  matrix products  3.15 us (3%)
  local copies, waits for them, and re-layouts  1.43 us (1%)
    all_to_all x1, waiting for transfers between devices, on_device(): lax.all_to_all(send_rows.reshape(groups, capacity, -1), 'dp', split_axis=...  32.4 us
    all_to_all x1, blocking collectives, on_device(): lax.all_to_all(lanes, 'dp', split_axis=0, concat_axis=0, tiled=True)  21.6 us
    all_to_all x1, starting transfers between devices, on_device(): lax.all_to_all(send_rows.reshape(groups, capacity, -1), 'dp', split_axis=...  19.1 us
    ppermute x1, waiting for transfers between devices, pair_best(): from_above = lax.ppermute(block, 'pair', down)  7.74 us
    ppermute x1, starting transfers between devices, pair_best(): swapped = lax.ppermute(jnp.concatenate([block, from_above]), 'pair', swap)  7.33 us
    ppermute x1, starting transfers between devices, pair_best(): from_chip_above = lax.ppermute(for_below, 'pair', down)  4.57 us
    ppermute x1, starting transfers between devices, pair_best(): from_above = lax.ppermute(block, 'pair', down)  3.36 us
    ppermute x1, starting transfers between devices, pair_best(): from_below = lax.ppermute(block, 'pair', up)  3.2 us
  transfers between devices with their start and end apart: 6, of which 4 were waited for; matrix products, arithmetic and copies ran while one was open for 4% of the time, Pallas kernels for 0%

profile of v14, /device:TPU:1, one launch (start us, length us, event | category | flops | bytes accessed | tf_op | source)
XLA Modules:
  0.0 114.9 jit_solution(6293639111179844272)
XLA Ops:
  0.0 0.7 and_select_fusion.6
  1.2 1.1 fusion.9
  2.2 1.1 fusion.10
  3.4 1.3 %scatter_custom_fusion = bf16[256,1152]{1,0:T(8,128)(2,1)S(1)} fusion(s32[128]{0:T(128)S(1)} %get-tuple-element.11, bf16[128,128]{1,0:T(8,128)(2,1)S(1)} %select_convert_fusion, bf16[]{:T(256)} %constant.162, bf16[128,1024]{1,0:T(8,128)(2,1)S(1)} %fusion.10, bf16[]{:T(256)} %constant.136.clone.1), kind=kCustom, calls=%fused_computation.28 | custom fusion | flops 589824 | bytes 884740 | tf_op jit(solution)/shard_map/scatter | solution.py:92
  4.8 0.9 reshape.428
  5.7 19.1 %all-to-all-start = ((bf16[64,4,1152]{2,1,0:T(4,128)(2,1)}), bf16[64,4,1152]{2,1,0:T(4,128)(2,1)S(1)}, u32[]{:S(2)}, u32[]{:S(2)}) async-start(bf16[64,4,1152]{2,1,0:T(4,128)(2,1)} %reshape.428), calls=%async_computation | async-start | bytes 1179648 | tf_op jit(solution)/shard_map/all_to_all | solution.py:93
  24.9 32.4 %all-to-all-done = bf16[64,4,1152]{2,1,0:T(4,128)(2,1)S(1)} async-done(((bf16[64,4,1152]{2,1,0:T(4,128)(2,1)}), bf16[64,4,1152]{2,1,0:T(4,128)(2,1)S(1)}, u32[]{:S(2)}, u32[]{:S(2)}) %all-to-all-start) | async-done | bytes 589856 | tf_op jit(solution)/shard_map/all_to_all | solution.py:93
  57.4 3.2 %collective-permute-start = (bf16[256,1152]{1,0:T(8,128)(2,1)S(1)}, bf16[256,1152]{1,0:T(8,128)(2,1)S(1)}, u32[]{:S(2)}, u32[]{:S(2)}) collective-permute-start(bf16[256,1152]{1,0:T(8,128)(2,1)S(1)} %reshape.429), channel_id=1, source_target_pairs={{0,2},{1,3},{2,4},{3,5},{4,6},{5,7},{6,0},{7,1},{8,10},{9,11},{10,... | collective-permute-start | bytes 1769480 | tf_op jit(solution)/shard_map/ppermute | solution.py:49
  60.6 3.4 %collective-permute-start.1 = (bf16[256,1152]{1,0:T(8,128)(2,1)S(1)}, bf16[256,1152]{1,0:T(8,128)(2,1)S(1)}, u32[]{:S(2)}, u32[]{:S(2)}) collective-permute-start(bf16[256,1152]{1,0:T(8,128)(2,1)S(1)} %reshape.429), channel_id=1, source_target_pairs={{0,6},{1,7},{2,0},{3,1},{4,2},{5,3},{6,4},{7,5},{8,14},{9,15},{10,... | collective-permute-start | bytes 1769480 | tf_op jit(solution)/shard_map/ppermute | solution.py:50
  65.0 7.7 %collective-permute-done.1 = bf16[256,1152]{1,0:T(8,128)(2,1)S(1)} collective-permute-done((bf16[256,1152]{1,0:T(8,128)(2,1)S(1)}, bf16[256,1152]{1,0:T(8,128)(2,1)S(1)}, u32[]{:S(2)}, u32[]{:S(2)}) %collective-permute-start.1) | collective-permute-done | bytes 589856 | tf_op jit(solution)/shard_map/ppermute | solution.py:50
  72.9 7.3 %collective-permute-start.2 = (bf16[512,1152]{1,0:T(8,128)(2,1)S(1)}, bf16[512,1152]{1,0:T(8,128)(2,1)S(1)}, u32[]{:S(2)}, u32[]{:S(2)}) collective-permute-start(bf16[512,1152]{1,0:T(8,128)(2,1)S(1)} %pad_maximum_fusion), channel_id=1, source_target_pairs={{0,1},{1,0},{2,3},{3,2},{4,5},{5,4},{6,7},{7,6},{8,9},{9,8},{10,11... | collective-permute-start | bytes 3538952 | tf_op jit(solution)/shard_map/ppermute | solution.py:51
  80.8 0.4 fusion.1
  81.2 0.4 fusion.2
  81.6 0.4 fusion.6
  82.0 0.7 collective-permute-done.2
  83.2 0.4 fusion.7
  83.6 4.6 %collective-permute-start.4 = (f32[256]{0:T(256)S(1)}, f32[256]{0:T(256)S(1)}, u32[]{:S(2)}, u32[]{:S(2)}) collective-permute-start(f32[256]{0:T(256)S(1)} %max.25), channel_id=1, source_target_pairs={{0,6},{1,7},{2,0},{3,1},{4,2},{5,3},{6,4},{7,5},{8,14},{9,15},{10,... | collective-permute-start | bytes 3080 | tf_op jit(solution)/shard_map/ppermute | solution.py:66
  88.2 0.4 fusion.5
  88.6 0.4 fusion.4
  89.0 2.6 %collective-permute-start.3 = (f32[256]{0:T(256)S(1)}, f32[256]{0:T(256)S(1)}, u32[]{:S(2)}, u32[]{:S(2)}) collective-permute-start(f32[256]{0:T(256)S(1)} %max.24), channel_id=1, source_target_pairs={{0,1},{1,0},{2,3},{3,2},{4,5},{5,4},{6,7},{7,6},{8,9},{9,8},{10,11... | collective-permute-start | bytes 3080 | tf_op jit(solution)/shard_map/ppermute | solution.py:65
  91.6 0.4 fusion.3
  92.0 0.4 collective-permute-done.3
  92.5 21.6 %all_to_all.17 = f32[64,1,128]{2,1,0:T(1,128)S(1)} all-to-all(f32[64,1,128]{2,1,0:T(1,128)S(1)} %bitcast.12), channel_id=1, replica_groups=mesh['dp'=64,'pair'=8] {'dp'}, dimensions={0} | all-to-all | bytes 65536 | tf_op jit(solution)/shard_map/all_to_all | solution.py:98
  114.2 0.7 select_reduce_fusion
  (36 shorter events, 3.2 us)
Async XLA Ops:
  5.7 51.5 %all-to-all-start = ((bf16[64,4,1152]{2,1,0:T(4,128)(2,1)}), bf16[64,4,1152]{2,1,0:T(4,128)(2,1)S(1)}, u32[]{:S(2)}, u32[]{:S(2)}) async-start(bf16[64,4,1152]{2,1,0:T(4,128)(2,1)} %reshape.428), calls=%async_computation | async-start | bytes 1179648 | tf_op jit(solution)/shard_map/all_to_all | solution.py:93
  57.4 22.9 %collective-permute-start = (bf16[256,1152]{1,0:T(8,128)(2,1)S(1)}, bf16[256,1152]{1,0:T(8,128)(2,1)S(1)}, u32[]{:S(2)}, u32[]{:S(2)}) collective-permute-start(bf16[256,1152]{1,0:T(8,128)(2,1)S(1)} %reshape.429), channel_id=1, source_target_pairs={{0,2},{1,3},{2,4},{3,5},{4,6},{5,7},{6,0},{7,1},{8,10},{9,11},{10,... | collective-permute-start | bytes 1769480 | tf_op jit(solution)/shard_map/ppermute | solution.py:49
  60.6 12.2 %collective-permute-start.1 = (bf16[256,1152]{1,0:T(8,128)(2,1)S(1)}, bf16[256,1152]{1,0:T(8,128)(2,1)S(1)}, u32[]{:S(2)}, u32[]{:S(2)}) collective-permute-start(bf16[256,1152]{1,0:T(8,128)(2,1)S(1)} %reshape.429), channel_id=1, source_target_pairs={{0,6},{1,7},{2,0},{3,1},{4,2},{5,3},{6,4},{7,5},{8,14},{9,15},{10,... | collective-permute-start | bytes 1769480 | tf_op jit(solution)/shard_map/ppermute | solution.py:50
  72.9 9.8 %collective-permute-start.2 = (bf16[512,1152]{1,0:T(8,128)(2,1)S(1)}, bf16[512,1152]{1,0:T(8,128)(2,1)S(1)}, u32[]{:S(2)}, u32[]{:S(2)}) collective-permute-start(bf16[512,1152]{1,0:T(8,128)(2,1)S(1)} %pad_maximum_fusion), channel_id=1, source_target_pairs={{0,1},{1,0},{2,3},{3,2},{4,5},{5,4},{6,7},{7,6},{8,9},{9,8},{10,11... | collective-permute-start | bytes 3538952 | tf_op jit(solution)/shard_map/ppermute | solution.py:51
  83.6 8.4 %collective-permute-start.4 = (f32[256]{0:T(256)S(1)}, f32[256]{0:T(256)S(1)}, u32[]{:S(2)}, u32[]{:S(2)}) collective-permute-start(f32[256]{0:T(256)S(1)} %max.25), channel_id=1, source_target_pairs={{0,6},{1,7},{2,0},{3,1},{4,2},{5,3},{6,4},{7,5},{8,14},{9,15},{10,... | collective-permute-start | bytes 3080 | tf_op jit(solution)/shard_map/ppermute | solution.py:66
  89.0 3.4 %collective-permute-start.3 = (f32[256]{0:T(256)S(1)}, f32[256]{0:T(256)S(1)}, u32[]{:S(2)}, u32[]{:S(2)}) collective-permute-start(f32[256]{0:T(256)S(1)} %max.24), channel_id=1, source_target_pairs={{0,1},{1,0},{2,3},{3,2},{4,5},{5,4},{6,7},{7,6},{8,9},{9,8},{10,11... | collective-permute-start | bytes 3080 | tf_op jit(solution)/shard_map/ppermute | solution.py:65

commit v15 on v14

--- a/solution.py
+++ b/solution.py
@@ -8,6 +8,7 @@
 CL_OWN = 2
 META = 128
 LANES = 128
+META_ROWS = 16
 
 
 def tile_best(own_rows, own_key, other_rows, other_key, rows_total):
@@ -17,24 +18,30 @@
     return jnp.max(jnp.where(earlier, scores, -1.0), axis=1)
 
 
-def slot_keys(rows, width, rows_total):
-    meta = rows[:, width : width + 3].astype(jnp.int32)
-    return meta[:, 0] * rows_total + meta[:, 1] * 256 + meta[:, 2]
+def to_block(got, width):
+    slots = got.shape[0]
+    meta = got[:, width : width + 3].T
+    meta = jnp.pad(meta, ((0, META_ROWS - 3), (0, width - slots)))
+    return jnp.concatenate([got[:, :width], meta], axis=0)
 
 
-def query_view(rows, width):
-    column = lax.broadcasted_iota(jnp.int32, rows.shape, 1)
-    return jnp.where(column < width, rows, jnp.zeros_like(rows))
+def block_best(query_block, key_block, slots, rows_total):
+    query_key = block_keys(query_block, slots, rows_total)
+    key_key = block_keys(key_block, slots, rows_total)
+    return tile_best(query_block[:slots], query_key, key_block[:slots], key_key, rows_total)
 
 
-def pair_best(block, width, rows_total, pairs):
-    own_key = slot_keys(block, width, rows_total)
-    own_query = query_view(block, width)
+def block_keys(block, slots, rows_total):
+    meta = block[slots : slots + 3, :slots].astype(jnp.int32)
+    return meta[0] * rows_total + meta[1] * 256 + meta[2]
+
+
+def pair_best(block, slots, rows_total, pairs):
     chips = pairs // 2
     if pairs % 2 or chips != 4:
-        gathered = lax.all_gather(block, "pair", axis=0, tiled=True)
-        return tile_best(own_query, own_key, gathered, slot_keys(gathered, width, rows_total),
-                         rows_total)
+        gathered = lax.all_gather(block, "pair", axis=0, tiled=False)
+        found = [block_best(block, gathered[i], slots, rows_total) for i in range(pairs)]
+        return functools.reduce(jnp.maximum, found)
 
     def at(y, c):
         return (y % chips) * 2 + c
@@ -51,17 +58,13 @@
     swapped = lax.ppermute(jnp.concatenate([block, from_above]), "pair", swap)
     sibling, sibling_above = swapped[:rows], swapped[rows:]
 
-    def best_over(query, query_key, keys):
-        found = [tile_best(query, query_key, k, slot_keys(k, width, rows_total), rows_total)
-                 for k in keys]
+    def best_over(query, keys):
+        found = [block_best(query, k, slots, rows_total) for k in keys]
         return functools.reduce(jnp.maximum, found)
 
-    best = best_over(own_query, own_key, [block, from_below, from_above, sibling])
-    for_sibling = best_over(query_view(sibling, width), slot_keys(sibling, width, rows_total),
-                            [from_below, from_above])
-    for_below = best_over(query_view(from_below, width),
-                          slot_keys(from_below, width, rows_total),
-                          [from_above, sibling_above])
+    best = best_over(block, [block, from_below, from_above, sibling])
+    for_sibling = best_over(sibling, [from_below, from_above])
+    for_below = best_over(from_below, [from_above, sibling_above])
     from_sibling = lax.ppermute(for_sibling, "pair", swap)
     from_chip_above = lax.ppermute(for_below, "pair", down)
     return jnp.maximum(best, jnp.maximum(from_sibling, from_chip_above))
@@ -93,7 +96,7 @@
     got_rows = lax.all_to_all(
         send_rows.reshape(groups, capacity, -1), "dp", split_axis=0, concat_axis=0, tiled=True
     ).reshape(slot_count, -1)
-    best_seen = pair_best(got_rows, width, rows_total, pairs)
+    best_seen = pair_best(to_block(got_rows, width), slot_count, rows_total, pairs)
     lanes = jnp.pad(best_seen.reshape(groups, capacity), ((0, 0), (0, LANES - capacity)))
     answered = lax.all_to_all(lanes, "dp", split_axis=0, concat_axis=0, tiled=True)
     answered = answered[:, :capacity].reshape(1, slot_count)

time: 115 us -> 112 us (0.974); the launches traced: 115 us -> 110 us
  blocking collectives: 21.6 us -> 72.8 us
  waiting for transfers between devices: 41.2 us -> 6.86 us
  starting transfers between devices: 40.1 us -> 21.2 us
  other arithmetic: 7.21 us -> 5.7 us
    all_to_all x0 -> x1, blocking collectives: none -> 51.3 us  [on_device(): lax.all_to_all(send_rows.reshape(groups, capacity, -1), 'dp', split_axis=...]
    all_to_all x1 -> x0, waiting for transfers between devices: 32.4 us -> none  [on_device(): lax.all_to_all(send_rows.reshape(groups, capacity, -1), 'dp', split_axis=...]
    all_to_all x1 -> x0, starting transfers between devices: 19.1 us -> none  [on_device(): lax.all_to_all(send_rows.reshape(groups, capacity, -1), 'dp', split_axis=...]
    ppermute x1, waiting for transfers between devices: 7.74 us -> 5.34 us  [pair_best(): from_above = lax.ppermute(block, 'pair', down)]
    ppermute x1, starting transfers between devices: 3.36 us -> 4.64 us  [pair_best(): from_above = lax.ppermute(block, 'pair', down)]
    ppermute x1, starting transfers between devices: 3.2 us -> 1.92 us  [pair_best(): from_below = lax.ppermute(block, 'pair', up)]
  transfers between devices with their start and end apart: 6 -> 5, of which waited for: 4 -> 3; matrix products, arithmetic and copies ran while one was open for 4% -> 2% of each run, Pallas kernels for 0% -> 0%
where the time goes in v15:
time: 112 us; the launch traced here: 110 us
  blocking collectives  72.8 us (65%)
  starting transfers between devices  21.2 us (19%)
  waiting for transfers between devices  6.86 us (6%)
  other arithmetic  5.7 us (5%)
  matrix products  2.84 us (3%)
    all_to_all x1, blocking collectives, on_device(): lax.all_to_all(send_rows.reshape(groups, capacity, -1), 'dp', split_axis=...  51.3 us
    all_to_all x1, blocking collectives, on_device(): lax.all_to_all(lanes, 'dp', split_axis=0, concat_axis=0, tiled=True)  21.6 us
    ppermute x1, starting transfers between devices, pair_best(): swapped = lax.ppermute(jnp.concatenate([block, from_above]), 'pair', swap)  7.05 us
    ppermute x1, waiting for transfers between devices, pair_best(): from_above = lax.ppermute(block, 'pair', down)  5.34 us
    ppermute x1, starting transfers between devices, pair_best(): from_above = lax.ppermute(block, 'pair', down)  4.64 us
    ppermute x1, starting transfers between devices, pair_best(): from_chip_above = lax.ppermute(for_below, 'pair', down)  3.94 us
    ppermute x1, starting transfers between devices, pair_best(): from_sibling = lax.ppermute(for_sibling, 'pair', swap)  3.67 us
    dot_general x8, matrix products, tile_best(): scores = jnp.dot(own_rows, other_rows.T, preferred_element_type=jnp.float32)  2.84 us
  transfers between devices with their start and end apart: 5, of which 3 were waited for; matrix products, arithmetic and copies ran while one was open for 2% of the time, Pallas kernels for 0%

profile of v15, /device:TPU:1, one launch (start us, length us, event | category | flops | bytes accessed | tf_op | source)
XLA Modules:
  0.0 110.4 jit_solution(9366694528665503831)
XLA Ops:
  0.0 0.7 and_select_fusion.9
  0.8 0.2 reduce_window_sum.11
  1.2 1.1 fusion.8
  2.2 1.1 fusion.9
  3.4 1.3 %scatter_custom_fusion = bf16[256,1152]{1,0:T(8,128)(2,1)S(1)} fusion(s32[128]{0:T(128)S(1)} %get-tuple-element.15, bf16[128,128]{1,0:T(8,128)(2,1)S(1)} %select_convert_fusion, bf16[]{:T(256)} %constant.155, bf16[128,1024]{1,0:T(8,128)(2,1)S(1)} %fusion.9, bf16[]{:T(256)} %constant.136.clone.1), kind=kCustom, calls=%fused_computation.34 | custom fusion | flops 589824 | bytes 884740 | tf_op jit(solution)/shard_map/scatter | solution.py:95
  4.9 51.3 %all_to_all.17 = bf16[64,4,1152]{2,1,0:T(4,128)(2,1)S(1)} all-to-all(bf16[64,4,1152]{2,1,0:T(4,128)(2,1)S(1)} %reshape.331), channel_id=1, replica_groups=mesh['dp'=64,'pair'=8] {'dp'}, dimensions={0} | all-to-all | bytes 1179648 | tf_op jit(solution)/shard_map/all_to_all | solution.py:96
  56.6 4.6 %collective-permute-start.1 = (bf16[272,1024]{1,0:T(8,128)(2,1)S(1)}, bf16[272,1024]{1,0:T(8,128)(2,1)S(1)}, u32[]{:S(2)}, u32[]{:S(2)}) collective-permute-start(bf16[272,1024]{1,0:T(8,128)(2,1)S(1)} %pad_maximum_fusion.1), channel_id=1, source_target_pairs={{0,6},{1,7},{2,0},{3,1},{4,2},{5,3},{6,4},{7,5},{8,14},{9,15},{10,... | collective-permute-start | bytes 1671176 | tf_op jit(solution)/shard_map/ppermute | solution.py:57
  61.2 1.9 %collective-permute-start = (bf16[272,1024]{1,0:T(8,128)(2,1)S(1)}, bf16[272,1024]{1,0:T(8,128)(2,1)S(1)}, u32[]{:S(2)}, u32[]{:S(2)}) collective-permute-start(bf16[272,1024]{1,0:T(8,128)(2,1)S(1)} %pad_maximum_fusion.1), channel_id=1, source_target_pairs={{0,2},{1,3},{2,4},{3,5},{4,6},{5,7},{6,0},{7,1},{8,10},{9,11},{10,... | collective-permute-start | bytes 1671176 | tf_op jit(solution)/shard_map/ppermute | solution.py:56
  63.2 0.4 fusion
  63.6 5.3 %collective-permute-done.1 = bf16[272,1024]{1,0:T(8,128)(2,1)S(1)} collective-permute-done((bf16[272,1024]{1,0:T(8,128)(2,1)S(1)}, bf16[272,1024]{1,0:T(8,128)(2,1)S(1)}, u32[]{:S(2)}, u32[]{:S(2)}) %collective-permute-start.1) | collective-permute-done | bytes 557088 | tf_op jit(solution)/shard_map/ppermute | solution.py:57
  69.0 7.1 %collective-permute-start.2 = (bf16[544,1024]{1,0:T(8,128)(2,1)S(1)}, bf16[544,1024]{1,0:T(8,128)(2,1)S(1)}, u32[]{:S(2)}, u32[]{:S(2)}) collective-permute-start(bf16[544,1024]{1,0:T(8,128)(2,1)S(1)} %pad_maximum_fusion), channel_id=1, source_target_pairs={{0,1},{1,0},{2,3},{3,2},{4,5},{5,4},{6,7},{7,6},{8,9},{9,8},{10,11... | collective-permute-start | bytes 3342344 | tf_op jit(solution)/shard_map/ppermute | solution.py:58
  76.1 0.4 fusion.2
  76.5 0.4 fusion.6
  76.9 0.4 fusion.1
  77.2 1.2 %collective-permute-done.2 = bf16[544,1024]{1,0:T(8,128)(2,1)S(1)} collective-permute-done((bf16[544,1024]{1,0:T(8,128)(2,1)S(1)}, bf16[544,1024]{1,0:T(8,128)(2,1)S(1)}, u32[]{:S(2)}, u32[]{:S(2)}) %collective-permute-start.2) | collective-permute-done | bytes 1114144 | tf_op jit(solution)/shard_map/ppermute | solution.py:58
  78.4 0.4 fusion.4
  78.8 0.4 fusion.5
  79.2 3.7 %collective-permute-start.3 = (f32[256]{0:T(256)S(1)}, f32[256]{0:T(256)S(1)}, u32[]{:S(2)}, u32[]{:S(2)}) collective-permute-start(f32[256]{0:T(256)S(1)} %max.24), channel_id=1, source_target_pairs={{0,1},{1,0},{2,3},{3,2},{4,5},{5,4},{6,7},{7,6},{8,9},{9,8},{10,11... | collective-permute-start | bytes 3080 | tf_op jit(solution)/shard_map/ppermute | solution.py:68
  82.9 0.4 fusion.7
  83.2 3.9 %collective-permute-start.4 = (f32[256]{0:T(256)S(1)}, f32[256]{0:T(256)S(1)}, u32[]{:S(2)}, u32[]{:S(2)}) collective-permute-start(f32[256]{0:T(256)S(1)} %max.25), channel_id=1, source_target_pairs={{0,6},{1,7},{2,0},{3,1},{4,2},{5,3},{6,4},{7,5},{8,14},{9,15},{10,... | collective-permute-start | bytes 3080 | tf_op jit(solution)/shard_map/ppermute | solution.py:69
  87.2 0.3 fusion.3
  87.5 0.3 collective-permute-done.4
  88.0 21.6 %all_to_all.18 = f32[64,1,128]{2,1,0:T(1,128)S(1)} all-to-all(f32[64,1,128]{2,1,0:T(1,128)S(1)} %bitcast.17), channel_id=1, replica_groups=mesh['dp'=64,'pair'=8] {'dp'}, dimensions={0} | all-to-all | bytes 65536 | tf_op jit(solution)/shard_map/all_to_all | solution.py:101
  109.7 0.7 select_reduce_fusion
  (35 shorter events, 1.3 us)
Async XLA Ops:
  56.6 12.3 %collective-permute-start.1 = (bf16[272,1024]{1,0:T(8,128)(2,1)S(1)}, bf16[272,1024]{1,0:T(8,128)(2,1)S(1)}, u32[]{:S(2)}, u32[]{:S(2)}) collective-permute-start(bf16[272,1024]{1,0:T(8,128)(2,1)S(1)} %pad_maximum_fusion.1), channel_id=1, source_target_pairs={{0,6},{1,7},{2,0},{3,1},{4,2},{5,3},{6,4},{7,5},{8,14},{9,15},{10,... | collective-permute-start | bytes 1671176 | tf_op jit(solution)/shard_map/ppermute | solution.py:57
  61.2 15.2 %collective-permute-start = (bf16[272,1024]{1,0:T(8,128)(2,1)S(1)}, bf16[272,1024]{1,0:T(8,128)(2,1)S(1)}, u32[]{:S(2)}, u32[]{:S(2)}) collective-permute-start(bf16[272,1024]{1,0:T(8,128)(2,1)S(1)} %pad_maximum_fusion.1), channel_id=1, source_target_pairs={{0,2},{1,3},{2,4},{3,5},{4,6},{5,7},{6,0},{7,1},{8,10},{9,11},{10,... | collective-permute-start | bytes 1671176 | tf_op jit(solution)/shard_map/ppermute | solution.py:56
  69.0 9.4 %collective-permute-start.2 = (bf16[544,1024]{1,0:T(8,128)(2,1)S(1)}, bf16[544,1024]{1,0:T(8,128)(2,1)S(1)}, u32[]{:S(2)}, u32[]{:S(2)}) collective-permute-start(bf16[544,1024]{1,0:T(8,128)(2,1)S(1)} %pad_maximum_fusion), channel_id=1, source_target_pairs={{0,1},{1,0},{2,3},{3,2},{4,5},{5,4},{6,7},{7,6},{8,9},{9,8},{10,11... | collective-permute-start | bytes 3342344 | tf_op jit(solution)/shard_map/ppermute | solution.py:58
  79.2 8.4 %collective-permute-start.3 = (f32[256]{0:T(256)S(1)}, f32[256]{0:T(256)S(1)}, u32[]{:S(2)}, u32[]{:S(2)}) collective-permute-start(f32[256]{0:T(256)S(1)} %max.24), channel_id=1, source_target_pairs={{0,1},{1,0},{2,3},{3,2},{4,5},{5,4},{6,7},{7,6},{8,9},{9,8},{10,11... | collective-permute-start | bytes 3080 | tf_op jit(solution)/shard_map/ppermute | solution.py:68
  83.2 4.7 %collective-permute-start.4 = (f32[256]{0:T(256)S(1)}, f32[256]{0:T(256)S(1)}, u32[]{:S(2)}, u32[]{:S(2)}) collective-permute-start(f32[256]{0:T(256)S(1)} %max.25), channel_id=1, source_target_pairs={{0,6},{1,7},{2,0},{3,1},{4,2},{5,3},{6,4},{7,5},{8,14},{9,15},{10,... | collective-permute-start | bytes 3080 | tf_op jit(solution)/shard_map/ppermute | solution.py:69

commit v16 on v15

--- a/solution.py
+++ b/solution.py
@@ -55,19 +55,20 @@
     rows = block.shape[0]
     from_below = lax.ppermute(block, "pair", up)
     from_above = lax.ppermute(block, "pair", down)
-    swapped = lax.ppermute(jnp.concatenate([block, from_above]), "pair", swap)
-    sibling, sibling_above = swapped[:rows], swapped[rows:]
+    swapped = lax.ppermute(jnp.concatenate([block, from_above, from_below]), "pair", swap)
+    sibling, sibling_above = swapped[:rows], swapped[rows : 2 * rows]
+    sibling_below = swapped[2 * rows :]
 
     def best_over(query, keys):
         found = [block_best(query, k, slots, rows_total) for k in keys]
         return functools.reduce(jnp.maximum, found)
 
-    best = best_over(block, [block, from_below, from_above, sibling])
-    for_sibling = best_over(sibling, [from_below, from_above])
+    best = best_over(
+        block, [block, from_below, from_above, sibling, sibling_above, sibling_below]
+    )
     for_below = best_over(from_below, [from_above, sibling_above])
-    from_sibling = lax.ppermute(for_sibling, "pair", swap)
     from_chip_above = lax.ppermute(for_below, "pair", down)
-    return jnp.maximum(best, jnp.maximum(from_sibling, from_chip_above))
+    return jnp.maximum(best, from_chip_above)
 
 
 def on_device(embedding, labels, order_ids):

time: 112 us -> 113 us (level)
  waiting for transfers between devices: 6.86 us -> 13.7 us
  starting transfers between devices: 21.2 us -> 15.8 us
    ppermute x1, waiting for transfers between devices: 0.01 us -> 5.05 us  [pair_best(): from_below = lax.ppermute(block, 'pair', up)]
    ppermute x2 -> x1, starting transfers between devices: 10.7 us -> 7.33 us  [pair_best(): lax.ppermute(jnp.concatenate([block, from_above, from_below]), 'pair', swap)]
    ppermute x1, starting transfers between devices: 3.94 us -> 1.92 us  [pair_best(): from_chip_above = lax.ppermute(for_below, 'pair', down)]
  transfers between devices with their start and end apart: 5 -> 4, of which waited for: 3 -> 4; matrix products, arithmetic and copies ran while one was open for 2% -> 2% of each run, Pallas kernels for 0% -> 0%
where the time goes in v16:
time: 113 us; the launch traced here: 112 us
  blocking collectives  72.8 us (64%)
  starting transfers between devices  15.8 us (14%)
  waiting for transfers between devices  13.7 us (12%)
  other arithmetic  5.81 us (5%)
  matrix products  2.84 us (3%)
    all_to_all x1, blocking collectives, on_device(): lax.all_to_all(send_rows.reshape(groups, capacity, -1), 'dp', split_axis=...  51.3 us
    all_to_all x1, blocking collectives, on_device(): lax.all_to_all(lanes, 'dp', split_axis=0, concat_axis=0, tiled=True)  21.6 us
    ppermute x1, starting transfers between devices, pair_best(): lax.ppermute(jnp.concatenate([block, from_above, from_below]), 'pair', swap)  7.33 us
    ppermute x1, waiting for transfers between devices, pair_best(): from_above = lax.ppermute(block, 'pair', down)  5.36 us
    ppermute x1, waiting for transfers between devices, pair_best(): from_below = lax.ppermute(block, 'pair', up)  5.05 us
    ppermute x1, starting transfers between devices, pair_best(): from_above = lax.ppermute(block, 'pair', down)  4.64 us
    dot_general x8, matrix products, tile_best(): scores = jnp.dot(own_rows, other_rows.T, preferred_element_type=jnp.float32)  2.84 us
  transfers between devices with their start and end apart: 4, of which 4 were waited for; matrix products, arithmetic and copies ran while one was open for 2% of the time, Pallas kernels for 0%

profile of v16, /device:TPU:1, one launch (start us, length us, event | category | flops | bytes accessed | tf_op | source)
XLA Modules:
  0.0 111.9 jit_solution(13203407471449464860)
XLA Ops:
  0.0 1.1 fusion.8
  1.1 0.7 and_select_fusion.9
  2.2 1.1 fusion.9
  3.4 1.3 %scatter_custom_fusion = bf16[256,1152]{1,0:T(8,128)(2,1)S(1)} fusion(s32[128]{0:T(128)S(1)} %get-tuple-element.17, bf16[128,128]{1,0:T(8,128)(2,1)S(1)} %select_convert_fusion, bf16[]{:T(256)} %constant.155, bf16[128,1024]{1,0:T(8,128)(2,1)S(1)} %fusion.9, bf16[]{:T(256)} %constant.136.clone.1), kind=kCustom, calls=%fused_computation.32 | custom fusion | flops 589824 | bytes 884740 | tf_op jit(solution)/shard_map/scatter | solution.py:96
  4.9 51.3 %all_to_all.17 = bf16[64,4,1152]{2,1,0:T(4,128)(2,1)S(1)} all-to-all(bf16[64,4,1152]{2,1,0:T(4,128)(2,1)S(1)} %reshape.285), channel_id=1, replica_groups=mesh['dp'=64,'pair'=8] {'dp'}, dimensions={0} | all-to-all | bytes 1179648 | tf_op jit(solution)/shard_map/all_to_all | solution.py:97
  56.6 4.6 %collective-permute-start.1 = (bf16[272,1024]{1,0:T(8,128)(2,1)S(1)}, bf16[272,1024]{1,0:T(8,128)(2,1)S(1)}, u32[]{:S(2)}, u32[]{:S(2)}) collective-permute-start(bf16[272,1024]{1,0:T(8,128)(2,1)S(1)} %pad_maximum_fusion.1), channel_id=1, source_target_pairs={{0,6},{1,7},{2,0},{3,1},{4,2},{5,3},{6,4},{7,5},{8,14},{9,15},{10,... | collective-permute-start | bytes 1671176 | tf_op jit(solution)/shard_map/ppermute | solution.py:57
  61.2 1.9 %collective-permute-start = (bf16[272,1024]{1,0:T(8,128)(2,1)S(1)}, bf16[272,1024]{1,0:T(8,128)(2,1)S(1)}, u32[]{:S(2)}, u32[]{:S(2)}) collective-permute-start(bf16[272,1024]{1,0:T(8,128)(2,1)S(1)} %pad_maximum_fusion.1), channel_id=1, source_target_pairs={{0,2},{1,3},{2,4},{3,5},{4,6},{5,7},{6,0},{7,1},{8,10},{9,11},{10,... | collective-permute-start | bytes 1671176 | tf_op jit(solution)/shard_map/ppermute | solution.py:56
  63.2 0.3 fusion
  63.6 5.4 %collective-permute-done.1 = bf16[272,1024]{1,0:T(8,128)(2,1)S(1)} collective-permute-done((bf16[272,1024]{1,0:T(8,128)(2,1)S(1)}, bf16[272,1024]{1,0:T(8,128)(2,1)S(1)}, u32[]{:S(2)}, u32[]{:S(2)}) %collective-permute-start.1) | collective-permute-done | bytes 557088 | tf_op jit(solution)/shard_map/ppermute | solution.py:57
  68.9 5.0 %collective-permute-done = bf16[272,1024]{1,0:T(8,128)(2,1)S(1)} collective-permute-done((bf16[272,1024]{1,0:T(8,128)(2,1)S(1)}, bf16[272,1024]{1,0:T(8,128)(2,1)S(1)}, u32[]{:S(2)}, u32[]{:S(2)}) %collective-permute-start) | collective-permute-done | bytes 557088 | tf_op jit(solution)/shard_map/ppermute | solution.py:56
  74.0 0.2 pad_maximum_fusion
  74.1 7.3 %collective-permute-start.2 = (bf16[816,1024]{1,0:T(8,128)(2,1)S(1)}, bf16[816,1024]{1,0:T(8,128)(2,1)S(1)}, u32[]{:S(2)}, u32[]{:S(2)}) collective-permute-start(bf16[816,1024]{1,0:T(8,128)(2,1)S(1)} %pad_maximum_fusion), channel_id=1, source_target_pairs={{0,1},{1,0},{2,3},{3,2},{4,5},{5,4},{6,7},{7,6},{8,9},{9,8},{10,11... | collective-permute-start | bytes 5013512 | tf_op jit(solution)/shard_map/ppermute | solution.py:58
  81.5 0.3 fusion.2
  81.9 0.3 fusion.1
  82.3 0.4 fusion.6
  82.6 2.0 %collective-permute-done.2 = bf16[816,1024]{1,0:T(8,128)(2,1)S(1)} collective-permute-done((bf16[816,1024]{1,0:T(8,128)(2,1)S(1)}, bf16[816,1024]{1,0:T(8,128)(2,1)S(1)}, u32[]{:S(2)}, u32[]{:S(2)}) %collective-permute-start.2) | collective-permute-done | bytes 1671200 | tf_op jit(solution)/shard_map/ppermute | solution.py:58
  84.7 0.4 fusion.7
  85.1 1.9 %collective-permute-start.3 = (f32[256]{0:T(256)S(1)}, f32[256]{0:T(256)S(1)}, u32[]{:S(2)}, u32[]{:S(2)}) collective-permute-start(f32[256]{0:T(256)S(1)} %max.26), channel_id=1, source_target_pairs={{0,6},{1,7},{2,0},{3,1},{4,2},{5,3},{6,4},{7,5},{8,14},{9,15},{10,... | collective-permute-start | bytes 3080 | tf_op jit(solution)/shard_map/ppermute | solution.py:70
  87.0 0.4 fusion.4
  87.4 0.4 fusion.3
  87.7 0.4 fusion.5
  88.1 1.3 %collective-permute-done.3 = f32[256]{0:T(256)S(1)} collective-permute-done((f32[256]{0:T(256)S(1)}, f32[256]{0:T(256)S(1)}, u32[]{:S(2)}, u32[]{:S(2)}) %collective-permute-start.3) | collective-permute-done | bytes 1056 | tf_op jit(solution)/shard_map/ppermute | solution.py:70
  89.5 21.6 %all_to_all.18 = f32[64,1,128]{2,1,0:T(1,128)S(1)} all-to-all(f32[64,1,128]{2,1,0:T(1,128)S(1)} %bitcast.20), channel_id=1, replica_groups=mesh['dp'=64,'pair'=8] {'dp'}, dimensions={0} | all-to-all | bytes 65536 | tf_op jit(solution)/shard_map/all_to_all | solution.py:102
  111.2 0.7 select_reduce_fusion
  (32 shorter events, 1.4 us)
Async XLA Ops:
  56.6 12.3 %collective-permute-start.1 = (bf16[272,1024]{1,0:T(8,128)(2,1)S(1)}, bf16[272,1024]{1,0:T(8,128)(2,1)S(1)}, u32[]{:S(2)}, u32[]{:S(2)}) collective-permute-start(bf16[272,1024]{1,0:T(8,128)(2,1)S(1)} %pad_maximum_fusion.1), channel_id=1, source_target_pairs={{0,6},{1,7},{2,0},{3,1},{4,2},{5,3},{6,4},{7,5},{8,14},{9,15},{10,... | collective-permute-start | bytes 1671176 | tf_op jit(solution)/shard_map/ppermute | solution.py:57
  61.2 12.7 %collective-permute-start = (bf16[272,1024]{1,0:T(8,128)(2,1)S(1)}, bf16[272,1024]{1,0:T(8,128)(2,1)S(1)}, u32[]{:S(2)}, u32[]{:S(2)}) collective-permute-start(bf16[272,1024]{1,0:T(8,128)(2,1)S(1)} %pad_maximum_fusion.1), channel_id=1, source_target_pairs={{0,2},{1,3},{2,4},{3,5},{4,6},{5,7},{6,0},{7,1},{8,10},{9,11},{10,... | collective-permute-start | bytes 1671176 | tf_op jit(solution)/shard_map/ppermute | solution.py:56
  74.1 10.5 %collective-permute-start.2 = (bf16[816,1024]{1,0:T(8,128)(2,1)S(1)}, bf16[816,1024]{1,0:T(8,128)(2,1)S(1)}, u32[]{:S(2)}, u32[]{:S(2)}) collective-permute-start(bf16[816,1024]{1,0:T(8,128)(2,1)S(1)} %pad_maximum_fusion), channel_id=1, source_target_pairs={{0,1},{1,0},{2,3},{3,2},{4,5},{5,4},{6,7},{7,6},{8,9},{9,8},{10,11... | collective-permute-start | bytes 5013512 | tf_op jit(solution)/shard_map/ppermute | solution.py:58
  85.1 4.3 %collective-permute-start.3 = (f32[256]{0:T(256)S(1)}, f32[256]{0:T(256)S(1)}, u32[]{:S(2)}, u32[]{:S(2)}) collective-permute-start(f32[256]{0:T(256)S(1)} %max.26), channel_id=1, source_target_pairs={{0,6},{1,7},{2,0},{3,1},{4,2},{5,3},{6,4},{7,5},{8,14},{9,15},{10,... | collective-permute-start | bytes 3080 | tf_op jit(solution)/shard_map/ppermute | solution.py:70

commit v17 on v16

--- a/solution.py
+++ b/solution.py
@@ -79,7 +79,11 @@
     capacity = 2 * rows_here // groups
     slot_count = groups * capacity
     values = embedding.astype(jnp.float32)
-    squares = jnp.sum(values * values, axis=1, keepdims=True)
+    gram = jnp.dot(embedding, embedding.T, preferred_element_type=jnp.float32)
+    diagonal = lax.broadcasted_iota(jnp.int32, gram.shape, 0) == lax.broadcasted_iota(
+        jnp.int32, gram.shape, 1
+    )
+    squares = jnp.sum(jnp.where(diagonal, gram, 0.0), axis=1, keepdims=True)
     shifted = squares + 1e-06
     unit_rows = (values * lax.rsqrt(shifted)).astype(jnp.bfloat16)
     owner_group = labels // CL_OWN

time: 113 us -> 113 us (level)
  matrix products: 2.84 us -> 4.12 us
    dot_general x0 -> x1, matrix products: none -> 1.28 us  [on_device(): gram = jnp.dot(embedding, embedding.T, preferred_element_type=jnp.float32)]
where the time goes in v17:
time: 113 us; the launch traced here: 112 us
  blocking collectives  72.8 us (64%)
  starting transfers between devices  15.8 us (14%)
  waiting for transfers between devices  13.7 us (12%)
  other arithmetic  4.72 us (4%)
  matrix products  4.12 us (4%)
    all_to_all x1, blocking collectives, on_device(): lax.all_to_all(send_rows.reshape(groups, capacity, -1), 'dp', split_axis=...  51.3 us
    all_to_all x1, blocking collectives, on_device(): lax.all_to_all(lanes, 'dp', split_axis=0, concat_axis=0, tiled=True)  21.6 us
    ppermute x1, starting transfers between devices, pair_best(): lax.ppermute(jnp.concatenate([block, from_above, from_below]), 'pair', swap)  7.33 us
    ppermute x1, waiting for transfers between devices, pair_best(): from_above = lax.ppermute(block, 'pair', down)  5.35 us
    ppermute x1, waiting for transfers between devices, pair_best(): from_below = lax.ppermute(block, 'pair', up)  5.05 us
    ppermute x1, starting transfers between devices, pair_best(): from_above = lax.ppermute(block, 'pair', down)  4.65 us
    dot_general x8, matrix products, tile_best(): scores = jnp.dot(own_rows, other_rows.T, preferred_element_type=jnp.float32)  2.84 us
  transfers between devices with their start and end apart: 4, of which 4 were waited for; matrix products, arithmetic and copies ran while one was open for 2% of the time, Pallas kernels for 0%

profile of v17, /device:TPU:1, one launch (start us, length us, event | category | flops | bytes accessed | tf_op | source)
XLA Modules:
  0.0 112.1 jit_solution(15560490091060348760)
XLA Ops:
  0.0 1.3 %fusion.8 = f32[128]{0:T(128)S(1)} fusion(bf16[128,1024]{1,0:T(8,128)(2,1)} %param.3), kind=kOutput, calls=%fused_computation.19 | convolution fusion | flops 33603456 | bytes 262656 | tf_op jit(solution)/shard_map/dot_general | solution.py:82
  1.3 0.7 and_select_fusion.9
  2.4 1.1 multiply_convert_fusion
  3.6 1.3 %scatter_custom_fusion = bf16[256,1152]{1,0:T(8,128)(2,1)S(1)} fusion(s32[128]{0:T(128)S(1)} %get-tuple-element.17, bf16[128,128]{1,0:T(8,128)(2,1)S(1)} %select_convert_fusion, bf16[]{:T(256)} %constant.155, bf16[128,1024]{1,0:T(8,128)(2,1)S(1)} %multiply_convert_fusion, bf16[]{:T(256)} %constant.136.clone.1), kind=kCustom, calls=%fused_computation.31 | custom fusion | flops 589824 | bytes 884740 | tf_op jit(solution)/shard_map/scatter | solution.py:100
  5.1 51.3 %all_to_all.17 = bf16[64,4,1152]{2,1,0:T(4,128)(2,1)S(1)} all-to-all(bf16[64,4,1152]{2,1,0:T(4,128)(2,1)S(1)} %reshape.285), channel_id=1, replica_groups=mesh['dp'=64,'pair'=8] {'dp'}, dimensions={0} | all-to-all | bytes 1179648 | tf_op jit(solution)/shard_map/all_to_all | solution.py:101
  56.8 4.6 %collective-permute-start.1 = (bf16[272,1024]{1,0:T(8,128)(2,1)S(1)}, bf16[272,1024]{1,0:T(8,128)(2,1)S(1)}, u32[]{:S(2)}, u32[]{:S(2)}) collective-permute-start(bf16[272,1024]{1,0:T(8,128)(2,1)S(1)} %pad_maximum_fusion.1), channel_id=1, source_target_pairs={{0,6},{1,7},{2,0},{3,1},{4,2},{5,3},{6,4},{7,5},{8,14},{9,15},{10,... | collective-permute-start | bytes 1671176 | tf_op jit(solution)/shard_map/ppermute | solution.py:57
  61.4 1.9 %collective-permute-start = (bf16[272,1024]{1,0:T(8,128)(2,1)S(1)}, bf16[272,1024]{1,0:T(8,128)(2,1)S(1)}, u32[]{:S(2)}, u32[]{:S(2)}) collective-permute-start(bf16[272,1024]{1,0:T(8,128)(2,1)S(1)} %pad_maximum_fusion.1), channel_id=1, source_target_pairs={{0,2},{1,3},{2,4},{3,5},{4,6},{5,7},{6,0},{7,1},{8,10},{9,11},{10,... | collective-permute-start | bytes 1671176 | tf_op jit(solution)/shard_map/ppermute | solution.py:56
  63.4 0.4 fusion
  63.8 5.4 %collective-permute-done.1 = bf16[272,1024]{1,0:T(8,128)(2,1)S(1)} collective-permute-done((bf16[272,1024]{1,0:T(8,128)(2,1)S(1)}, bf16[272,1024]{1,0:T(8,128)(2,1)S(1)}, u32[]{:S(2)}, u32[]{:S(2)}) %collective-permute-start.1) | collective-permute-done | bytes 557088 | tf_op jit(solution)/shard_map/ppermute | solution.py:57
  69.1 5.0 %collective-permute-done = bf16[272,1024]{1,0:T(8,128)(2,1)S(1)} collective-permute-done((bf16[272,1024]{1,0:T(8,128)(2,1)S(1)}, bf16[272,1024]{1,0:T(8,128)(2,1)S(1)}, u32[]{:S(2)}, u32[]{:S(2)}) %collective-permute-start) | collective-permute-done | bytes 557088 | tf_op jit(solution)/shard_map/ppermute | solution.py:56
  74.2 0.2 pad_maximum_fusion
  74.3 7.3 %collective-permute-start.2 = (bf16[816,1024]{1,0:T(8,128)(2,1)S(1)}, bf16[816,1024]{1,0:T(8,128)(2,1)S(1)}, u32[]{:S(2)}, u32[]{:S(2)}) collective-permute-start(bf16[816,1024]{1,0:T(8,128)(2,1)S(1)} %pad_maximum_fusion), channel_id=1, source_target_pairs={{0,1},{1,0},{2,3},{3,2},{4,5},{5,4},{6,7},{7,6},{8,9},{9,8},{10,11... | collective-permute-start | bytes 5013512 | tf_op jit(solution)/shard_map/ppermute | solution.py:58
  81.7 0.4 fusion.2
  82.1 0.3 fusion.1
  82.5 0.4 fusion.6
  82.8 2.0 %collective-permute-done.2 = bf16[816,1024]{1,0:T(8,128)(2,1)S(1)} collective-permute-done((bf16[816,1024]{1,0:T(8,128)(2,1)S(1)}, bf16[816,1024]{1,0:T(8,128)(2,1)S(1)}, u32[]{:S(2)}, u32[]{:S(2)}) %collective-permute-start.2) | collective-permute-done | bytes 1671200 | tf_op jit(solution)/shard_map/ppermute | solution.py:58
  84.9 0.4 fusion.7
  85.3 1.9 %collective-permute-start.3 = (f32[256]{0:T(256)S(1)}, f32[256]{0:T(256)S(1)}, u32[]{:S(2)}, u32[]{:S(2)}) collective-permute-start(f32[256]{0:T(256)S(1)} %max.26), channel_id=1, source_target_pairs={{0,6},{1,7},{2,0},{3,1},{4,2},{5,3},{6,4},{7,5},{8,14},{9,15},{10,... | collective-permute-start | bytes 3080 | tf_op jit(solution)/shard_map/ppermute | solution.py:70
  87.2 0.4 fusion.4
  87.6 0.4 fusion.3
  87.9 0.4 fusion.5
  88.3 1.3 %collective-permute-done.3 = f32[256]{0:T(256)S(1)} collective-permute-done((f32[256]{0:T(256)S(1)}, f32[256]{0:T(256)S(1)}, u32[]{:S(2)}, u32[]{:S(2)}) %collective-permute-start.3) | collective-permute-done | bytes 1056 | tf_op jit(solution)/shard_map/ppermute | solution.py:70
  89.7 21.6 %all_to_all.18 = f32[64,1,128]{2,1,0:T(1,128)S(1)} all-to-all(f32[64,1,128]{2,1,0:T(1,128)S(1)} %bitcast.22), channel_id=1, replica_groups=mesh['dp'=64,'pair'=8] {'dp'}, dimensions={0} | all-to-all | bytes 65536 | tf_op jit(solution)/shard_map/all_to_all | solution.py:106
  111.4 0.7 select_reduce_fusion
  (32 shorter events, 1.4 us)
Async XLA Ops:
  56.8 12.3 %collective-permute-start.1 = (bf16[272,1024]{1,0:T(8,128)(2,1)S(1)}, bf16[272,1024]{1,0:T(8,128)(2,1)S(1)}, u32[]{:S(2)}, u32[]{:S(2)}) collective-permute-start(bf16[272,1024]{1,0:T(8,128)(2,1)S(1)} %pad_maximum_fusion.1), channel_id=1, source_target_pairs={{0,6},{1,7},{2,0},{3,1},{4,2},{5,3},{6,4},{7,5},{8,14},{9,15},{10,... | collective-permute-start | bytes 1671176 | tf_op jit(solution)/shard_map/ppermute | solution.py:57
  61.4 12.7 %collective-permute-start = (bf16[272,1024]{1,0:T(8,128)(2,1)S(1)}, bf16[272,1024]{1,0:T(8,128)(2,1)S(1)}, u32[]{:S(2)}, u32[]{:S(2)}) collective-permute-start(bf16[272,1024]{1,0:T(8,128)(2,1)S(1)} %pad_maximum_fusion.1), channel_id=1, source_target_pairs={{0,2},{1,3},{2,4},{3,5},{4,6},{5,7},{6,0},{7,1},{8,10},{9,11},{10,... | collective-permute-start | bytes 1671176 | tf_op jit(solution)/shard_map/ppermute | solution.py:56
  74.3 10.5 %collective-permute-start.2 = (bf16[816,1024]{1,0:T(8,128)(2,1)S(1)}, bf16[816,1024]{1,0:T(8,128)(2,1)S(1)}, u32[]{:S(2)}, u32[]{:S(2)}) collective-permute-start(bf16[816,1024]{1,0:T(8,128)(2,1)S(1)} %pad_maximum_fusion), channel_id=1, source_target_pairs={{0,1},{1,0},{2,3},{3,2},{4,5},{5,4},{6,7},{7,6},{8,9},{9,8},{10,11... | collective-permute-start | bytes 5013512 | tf_op jit(solution)/shard_map/ppermute | solution.py:58
  85.3 4.3 %collective-permute-start.3 = (f32[256]{0:T(256)S(1)}, f32[256]{0:T(256)S(1)}, u32[]{:S(2)}, u32[]{:S(2)}) collective-permute-start(f32[256]{0:T(256)S(1)} %max.26), channel_id=1, source_target_pairs={{0,6},{1,7},{2,0},{3,1},{4,2},{5,3},{6,4},{7,5},{8,14},{9,15},{10,... | collective-permute-start | bytes 3080 | tf_op jit(solution)/shard_map/ppermute | solution.py:70

commit v18 on v15

--- a/solution.py
+++ b/solution.py
@@ -62,11 +62,12 @@
         found = [block_best(query, k, slots, rows_total) for k in keys]
         return functools.reduce(jnp.maximum, found)
 
+    for_below = best_over(from_below, [from_above, sibling_above])
+    from_chip_above = lax.ppermute(for_below, "pair", down)
+    sibling, _ = lax.optimization_barrier((sibling, for_below))
     best = best_over(block, [block, from_below, from_above, sibling])
     for_sibling = best_over(sibling, [from_below, from_above])
-    for_below = best_over(from_below, [from_above, sibling_above])
     from_sibling = lax.ppermute(for_sibling, "pair", swap)
-    from_chip_above = lax.ppermute(for_below, "pair", down)
     return jnp.maximum(best, jnp.maximum(from_sibling, from_chip_above))
 
 

time: 112 us -> 111 us (level); the launches traced: 110 us -> 111 us
    ppermute x1, starting transfers between devices: 3.94 us -> 5.32 us  [pair_best(): from_chip_above = lax.ppermute(for_below, 'pair', down)]
where the time goes in v18:
time: 111 us
  blocking collectives  72.8 us (66%)
  starting transfers between devices  21.5 us (19%)
  waiting for transfers between devices  6.96 us (6%)
  other arithmetic  5.71 us (5%)
  matrix products  2.86 us (3%)
    all_to_all x1, blocking collectives, on_device(): lax.all_to_all(send_rows.reshape(groups, capacity, -1), 'dp', split_axis=...  51.3 us
    all_to_all x1, blocking collectives, on_device(): lax.all_to_all(lanes, 'dp', split_axis=0, concat_axis=0, tiled=True)  21.6 us
    ppermute x1, starting transfers between devices, pair_best(): swapped = lax.ppermute(jnp.concatenate([block, from_above]), 'pair', swap)  7.05 us
    ppermute x1, waiting for transfers between devices, pair_best(): from_above = lax.ppermute(block, 'pair', down)  5.34 us
    ppermute x1, starting transfers between devices, pair_best(): from_chip_above = lax.ppermute(for_below, 'pair', down)  5.32 us
    ppermute x1, starting transfers between devices, pair_best(): from_above = lax.ppermute(block, 'pair', down)  4.64 us
    dot_general x8, matrix products, tile_best(): scores = jnp.dot(own_rows, other_rows.T, preferred_element_type=jnp.float32)  2.86 us
    ppermute x1, starting transfers between devices, pair_best(): from_sibling = lax.ppermute(for_sibling, 'pair', swap)  2.57 us
  transfers between devices with their start and end apart: 5, of which 3 were waited for; matrix products, arithmetic and copies ran while one was open for 2% of the time, Pallas kernels for 0%

profile of v18, /device:TPU:1, one launch (start us, length us, event | category | flops | bytes accessed | tf_op | source)
XLA Modules:
  0.0 110.8 jit_solution(575778628301305668)
XLA Ops:
  0.0 0.7 and_select_fusion.9
  0.8 0.2 reduce_window_sum.11
  1.2 1.1 fusion.8
  2.2 1.1 fusion.9
  3.4 1.3 %scatter_custom_fusion = bf16[256,1152]{1,0:T(8,128)(2,1)S(1)} fusion(s32[128]{0:T(128)S(1)} %get-tuple-element.17, bf16[128,128]{1,0:T(8,128)(2,1)S(1)} %select_convert_fusion, bf16[]{:T(256)} %constant.155, bf16[128,1024]{1,0:T(8,128)(2,1)S(1)} %fusion.9, bf16[]{:T(256)} %constant.136.clone.1), kind=kCustom, calls=%fused_computation.34 | custom fusion | flops 589824 | bytes 884740 | tf_op jit(solution)/shard_map/scatter | solution.py:96
  4.9 51.3 %all_to_all.17 = bf16[64,4,1152]{2,1,0:T(4,128)(2,1)S(1)} all-to-all(bf16[64,4,1152]{2,1,0:T(4,128)(2,1)S(1)} %reshape.331), channel_id=1, replica_groups=mesh['dp'=64,'pair'=8] {'dp'}, dimensions={0} | all-to-all | bytes 1179648 | tf_op jit(solution)/shard_map/all_to_all | solution.py:97
  56.6 4.6 %collective-permute-start.1 = (bf16[272,1024]{1,0:T(8,128)(2,1)S(1)}, bf16[272,1024]{1,0:T(8,128)(2,1)S(1)}, u32[]{:S(2)}, u32[]{:S(2)}) collective-permute-start(bf16[272,1024]{1,0:T(8,128)(2,1)S(1)} %pad_maximum_fusion.1), channel_id=1, source_target_pairs={{0,6},{1,7},{2,0},{3,1},{4,2},{5,3},{6,4},{7,5},{8,14},{9,15},{10,... | collective-permute-start | bytes 1671176 | tf_op jit(solution)/shard_map/ppermute | solution.py:57
  61.2 1.9 %collective-permute-start = (bf16[272,1024]{1,0:T(8,128)(2,1)S(1)}, bf16[272,1024]{1,0:T(8,128)(2,1)S(1)}, u32[]{:S(2)}, u32[]{:S(2)}) collective-permute-start(bf16[272,1024]{1,0:T(8,128)(2,1)S(1)} %pad_maximum_fusion.1), channel_id=1, source_target_pairs={{0,2},{1,3},{2,4},{3,5},{4,6},{5,7},{6,0},{7,1},{8,10},{9,11},{10,... | collective-permute-start | bytes 1671176 | tf_op jit(solution)/shard_map/ppermute | solution.py:56
  63.2 0.4 fusion
  63.6 5.3 %collective-permute-done.1 = bf16[272,1024]{1,0:T(8,128)(2,1)S(1)} collective-permute-done((bf16[272,1024]{1,0:T(8,128)(2,1)S(1)}, bf16[272,1024]{1,0:T(8,128)(2,1)S(1)}, u32[]{:S(2)}, u32[]{:S(2)}) %collective-permute-start.1) | collective-permute-done | bytes 557088 | tf_op jit(solution)/shard_map/ppermute | solution.py:57
  69.0 7.1 %collective-permute-start.2 = (bf16[544,1024]{1,0:T(8,128)(2,1)S(1)}, bf16[544,1024]{1,0:T(8,128)(2,1)S(1)}, u32[]{:S(2)}, u32[]{:S(2)}) collective-permute-start(bf16[544,1024]{1,0:T(8,128)(2,1)S(1)} %pad_maximum_fusion), channel_id=1, source_target_pairs={{0,1},{1,0},{2,3},{3,2},{4,5},{5,4},{6,7},{7,6},{8,9},{9,8},{10,11... | collective-permute-start | bytes 3342344 | tf_op jit(solution)/shard_map/ppermute | solution.py:58
  76.1 0.4 fusion.2
  76.5 0.4 fusion.3
  76.9 0.4 fusion.1
  77.2 1.2 %collective-permute-done.2 = bf16[544,1024]{1,0:T(8,128)(2,1)S(1)} collective-permute-done((bf16[544,1024]{1,0:T(8,128)(2,1)S(1)}, bf16[544,1024]{1,0:T(8,128)(2,1)S(1)}, u32[]{:S(2)}, u32[]{:S(2)}) %collective-permute-start.2) | collective-permute-done | bytes 1114144 | tf_op jit(solution)/shard_map/ppermute | solution.py:58
  78.4 0.4 fusion.4
  78.8 5.3 %collective-permute-start.4 = (f32[256]{0:T(256)S(1)}, f32[256]{0:T(256)S(1)}, u32[]{:S(2)}, u32[]{:S(2)}) collective-permute-start(f32[256]{0:T(256)S(1)} %max.23), channel_id=1, source_target_pairs={{0,6},{1,7},{2,0},{3,1},{4,2},{5,3},{6,4},{7,5},{8,14},{9,15},{10,... | collective-permute-start | bytes 3080 | tf_op jit(solution)/shard_map/ppermute | solution.py:66
  84.2 0.4 fusion.6
  84.6 0.4 fusion.7
  85.0 2.6 %collective-permute-start.3 = (f32[256]{0:T(256)S(1)}, f32[256]{0:T(256)S(1)}, u32[]{:S(2)}, u32[]{:S(2)}) collective-permute-start(f32[256]{0:T(256)S(1)} %max.25), channel_id=1, source_target_pairs={{0,1},{1,0},{2,3},{3,2},{4,5},{5,4},{6,7},{7,6},{8,9},{9,8},{10,11... | collective-permute-start | bytes 3080 | tf_op jit(solution)/shard_map/ppermute | solution.py:70
  87.5 0.4 fusion.5
  87.9 0.4 collective-permute-done.3
  88.5 21.6 %all_to_all.18 = f32[64,1,128]{2,1,0:T(1,128)S(1)} all-to-all(f32[64,1,128]{2,1,0:T(1,128)S(1)} %bitcast.17), channel_id=1, replica_groups=mesh['dp'=64,'pair'=8] {'dp'}, dimensions={0} | all-to-all | bytes 65536 | tf_op jit(solution)/shard_map/all_to_all | solution.py:102
  110.1 0.7 select_reduce_fusion
  (37 shorter events, 1.4 us)
Async XLA Ops:
  56.6 12.3 %collective-permute-start.1 = (bf16[272,1024]{1,0:T(8,128)(2,1)S(1)}, bf16[272,1024]{1,0:T(8,128)(2,1)S(1)}, u32[]{:S(2)}, u32[]{:S(2)}) collective-permute-start(bf16[272,1024]{1,0:T(8,128)(2,1)S(1)} %pad_maximum_fusion.1), channel_id=1, source_target_pairs={{0,6},{1,7},{2,0},{3,1},{4,2},{5,3},{6,4},{7,5},{8,14},{9,15},{10,... | collective-permute-start | bytes 1671176 | tf_op jit(solution)/shard_map/ppermute | solution.py:57
  61.2 15.2 %collective-permute-start = (bf16[272,1024]{1,0:T(8,128)(2,1)S(1)}, bf16[272,1024]{1,0:T(8,128)(2,1)S(1)}, u32[]{:S(2)}, u32[]{:S(2)}) collective-permute-start(bf16[272,1024]{1,0:T(8,128)(2,1)S(1)} %pad_maximum_fusion.1), channel_id=1, source_target_pairs={{0,2},{1,3},{2,4},{3,5},{4,6},{5,7},{6,0},{7,1},{8,10},{9,11},{10,... | collective-permute-start | bytes 1671176 | tf_op jit(solution)/shard_map/ppermute | solution.py:56
  69.0 9.4 %collective-permute-start.2 = (bf16[544,1024]{1,0:T(8,128)(2,1)S(1)}, bf16[544,1024]{1,0:T(8,128)(2,1)S(1)}, u32[]{:S(2)}, u32[]{:S(2)}) collective-permute-start(bf16[544,1024]{1,0:T(8,128)(2,1)S(1)} %pad_maximum_fusion), channel_id=1, source_target_pairs={{0,1},{1,0},{2,3},{3,2},{4,5},{5,4},{6,7},{7,6},{8,9},{9,8},{10,11... | collective-permute-start | bytes 3342344 | tf_op jit(solution)/shard_map/ppermute | solution.py:58
  78.8 9.5 %collective-permute-start.4 = (f32[256]{0:T(256)S(1)}, f32[256]{0:T(256)S(1)}, u32[]{:S(2)}, u32[]{:S(2)}) collective-permute-start(f32[256]{0:T(256)S(1)} %max.23), channel_id=1, source_target_pairs={{0,6},{1,7},{2,0},{3,1},{4,2},{5,3},{6,4},{7,5},{8,14},{9,15},{10,... | collective-permute-start | bytes 3080 | tf_op jit(solution)/shard_map/ppermute | solution.py:66
  85.0 3.4 %collective-permute-start.3 = (f32[256]{0:T(256)S(1)}, f32[256]{0:T(256)S(1)}, u32[]{:S(2)}, u32[]{:S(2)}) collective-permute-start(f32[256]{0:T(256)S(1)} %max.25), channel_id=1, source_target_pairs={{0,1},{1,0},{2,3},{3,2},{4,5},{5,4},{6,7},{7,6},{8,9},{9,8},{10,11... | collective-permute-start | bytes 3080 | tf_op jit(solution)/shard_map/ppermute | solution.py:70

commit v19 on v15

--- a/solution.py
+++ b/solution.py
@@ -62,12 +62,14 @@
         found = [block_best(query, k, slots, rows_total) for k in keys]
         return functools.reduce(jnp.maximum, found)
 
-    best = best_over(block, [block, from_below, from_above, sibling])
-    for_sibling = best_over(sibling, [from_below, from_above])
+    sibling_below = lax.ppermute(from_below, "pair", swap)
     for_below = best_over(from_below, [from_above, sibling_above])
-    from_sibling = lax.ppermute(for_sibling, "pair", swap)
     from_chip_above = lax.ppermute(for_below, "pair", down)
-    return jnp.maximum(best, jnp.maximum(from_sibling, from_chip_above))
+    sibling, sibling_below, _ = lax.optimization_barrier((sibling, sibling_below, for_below))
+    best = best_over(
+        block, [block, from_below, from_above, sibling, sibling_above, sibling_below]
+    )
+    return jnp.maximum(best, from_chip_above)
 
 
 def on_device(embedding, labels, order_ids):

time: 112 us -> 110 us (0.982); the launches traced: 110 us -> 110 us
    ppermute x1, starting transfers between devices: 3.94 us -> 2.07 us  [pair_best(): from_chip_above = lax.ppermute(for_below, 'pair', down)]
    ppermute x1, starting transfers between devices: 3.67 us -> 5.19 us  [pair_best(): sibling_below = lax.ppermute(from_below, 'pair', swap)]
    ppermute x1, waiting for transfers between devices: 1.18 us -> 0.01 us  [pair_best(): swapped = lax.ppermute(jnp.concatenate([block, from_above]), 'pair', swap)]
  transfers between devices with their start and end apart: 5 -> 5, of which waited for: 3 -> 2; matrix products, arithmetic and copies ran while one was open for 2% -> 3% of each run, Pallas kernels for 0% -> 0%
where the time goes in v19:
time: 110 us
  blocking collectives  72.8 us (66%)
  starting transfers between devices  20.9 us (19%)
  waiting for transfers between devices  6.41 us (6%)
  other arithmetic  5.71 us (5%)
  matrix products  2.85 us (3%)
    all_to_all x1, blocking collectives, on_device(): lax.all_to_all(send_rows.reshape(groups, capacity, -1), 'dp', split_axis=...  51.3 us
    all_to_all x1, blocking collectives, on_device(): lax.all_to_all(lanes, 'dp', split_axis=0, concat_axis=0, tiled=True)  21.5 us
    ppermute x1, starting transfers between devices, pair_best(): swapped = lax.ppermute(jnp.concatenate([block, from_above]), 'pair', swap)  7.05 us
    ppermute x1, waiting for transfers between devices, pair_best(): from_above = lax.ppermute(block, 'pair', down)  5.36 us
    ppermute x1, starting transfers between devices, pair_best(): sibling_below = lax.ppermute(from_below, 'pair', swap)  5.19 us
    ppermute x1, starting transfers between devices, pair_best(): from_above = lax.ppermute(block, 'pair', down)  4.64 us
    dot_general x8, matrix products, tile_best(): scores = jnp.dot(own_rows, other_rows.T, preferred_element_type=jnp.float32)  2.85 us
  transfers between devices with their start and end apart: 5, of which 2 were waited for; matrix products, arithmetic and copies ran while one was open for 3% of the time, Pallas kernels for 0%

profile of v19, /device:TPU:1, one launch (start us, length us, event | category | flops | bytes accessed | tf_op | source)
XLA Modules:
  0.0 109.6 jit_solution(283439364294593415)
XLA Ops:
  0.0 1.1 fusion.8
  1.1 0.7 and_select_fusion.9
  1.9 0.2 reduce_window_sum.11
  2.1 0.2 select_reduce_fusion.1
  2.2 1.1 fusion.9
  3.4 1.3 %scatter_custom_fusion = bf16[256,1152]{1,0:T(8,128)(2,1)S(1)} fusion(s32[128]{0:T(128)S(1)} %get-tuple-element.21, bf16[128,128]{1,0:T(8,128)(2,1)S(1)} %select_convert_fusion, bf16[]{:T(256)} %constant.155, bf16[128,1024]{1,0:T(8,128)(2,1)S(1)} %fusion.9, bf16[]{:T(256)} %constant.136.clone.1), kind=kCustom, calls=%fused_computation.32 | custom fusion | flops 589824 | bytes 884740 | tf_op jit(solution)/shard_map/scatter | solution.py:97
  4.9 51.3 %all_to_all.17 = bf16[64,4,1152]{2,1,0:T(4,128)(2,1)S(1)} all-to-all(bf16[64,4,1152]{2,1,0:T(4,128)(2,1)S(1)} %reshape.285), channel_id=1, replica_groups=mesh['dp'=64,'pair'=8] {'dp'}, dimensions={0} | all-to-all | bytes 1179648 | tf_op jit(solution)/shard_map/all_to_all | solution.py:98
  56.6 4.6 %collective-permute-start.1 = (bf16[272,1024]{1,0:T(8,128)(2,1)S(1)}, bf16[272,1024]{1,0:T(8,128)(2,1)S(1)}, u32[]{:S(2)}, u32[]{:S(2)}) collective-permute-start(bf16[272,1024]{1,0:T(8,128)(2,1)S(1)} %pad_maximum_fusion.1), channel_id=1, source_target_pairs={{0,6},{1,7},{2,0},{3,1},{4,2},{5,3},{6,4},{7,5},{8,14},{9,15},{10,... | collective-permute-start | bytes 1671176 | tf_op jit(solution)/shard_map/ppermute | solution.py:57
  61.2 1.9 %collective-permute-start = (bf16[272,1024]{1,0:T(8,128)(2,1)S(1)}, bf16[272,1024]{1,0:T(8,128)(2,1)S(1)}, u32[]{:S(2)}, u32[]{:S(2)}) collective-permute-start(bf16[272,1024]{1,0:T(8,128)(2,1)S(1)} %pad_maximum_fusion.1), channel_id=1, source_target_pairs={{0,2},{1,3},{2,4},{3,5},{4,6},{5,7},{6,0},{7,1},{8,10},{9,11},{10,... | collective-permute-start | bytes 1671176 | tf_op jit(solution)/shard_map/ppermute | solution.py:56
  63.2 0.3 fusion
  63.6 5.4 %collective-permute-done.1 = bf16[272,1024]{1,0:T(8,128)(2,1)S(1)} collective-permute-done((bf16[272,1024]{1,0:T(8,128)(2,1)S(1)}, bf16[272,1024]{1,0:T(8,128)(2,1)S(1)}, u32[]{:S(2)}, u32[]{:S(2)}) %collective-permute-start.1) | collective-permute-done | bytes 557088 | tf_op jit(solution)/shard_map/ppermute | solution.py:57
  69.0 7.1 %collective-permute-start.2 = (bf16[544,1024]{1,0:T(8,128)(2,1)S(1)}, bf16[544,1024]{1,0:T(8,128)(2,1)S(1)}, u32[]{:S(2)}, u32[]{:S(2)}) collective-permute-start(bf16[544,1024]{1,0:T(8,128)(2,1)S(1)} %pad_maximum_fusion), channel_id=1, source_target_pairs={{0,1},{1,0},{2,3},{3,2},{4,5},{5,4},{6,7},{7,6},{8,9},{9,8},{10,11... | collective-permute-start | bytes 3342344 | tf_op jit(solution)/shard_map/ppermute | solution.py:58
  76.1 5.2 %collective-permute-start.3 = (bf16[272,1024]{1,0:T(8,128)(2,1)S(1)}, bf16[272,1024]{1,0:T(8,128)(2,1)S(1)}, u32[]{:S(2)}, u32[]{:S(2)}) collective-permute-start(bf16[272,1024]{1,0:T(8,128)(2,1)S(1)} %collective-permute-done), channel_id=1, source_target_pairs={{0,1},{1,0},{2,3},{3,2},{4,5},{5,4},{6,7},{7,6},{8,9},{9,8},{10,11... | collective-permute-start | bytes 1671176 | tf_op jit(solution)/shard_map/ppermute | solution.py:65
  81.3 0.4 fusion.2
  81.7 0.4 fusion.1
  82.1 0.4 fusion.3
  82.5 0.4 fusion.4
  82.8 2.1 %collective-permute-start.4 = (f32[256]{0:T(256)S(1)}, f32[256]{0:T(256)S(1)}, u32[]{:S(2)}, u32[]{:S(2)}) collective-permute-start(f32[256]{0:T(256)S(1)} %max.23), channel_id=1, source_target_pairs={{0,6},{1,7},{2,0},{3,1},{4,2},{5,3},{6,4},{7,5},{8,14},{9,15},{10,... | collective-permute-start | bytes 3080 | tf_op jit(solution)/shard_map/ppermute | solution.py:67
  85.0 0.4 fusion.5
  85.4 0.4 fusion.7
  85.8 0.4 fusion.6
  86.1 1.0 collective-permute-done.4
  87.3 21.5 %all_to_all.18 = f32[64,1,128]{2,1,0:T(1,128)S(1)} all-to-all(f32[64,1,128]{2,1,0:T(1,128)S(1)} %bitcast.20), channel_id=1, replica_groups=mesh['dp'=64,'pair'=8] {'dp'}, dimensions={0} | all-to-all | bytes 65536 | tf_op jit(solution)/shard_map/all_to_all | solution.py:103
  108.9 0.7 select_reduce_fusion
  (37 shorter events, 1.2 us)
Async XLA Ops:
  56.6 12.3 %collective-permute-start.1 = (bf16[272,1024]{1,0:T(8,128)(2,1)S(1)}, bf16[272,1024]{1,0:T(8,128)(2,1)S(1)}, u32[]{:S(2)}, u32[]{:S(2)}) collective-permute-start(bf16[272,1024]{1,0:T(8,128)(2,1)S(1)} %pad_maximum_fusion.1), channel_id=1, source_target_pairs={{0,6},{1,7},{2,0},{3,1},{4,2},{5,3},{6,4},{7,5},{8,14},{9,15},{10,... | collective-permute-start | bytes 1671176 | tf_op jit(solution)/shard_map/ppermute | solution.py:57
  61.2 14.8 %collective-permute-start = (bf16[272,1024]{1,0:T(8,128)(2,1)S(1)}, bf16[272,1024]{1,0:T(8,128)(2,1)S(1)}, u32[]{:S(2)}, u32[]{:S(2)}) collective-permute-start(bf16[272,1024]{1,0:T(8,128)(2,1)S(1)} %pad_maximum_fusion.1), channel_id=1, source_target_pairs={{0,2},{1,3},{2,4},{3,5},{4,6},{5,7},{6,0},{7,1},{8,10},{9,11},{10,... | collective-permute-start | bytes 1671176 | tf_op jit(solution)/shard_map/ppermute | solution.py:56
  69.0 13.4 %collective-permute-start.2 = (bf16[544,1024]{1,0:T(8,128)(2,1)S(1)}, bf16[544,1024]{1,0:T(8,128)(2,1)S(1)}, u32[]{:S(2)}, u32[]{:S(2)}) collective-permute-start(bf16[544,1024]{1,0:T(8,128)(2,1)S(1)} %pad_maximum_fusion), channel_id=1, source_target_pairs={{0,1},{1,0},{2,3},{3,2},{4,5},{5,4},{6,7},{7,6},{8,9},{9,8},{10,11... | collective-permute-start | bytes 3342344 | tf_op jit(solution)/shard_map/ppermute | solution.py:58
  76.1 8.9 %collective-permute-start.3 = (bf16[272,1024]{1,0:T(8,128)(2,1)S(1)}, bf16[272,1024]{1,0:T(8,128)(2,1)S(1)}, u32[]{:S(2)}, u32[]{:S(2)}) collective-permute-start(bf16[272,1024]{1,0:T(8,128)(2,1)S(1)} %collective-permute-done), channel_id=1, source_target_pairs={{0,1},{1,0},{2,3},{3,2},{4,5},{5,4},{6,7},{7,6},{8,9},{9,8},{10,11... | collective-permute-start | bytes 1671176 | tf_op jit(solution)/shard_map/ppermute | solution.py:65
  82.8 4.3 %collective-permute-start.4 = (f32[256]{0:T(256)S(1)}, f32[256]{0:T(256)S(1)}, u32[]{:S(2)}, u32[]{:S(2)}) collective-permute-start(f32[256]{0:T(256)S(1)} %max.23), channel_id=1, source_target_pairs={{0,6},{1,7},{2,0},{3,1},{4,2},{5,3},{6,4},{7,5},{8,14},{9,15},{10,... | collective-permute-start | bytes 3080 | tf_op jit(solution)/shard_map/ppermute | solution.py:67

commit v20 on v19

--- a/solution.py
+++ b/solution.py
@@ -55,14 +55,14 @@
     rows = block.shape[0]
     from_below = lax.ppermute(block, "pair", up)
     from_above = lax.ppermute(block, "pair", down)
-    swapped = lax.ppermute(jnp.concatenate([block, from_above]), "pair", swap)
-    sibling, sibling_above = swapped[:rows], swapped[rows:]
+    sibling_above = lax.ppermute(from_above, "pair", swap)
 
     def best_over(query, keys):
         found = [block_best(query, k, slots, rows_total) for k in keys]
         return functools.reduce(jnp.maximum, found)
 
-    sibling_below = lax.ppermute(from_below, "pair", swap)
+    swapped = lax.ppermute(jnp.concatenate([block, from_below]), "pair", swap)
+    sibling, sibling_below = swapped[:rows], swapped[rows:]
     for_below = best_over(from_below, [from_above, sibling_above])
     from_chip_above = lax.ppermute(for_below, "pair", down)
     sibling, sibling_below, _ = lax.optimization_barrier((sibling, sibling_below, for_below))

time: 110 us -> 113 us (1.027)
  waiting for transfers between devices: 6.41 us -> 12.4 us
  starting transfers between devices: 20.9 us -> 17.7 us
    ppermute x1, waiting for transfers between devices: 0.01 us -> 5.02 us  [pair_best(): from_below = lax.ppermute(block, 'pair', up)]
    ppermute x2, starting transfers between devices: 12.2 us -> 9.25 us  [the longest x1 7.33 us: pair_best(): swapped = lax.ppermute(jnp.concatenate([block, from_below]), 'pair', swap)]
  transfers between devices with their start and end apart: 5 -> 5, of which waited for: 2 -> 4; matrix products, arithmetic and copies ran while one was open for 3% -> 3% of each run, Pallas kernels for 0% -> 0%
where the time goes in v20:
time: 113 us; the launch traced here: 112 us
  blocking collectives  72.8 us (64%)
  starting transfers between devices  17.7 us (16%)
  waiting for transfers between devices  12.4 us (11%)
  other arithmetic  5.72 us (5%)
  matrix products  2.85 us (3%)
    all_to_all x1, blocking collectives, on_device(): lax.all_to_all(send_rows.reshape(groups, capacity, -1), 'dp', split_axis=...  51.3 us
    all_to_all x1, blocking collectives, on_device(): lax.all_to_all(lanes, 'dp', split_axis=0, concat_axis=0, tiled=True)  21.6 us
    ppermute x1, starting transfers between devices, pair_best(): swapped = lax.ppermute(jnp.concatenate([block, from_below]), 'pair', swap)  7.33 us
    ppermute x1, waiting for transfers between devices, pair_best(): from_above = lax.ppermute(block, 'pair', down)  5.36 us
    ppermute x1, waiting for transfers between devices, pair_best(): from_below = lax.ppermute(block, 'pair', up)  5.02 us
    ppermute x1, starting transfers between devices, pair_best(): from_above = lax.ppermute(block, 'pair', down)  4.64 us
    dot_general x8, matrix products, tile_best(): scores = jnp.dot(own_rows, other_rows.T, preferred_element_type=jnp.float32)  2.85 us
  transfers between devices with their start and end apart: 5, of which 4 were waited for; matrix products, arithmetic and copies ran while one was open for 3% of the time, Pallas kernels for 0%

profile of v20, /device:TPU:1, one launch (start us, length us, event | category | flops | bytes accessed | tf_op | source)
XLA Modules:
  0.0 112.5 jit_solution(11911065967523877011)
XLA Ops:
  0.0 1.1 fusion.8
  1.1 0.7 and_select_fusion.9
  2.2 1.1 fusion.9
  3.4 1.3 %scatter_custom_fusion = bf16[256,1152]{1,0:T(8,128)(2,1)S(1)} fusion(s32[128]{0:T(128)S(1)} %get-tuple-element.21, bf16[128,128]{1,0:T(8,128)(2,1)S(1)} %select_convert_fusion, bf16[]{:T(256)} %constant.155, bf16[128,1024]{1,0:T(8,128)(2,1)S(1)} %fusion.9, bf16[]{:T(256)} %constant.136.clone.1), kind=kCustom, calls=%fused_computation.32 | custom fusion | flops 589824 | bytes 884740 | tf_op jit(solution)/shard_map/scatter | solution.py:97
  4.9 51.3 %all_to_all.17 = bf16[64,4,1152]{2,1,0:T(4,128)(2,1)S(1)} all-to-all(bf16[64,4,1152]{2,1,0:T(4,128)(2,1)S(1)} %reshape.285), channel_id=1, replica_groups=mesh['dp'=64,'pair'=8] {'dp'}, dimensions={0} | all-to-all | bytes 1179648 | tf_op jit(solution)/shard_map/all_to_all | solution.py:98
  56.6 4.6 %collective-permute-start.1 = (bf16[272,1024]{1,0:T(8,128)(2,1)S(1)}, bf16[272,1024]{1,0:T(8,128)(2,1)S(1)}, u32[]{:S(2)}, u32[]{:S(2)}) collective-permute-start(bf16[272,1024]{1,0:T(8,128)(2,1)S(1)} %pad_maximum_fusion.1), channel_id=1, source_target_pairs={{0,6},{1,7},{2,0},{3,1},{4,2},{5,3},{6,4},{7,5},{8,14},{9,15},{10,... | collective-permute-start | bytes 1671176 | tf_op jit(solution)/shard_map/ppermute | solution.py:57
  61.2 1.9 %collective-permute-start = (bf16[272,1024]{1,0:T(8,128)(2,1)S(1)}, bf16[272,1024]{1,0:T(8,128)(2,1)S(1)}, u32[]{:S(2)}, u32[]{:S(2)}) collective-permute-start(bf16[272,1024]{1,0:T(8,128)(2,1)S(1)} %pad_maximum_fusion.1), channel_id=1, source_target_pairs={{0,2},{1,3},{2,4},{3,5},{4,6},{5,7},{6,0},{7,1},{8,10},{9,11},{10,... | collective-permute-start | bytes 1671176 | tf_op jit(solution)/shard_map/ppermute | solution.py:56
  63.2 0.3 fusion
  63.6 5.4 %collective-permute-done.1 = bf16[272,1024]{1,0:T(8,128)(2,1)S(1)} collective-permute-done((bf16[272,1024]{1,0:T(8,128)(2,1)S(1)}, bf16[272,1024]{1,0:T(8,128)(2,1)S(1)}, u32[]{:S(2)}, u32[]{:S(2)}) %collective-permute-start.1) | collective-permute-done | bytes 557088 | tf_op jit(solution)/shard_map/ppermute | solution.py:57
  68.9 5.0 %collective-permute-done = bf16[272,1024]{1,0:T(8,128)(2,1)S(1)} collective-permute-done((bf16[272,1024]{1,0:T(8,128)(2,1)S(1)}, bf16[272,1024]{1,0:T(8,128)(2,1)S(1)}, u32[]{:S(2)}, u32[]{:S(2)}) %collective-permute-start) | collective-permute-done | bytes 557088 | tf_op jit(solution)/shard_map/ppermute | solution.py:56
  74.1 7.3 %collective-permute-start.2 = (bf16[544,1024]{1,0:T(8,128)(2,1)S(1)}, bf16[544,1024]{1,0:T(8,128)(2,1)S(1)}, u32[]{:S(2)}, u32[]{:S(2)}) collective-permute-start(bf16[544,1024]{1,0:T(8,128)(2,1)S(1)} %pad_maximum_fusion), channel_id=1, source_target_pairs={{0,1},{1,0},{2,3},{3,2},{4,5},{5,4},{6,7},{7,6},{8,9},{9,8},{10,11... | collective-permute-start | bytes 3342344 | tf_op jit(solution)/shard_map/ppermute | solution.py:64
  81.4 1.9 %collective-permute-start.3 = (bf16[272,1024]{1,0:T(8,128)(2,1)S(1)}, bf16[272,1024]{1,0:T(8,128)(2,1)S(1)}, u32[]{:S(2)}, u32[]{:S(2)}) collective-permute-start(bf16[272,1024]{1,0:T(8,128)(2,1)S(1)} %collective-permute-done.1), channel_id=1, source_target_pairs={{0,1},{1,0},{2,3},{3,2},{4,5},{5,4},{6,7},{7,6},{8,9},{9,8},{10,11... | collective-permute-start | bytes 1671176 | tf_op jit(solution)/shard_map/ppermute | solution.py:58
  83.4 0.4 fusion.1
  83.7 0.4 fusion.2
  84.1 0.4 fusion.3
  84.4 0.8 collective-permute-done.3
  85.3 0.4 fusion.4
  85.7 1.9 %collective-permute-start.4 = (f32[256]{0:T(256)S(1)}, f32[256]{0:T(256)S(1)}, u32[]{:S(2)}, u32[]{:S(2)}) collective-permute-start(f32[256]{0:T(256)S(1)} %max.23), channel_id=1, source_target_pairs={{0,6},{1,7},{2,0},{3,1},{4,2},{5,3},{6,4},{7,5},{8,14},{9,15},{10,... | collective-permute-start | bytes 3080 | tf_op jit(solution)/shard_map/ppermute | solution.py:67
  87.6 0.4 fusion.6
  88.1 0.4 fusion.5
  88.5 0.4 fusion.7
  88.8 1.1 %collective-permute-done.4 = f32[256]{0:T(256)S(1)} collective-permute-done((f32[256]{0:T(256)S(1)}, f32[256]{0:T(256)S(1)}, u32[]{:S(2)}, u32[]{:S(2)}) %collective-permute-start.4) | collective-permute-done | bytes 1056 | tf_op jit(solution)/shard_map/ppermute | solution.py:67
  90.1 21.6 %all_to_all.18 = f32[64,1,128]{2,1,0:T(1,128)S(1)} all-to-all(f32[64,1,128]{2,1,0:T(1,128)S(1)} %bitcast.20), channel_id=1, replica_groups=mesh['dp'=64,'pair'=8] {'dp'}, dimensions={0} | all-to-all | bytes 65536 | tf_op jit(solution)/shard_map/all_to_all | solution.py:103
  111.8 0.7 select_reduce_fusion
  (37 shorter events, 1.6 us)
Async XLA Ops:
  56.6 12.3 %collective-permute-start.1 = (bf16[272,1024]{1,0:T(8,128)(2,1)S(1)}, bf16[272,1024]{1,0:T(8,128)(2,1)S(1)}, u32[]{:S(2)}, u32[]{:S(2)}) collective-permute-start(bf16[272,1024]{1,0:T(8,128)(2,1)S(1)} %pad_maximum_fusion.1), channel_id=1, source_target_pairs={{0,6},{1,7},{2,0},{3,1},{4,2},{5,3},{6,4},{7,5},{8,14},{9,15},{10,... | collective-permute-start | bytes 1671176 | tf_op jit(solution)/shard_map/ppermute | solution.py:57
  61.2 12.7 %collective-permute-start = (bf16[272,1024]{1,0:T(8,128)(2,1)S(1)}, bf16[272,1024]{1,0:T(8,128)(2,1)S(1)}, u32[]{:S(2)}, u32[]{:S(2)}) collective-permute-start(bf16[272,1024]{1,0:T(8,128)(2,1)S(1)} %pad_maximum_fusion.1), channel_id=1, source_target_pairs={{0,2},{1,3},{2,4},{3,5},{4,6},{5,7},{6,0},{7,1},{8,10},{9,11},{10,... | collective-permute-start | bytes 1671176 | tf_op jit(solution)/shard_map/ppermute | solution.py:56
  74.1 13.9 %collective-permute-start.2 = (bf16[544,1024]{1,0:T(8,128)(2,1)S(1)}, bf16[544,1024]{1,0:T(8,128)(2,1)S(1)}, u32[]{:S(2)}, u32[]{:S(2)}) collective-permute-start(bf16[544,1024]{1,0:T(8,128)(2,1)S(1)} %pad_maximum_fusion), channel_id=1, source_target_pairs={{0,1},{1,0},{2,3},{3,2},{4,5},{5,4},{6,7},{7,6},{8,9},{9,8},{10,11... | collective-permute-start | bytes 3342344 | tf_op jit(solution)/shard_map/ppermute | solution.py:64
  81.4 3.9 %collective-permute-start.3 = (bf16[272,1024]{1,0:T(8,128)(2,1)S(1)}, bf16[272,1024]{1,0:T(8,128)(2,1)S(1)}, u32[]{:S(2)}, u32[]{:S(2)}) collective-permute-start(bf16[272,1024]{1,0:T(8,128)(2,1)S(1)} %collective-permute-done.1), channel_id=1, source_target_pairs={{0,1},{1,0},{2,3},{3,2},{4,5},{5,4},{6,7},{7,6},{8,9},{9,8},{10,11... | collective-permute-start | bytes 1671176 | tf_op jit(solution)/shard_map/ppermute | solution.py:58
  85.7 4.3 %collective-permute-start.4 = (f32[256]{0:T(256)S(1)}, f32[256]{0:T(256)S(1)}, u32[]{:S(2)}, u32[]{:S(2)}) collective-permute-start(f32[256]{0:T(256)S(1)} %max.23), channel_id=1, source_target_pairs={{0,6},{1,7},{2,0},{3,1},{4,2},{5,3},{6,4},{7,5},{8,14},{9,15},{10,... | collective-permute-start | bytes 3080 | tf_op jit(solution)/shard_map/ppermute | solution.py:67

commit v21 on v19

--- a/solution.py
+++ b/solution.py
@@ -62,10 +62,11 @@
         found = [block_best(query, k, slots, rows_total) for k in keys]
         return functools.reduce(jnp.maximum, found)
 
-    sibling_below = lax.ppermute(from_below, "pair", swap)
     for_below = best_over(from_below, [from_above, sibling_above])
     from_chip_above = lax.ppermute(for_below, "pair", down)
-    sibling, sibling_below, _ = lax.optimization_barrier((sibling, sibling_below, for_below))
+    later_below, _ = lax.optimization_barrier((from_below, for_below))
+    sibling_below = lax.ppermute(later_below, "pair", swap)
+    sibling, _ = lax.optimization_barrier((sibling, for_below))
     best = best_over(
         block, [block, from_below, from_above, sibling, sibling_above, sibling_below]
     )

time: 110 us -> 112 us (1.018)
    ppermute x1, starting transfers between devices: 2.07 us -> 5.33 us  [pair_best(): from_chip_above = lax.ppermute(for_below, 'pair', down)]
    ppermute x1, starting transfers between devices: 5.19 us -> 2.56 us  [pair_best(): sibling_below = lax.ppermute(later_below, 'pair', swap)]
    ppermute x1, waiting for transfers between devices: 0.01 us -> 1.19 us  [pair_best(): swapped = lax.ppermute(jnp.concatenate([block, from_above]), 'pair', swap)]
  transfers between devices with their start and end apart: 5 -> 5, of which waited for: 2 -> 3; matrix products, arithmetic and copies ran while one was open for 3% -> 2% of each run, Pallas kernels for 0% -> 0%
where the time goes in v21:
time: 112 us; the launch traced here: 111 us
  blocking collectives  72.8 us (65%)
  starting transfers between devices  21.5 us (19%)
  waiting for transfers between devices  7.37 us (7%)
  other arithmetic  5.72 us (5%)
  matrix products  2.84 us (3%)
    all_to_all x1, blocking collectives, on_device(): lax.all_to_all(send_rows.reshape(groups, capacity, -1), 'dp', split_axis=...  51.3 us
    all_to_all x1, blocking collectives, on_device(): lax.all_to_all(lanes, 'dp', split_axis=0, concat_axis=0, tiled=True)  21.6 us
    ppermute x1, starting transfers between devices, pair_best(): swapped = lax.ppermute(jnp.concatenate([block, from_above]), 'pair', swap)  7.05 us
    ppermute x1, waiting for transfers between devices, pair_best(): from_above = lax.ppermute(block, 'pair', down)  5.36 us
    ppermute x1, starting transfers between devices, pair_best(): from_chip_above = lax.ppermute(for_below, 'pair', down)  5.33 us
    ppermute x1, starting transfers between devices, pair_best(): from_above = lax.ppermute(block, 'pair', down)  4.64 us
    dot_general x8, matrix products, tile_best(): scores = jnp.dot(own_rows, other_rows.T, preferred_element_type=jnp.float32)  2.84 us
    ppermute x1, starting transfers between devices, pair_best(): sibling_below = lax.ppermute(later_below, 'pair', swap)  2.56 us
  transfers between devices with their start and end apart: 5, of which 3 were waited for; matrix products, arithmetic and copies ran while one was open for 2% of the time, Pallas kernels for 0%

profile of v21, /device:TPU:1, one launch (start us, length us, event | category | flops | bytes accessed | tf_op | source)
XLA Modules:
  0.0 111.2 jit_solution(1132433320874021714)
XLA Ops:
  0.0 1.1 fusion.8
  1.1 0.7 and_select_fusion.9
  1.9 0.2 reduce_window_sum.11
  2.2 1.1 fusion.9
  3.4 1.3 %scatter_custom_fusion = bf16[256,1152]{1,0:T(8,128)(2,1)S(1)} fusion(s32[128]{0:T(128)S(1)} %get-tuple-element.21, bf16[128,128]{1,0:T(8,128)(2,1)S(1)} %select_convert_fusion, bf16[]{:T(256)} %constant.155, bf16[128,1024]{1,0:T(8,128)(2,1)S(1)} %fusion.9, bf16[]{:T(256)} %constant.136.clone.1), kind=kCustom, calls=%fused_computation.32 | custom fusion | flops 589824 | bytes 884740 | tf_op jit(solution)/shard_map/scatter | solution.py:98
  4.9 51.3 %all_to_all.17 = bf16[64,4,1152]{2,1,0:T(4,128)(2,1)S(1)} all-to-all(bf16[64,4,1152]{2,1,0:T(4,128)(2,1)S(1)} %reshape.285), channel_id=1, replica_groups=mesh['dp'=64,'pair'=8] {'dp'}, dimensions={0} | all-to-all | bytes 1179648 | tf_op jit(solution)/shard_map/all_to_all | solution.py:99
  56.6 4.6 %collective-permute-start.1 = (bf16[272,1024]{1,0:T(8,128)(2,1)S(1)}, bf16[272,1024]{1,0:T(8,128)(2,1)S(1)}, u32[]{:S(2)}, u32[]{:S(2)}) collective-permute-start(bf16[272,1024]{1,0:T(8,128)(2,1)S(1)} %pad_maximum_fusion.1), channel_id=1, source_target_pairs={{0,6},{1,7},{2,0},{3,1},{4,2},{5,3},{6,4},{7,5},{8,14},{9,15},{10,... | collective-permute-start | bytes 1671176 | tf_op jit(solution)/shard_map/ppermute | solution.py:57
  61.2 1.9 %collective-permute-start = (bf16[272,1024]{1,0:T(8,128)(2,1)S(1)}, bf16[272,1024]{1,0:T(8,128)(2,1)S(1)}, u32[]{:S(2)}, u32[]{:S(2)}) collective-permute-start(bf16[272,1024]{1,0:T(8,128)(2,1)S(1)} %pad_maximum_fusion.1), channel_id=1, source_target_pairs={{0,2},{1,3},{2,4},{3,5},{4,6},{5,7},{6,0},{7,1},{8,10},{9,11},{10,... | collective-permute-start | bytes 1671176 | tf_op jit(solution)/shard_map/ppermute | solution.py:56
  63.2 0.3 fusion
  63.6 5.4 %collective-permute-done.1 = bf16[272,1024]{1,0:T(8,128)(2,1)S(1)} collective-permute-done((bf16[272,1024]{1,0:T(8,128)(2,1)S(1)}, bf16[272,1024]{1,0:T(8,128)(2,1)S(1)}, u32[]{:S(2)}, u32[]{:S(2)}) %collective-permute-start.1) | collective-permute-done | bytes 557088 | tf_op jit(solution)/shard_map/ppermute | solution.py:57
  69.0 7.1 %collective-permute-start.2 = (bf16[544,1024]{1,0:T(8,128)(2,1)S(1)}, bf16[544,1024]{1,0:T(8,128)(2,1)S(1)}, u32[]{:S(2)}, u32[]{:S(2)}) collective-permute-start(bf16[544,1024]{1,0:T(8,128)(2,1)S(1)} %pad_maximum_fusion), channel_id=1, source_target_pairs={{0,1},{1,0},{2,3},{3,2},{4,5},{5,4},{6,7},{7,6},{8,9},{9,8},{10,11... | collective-permute-start | bytes 3342344 | tf_op jit(solution)/shard_map/ppermute | solution.py:58
  76.1 0.4 fusion.2
  76.5 0.3 fusion.1
  76.9 0.4 fusion.3
  77.2 1.2 %collective-permute-done.2 = bf16[544,1024]{1,0:T(8,128)(2,1)S(1)} collective-permute-done((bf16[544,1024]{1,0:T(8,128)(2,1)S(1)}, bf16[544,1024]{1,0:T(8,128)(2,1)S(1)}, u32[]{:S(2)}, u32[]{:S(2)}) %collective-permute-start.2) | collective-permute-done | bytes 1114144 | tf_op jit(solution)/shard_map/ppermute | solution.py:58
  78.4 0.4 fusion.4
  78.8 5.3 %collective-permute-start.4 = (f32[256]{0:T(256)S(1)}, f32[256]{0:T(256)S(1)}, u32[]{:S(2)}, u32[]{:S(2)}) collective-permute-start(f32[256]{0:T(256)S(1)} %max.23), channel_id=1, source_target_pairs={{0,6},{1,7},{2,0},{3,1},{4,2},{5,3},{6,4},{7,5},{8,14},{9,15},{10,... | collective-permute-start | bytes 3080 | tf_op jit(solution)/shard_map/ppermute | solution.py:66
  84.2 2.6 %collective-permute-start.3 = (bf16[272,1024]{1,0:T(8,128)(2,1)S(1)}, bf16[272,1024]{1,0:T(8,128)(2,1)S(1)}, u32[]{:S(2)}, u32[]{:S(2)}) collective-permute-start(bf16[272,1024]{1,0:T(8,128)(2,1)S(1)} %collective-permute-done), channel_id=1, source_target_pairs={{0,1},{1,0},{2,3},{3,2},{4,5},{5,4},{6,7},{7,6},{8,9},{9,8},{10,11... | collective-permute-start | bytes 1671176 | tf_op jit(solution)/shard_map/ppermute | solution.py:68
  86.8 0.4 fusion.5
  87.1 0.4 fusion.6
  87.5 0.8 collective-permute-done.3
  88.4 0.4 fusion.7
  88.9 21.6 %all_to_all.18 = f32[64,1,128]{2,1,0:T(1,128)S(1)} all-to-all(f32[64,1,128]{2,1,0:T(1,128)S(1)} %bitcast.20), channel_id=1, replica_groups=mesh['dp'=64,'pair'=8] {'dp'}, dimensions={0} | all-to-all | bytes 65536 | tf_op jit(solution)/shard_map/all_to_all | solution.py:104
  110.5 0.7 select_reduce_fusion
  (37 shorter events, 1.4 us)
Async XLA Ops:
  56.6 12.3 %collective-permute-start.1 = (bf16[272,1024]{1,0:T(8,128)(2,1)S(1)}, bf16[272,1024]{1,0:T(8,128)(2,1)S(1)}, u32[]{:S(2)}, u32[]{:S(2)}) collective-permute-start(bf16[272,1024]{1,0:T(8,128)(2,1)S(1)} %pad_maximum_fusion.1), channel_id=1, source_target_pairs={{0,6},{1,7},{2,0},{3,1},{4,2},{5,3},{6,4},{7,5},{8,14},{9,15},{10,... | collective-permute-start | bytes 1671176 | tf_op jit(solution)/shard_map/ppermute | solution.py:57
  61.2 15.2 %collective-permute-start = (bf16[272,1024]{1,0:T(8,128)(2,1)S(1)}, bf16[272,1024]{1,0:T(8,128)(2,1)S(1)}, u32[]{:S(2)}, u32[]{:S(2)}) collective-permute-start(bf16[272,1024]{1,0:T(8,128)(2,1)S(1)} %pad_maximum_fusion.1), channel_id=1, source_target_pairs={{0,2},{1,3},{2,4},{3,5},{4,6},{5,7},{6,0},{7,1},{8,10},{9,11},{10,... | collective-permute-start | bytes 1671176 | tf_op jit(solution)/shard_map/ppermute | solution.py:56
  69.0 9.4 %collective-permute-start.2 = (bf16[544,1024]{1,0:T(8,128)(2,1)S(1)}, bf16[544,1024]{1,0:T(8,128)(2,1)S(1)}, u32[]{:S(2)}, u32[]{:S(2)}) collective-permute-start(bf16[544,1024]{1,0:T(8,128)(2,1)S(1)} %pad_maximum_fusion), channel_id=1, source_target_pairs={{0,1},{1,0},{2,3},{3,2},{4,5},{5,4},{6,7},{7,6},{8,9},{9,8},{10,11... | collective-permute-start | bytes 3342344 | tf_op jit(solution)/shard_map/ppermute | solution.py:58
  78.8 9.9 %collective-permute-start.4 = (f32[256]{0:T(256)S(1)}, f32[256]{0:T(256)S(1)}, u32[]{:S(2)}, u32[]{:S(2)}) collective-permute-start(f32[256]{0:T(256)S(1)} %max.23), channel_id=1, source_target_pairs={{0,6},{1,7},{2,0},{3,1},{4,2},{5,3},{6,4},{7,5},{8,14},{9,15},{10,... | collective-permute-start | bytes 3080 | tf_op jit(solution)/shard_map/ppermute | solution.py:66
  84.2 4.1 %collective-permute-start.3 = (bf16[272,1024]{1,0:T(8,128)(2,1)S(1)}, bf16[272,1024]{1,0:T(8,128)(2,1)S(1)}, u32[]{:S(2)}, u32[]{:S(2)}) collective-permute-start(bf16[272,1024]{1,0:T(8,128)(2,1)S(1)} %collective-permute-done), channel_id=1, source_target_pairs={{0,1},{1,0},{2,3},{3,2},{4,5},{5,4},{6,7},{7,6},{8,9},{9,8},{10,11... | collective-permute-start | bytes 1671176 | tf_op jit(solution)/shard_map/ppermute | solution.py:68

commit v22 on v19

--- a/solution.py
+++ b/solution.py
@@ -65,10 +65,10 @@
     sibling_below = lax.ppermute(from_below, "pair", swap)
     for_below = best_over(from_below, [from_above, sibling_above])
     from_chip_above = lax.ppermute(for_below, "pair", down)
-    sibling, sibling_below, _ = lax.optimization_barrier((sibling, sibling_below, for_below))
-    best = best_over(
-        block, [block, from_below, from_above, sibling, sibling_above, sibling_below]
+    late = lax.optimization_barrier(
+        (block, from_below, from_above, sibling, sibling_above, sibling_below, for_below)
     )
+    best = best_over(late[0], list(late[:6]))
     return jnp.maximum(best, from_chip_above)
 
 

time: 110 us -> 110 us (level)
  transfers between devices with their start and end apart: 5 -> 5, of which waited for: 2 -> 1; matrix products, arithmetic and copies ran while one was open for 3% -> 3% of each run, Pallas kernels for 0% -> 0%
where the time goes in v22:
time: 110 us; the launch traced here: 109 us
  blocking collectives  72.8 us (66%)
  starting transfers between devices  20.9 us (19%)
  other arithmetic  5.77 us (5%)
  waiting for transfers between devices  5.75 us (5%)
  matrix products  2.87 us (3%)
    all_to_all x1, blocking collectives, on_device(): lax.all_to_all(send_rows.reshape(groups, capacity, -1), 'dp', split_axis=...  51.3 us
    all_to_all x1, blocking collectives, on_device(): lax.all_to_all(lanes, 'dp', split_axis=0, concat_axis=0, tiled=True)  21.5 us
    ppermute x1, starting transfers between devices, pair_best(): swapped = lax.ppermute(jnp.concatenate([block, from_above]), 'pair', swap)  7.05 us
    ppermute x1, waiting for transfers between devices, pair_best(): from_above = lax.ppermute(block, 'pair', down)  5.74 us
    ppermute x1, starting transfers between devices, pair_best(): sibling_below = lax.ppermute(from_below, 'pair', swap)  5.21 us
    ppermute x1, starting transfers between devices, pair_best(): from_above = lax.ppermute(block, 'pair', down)  4.64 us
    dot_general x8, matrix products, tile_best(): scores = jnp.dot(own_rows, other_rows.T, preferred_element_type=jnp.float32)  2.87 us
  transfers between devices with their start and end apart: 5, of which 1 were waited for; matrix products, arithmetic and copies ran while one was open for 3% of the time, Pallas kernels for 0%

profile of v22, /device:TPU:1, one launch (start us, length us, event | category | flops | bytes accessed | tf_op | source)
XLA Modules:
  0.0 109.2 jit_solution(15566961829514709995)
XLA Ops:
  0.0 0.7 and_select_fusion.11
  0.8 0.2 reduce_window_sum.11
  1.0 0.2 select_reduce_fusion.1
  1.2 1.1 fusion.8
  2.2 1.1 fusion.9
  3.4 1.3 %scatter_custom_fusion = bf16[256,1152]{1,0:T(8,128)(2,1)S(1)} fusion(s32[128]{0:T(128)S(1)} %get-tuple-element.33, bf16[128,128]{1,0:T(8,128)(2,1)S(1)} %select_convert_fusion, bf16[]{:T(256)} %constant.165, bf16[128,1024]{1,0:T(8,128)(2,1)S(1)} %fusion.9, bf16[]{:T(256)} %constant.146.clone.1), kind=kCustom, calls=%fused_computation.32 | custom fusion | flops 589824 | bytes 884740 | tf_op jit(solution)/shard_map/scatter | solution.py:97
  4.8 0.1 reshape.321
  4.9 51.3 %all_to_all.17 = bf16[64,4,1152]{2,1,0:T(4,128)(2,1)S(1)} all-to-all(bf16[64,4,1152]{2,1,0:T(4,128)(2,1)S(1)} %reshape.321), channel_id=1, replica_groups=mesh['dp'=64,'pair'=8] {'dp'}, dimensions={0} | all-to-all | bytes 1179648 | tf_op jit(solution)/shard_map/all_to_all | solution.py:98
  56.6 4.6 %collective-permute-start.1 = (bf16[272,1024]{1,0:T(8,128)(2,1)S(1)}, bf16[272,1024]{1,0:T(8,128)(2,1)S(1)}, u32[]{:S(2)}, u32[]{:S(2)}) collective-permute-start(bf16[272,1024]{1,0:T(8,128)(2,1)S(1)} %pad_maximum_fusion.1), channel_id=1, source_target_pairs={{0,6},{1,7},{2,0},{3,1},{4,2},{5,3},{6,4},{7,5},{8,14},{9,15},{10,... | collective-permute-start | bytes 1671176 | tf_op jit(solution)/shard_map/ppermute | solution.py:57
  61.2 1.9 %collective-permute-start = (bf16[272,1024]{1,0:T(8,128)(2,1)S(1)}, bf16[272,1024]{1,0:T(8,128)(2,1)S(1)}, u32[]{:S(2)}, u32[]{:S(2)}) collective-permute-start(bf16[272,1024]{1,0:T(8,128)(2,1)S(1)} %pad_maximum_fusion.1), channel_id=1, source_target_pairs={{0,2},{1,3},{2,4},{3,5},{4,6},{5,7},{6,0},{7,1},{8,10},{9,11},{10,... | collective-permute-start | bytes 1671176 | tf_op jit(solution)/shard_map/ppermute | solution.py:56
  63.2 5.7 %collective-permute-done.1 = bf16[272,1024]{1,0:T(8,128)(2,1)S(1)} collective-permute-done((bf16[272,1024]{1,0:T(8,128)(2,1)S(1)}, bf16[272,1024]{1,0:T(8,128)(2,1)S(1)}, u32[]{:S(2)}, u32[]{:S(2)}) %collective-permute-start.1) | collective-permute-done | bytes 557088 | tf_op jit(solution)/shard_map/ppermute | solution.py:57
  69.0 7.1 %collective-permute-start.2 = (bf16[544,1024]{1,0:T(8,128)(2,1)S(1)}, bf16[544,1024]{1,0:T(8,128)(2,1)S(1)}, u32[]{:S(2)}, u32[]{:S(2)}) collective-permute-start(bf16[544,1024]{1,0:T(8,128)(2,1)S(1)} %pad_maximum_fusion), channel_id=1, source_target_pairs={{0,1},{1,0},{2,3},{3,2},{4,5},{5,4},{6,7},{7,6},{8,9},{9,8},{10,11... | collective-permute-start | bytes 3342344 | tf_op jit(solution)/shard_map/ppermute | solution.py:58
  76.1 5.2 %collective-permute-start.3 = (bf16[272,1024]{1,0:T(8,128)(2,1)S(1)}, bf16[272,1024]{1,0:T(8,128)(2,1)S(1)}, u32[]{:S(2)}, u32[]{:S(2)}) collective-permute-start(bf16[272,1024]{1,0:T(8,128)(2,1)S(1)} %collective-permute-done), channel_id=1, source_target_pairs={{0,1},{1,0},{2,3},{3,2},{4,5},{5,4},{6,7},{7,6},{8,9},{9,8},{10,11... | collective-permute-start | bytes 1671176 | tf_op jit(solution)/shard_map/ppermute | solution.py:65
  81.3 0.4 fusion
  81.8 0.4 fusion.1
  82.1 2.0 %collective-permute-start.4 = (f32[256]{0:T(256)S(1)}, f32[256]{0:T(256)S(1)}, u32[]{:S(2)}, u32[]{:S(2)}) collective-permute-start(f32[256]{0:T(256)S(1)} %max.21), channel_id=1, source_target_pairs={{0,6},{1,7},{2,0},{3,1},{4,2},{5,3},{6,4},{7,5},{8,14},{9,15},{10,... | collective-permute-start | bytes 3080 | tf_op jit(solution)/shard_map/ppermute | solution.py:67
  84.5 0.4 fusion.3
  84.8 0.4 fusion.4
  85.2 0.4 fusion.5
  85.6 0.4 fusion.6
  85.9 0.4 fusion.7
  86.3 0.4 fusion.2
  86.8 21.5 %all_to_all.18 = f32[64,1,128]{2,1,0:T(1,128)S(1)} all-to-all(f32[64,1,128]{2,1,0:T(1,128)S(1)} %bitcast.24), channel_id=1, replica_groups=mesh['dp'=64,'pair'=8] {'dp'}, dimensions={0} | all-to-all | bytes 65536 | tf_op jit(solution)/shard_map/all_to_all | solution.py:103
  108.4 0.7 select_reduce_fusion
  (43 shorter events, 1.1 us)
Async XLA Ops:
  56.6 12.3 %collective-permute-start.1 = (bf16[272,1024]{1,0:T(8,128)(2,1)S(1)}, bf16[272,1024]{1,0:T(8,128)(2,1)S(1)}, u32[]{:S(2)}, u32[]{:S(2)}) collective-permute-start(bf16[272,1024]{1,0:T(8,128)(2,1)S(1)} %pad_maximum_fusion.1), channel_id=1, source_target_pairs={{0,6},{1,7},{2,0},{3,1},{4,2},{5,3},{6,4},{7,5},{8,14},{9,15},{10,... | collective-permute-start | bytes 1671176 | tf_op jit(solution)/shard_map/ppermute | solution.py:57
  61.2 14.8 %collective-permute-start = (bf16[272,1024]{1,0:T(8,128)(2,1)S(1)}, bf16[272,1024]{1,0:T(8,128)(2,1)S(1)}, u32[]{:S(2)}, u32[]{:S(2)}) collective-permute-start(bf16[272,1024]{1,0:T(8,128)(2,1)S(1)} %pad_maximum_fusion.1), channel_id=1, source_target_pairs={{0,2},{1,3},{2,4},{3,5},{4,6},{5,7},{6,0},{7,1},{8,10},{9,11},{10,... | collective-permute-start | bytes 1671176 | tf_op jit(solution)/shard_map/ppermute | solution.py:56
  69.0 12.7 %collective-permute-start.2 = (bf16[544,1024]{1,0:T(8,128)(2,1)S(1)}, bf16[544,1024]{1,0:T(8,128)(2,1)S(1)}, u32[]{:S(2)}, u32[]{:S(2)}) collective-permute-start(bf16[544,1024]{1,0:T(8,128)(2,1)S(1)} %pad_maximum_fusion), channel_id=1, source_target_pairs={{0,1},{1,0},{2,3},{3,2},{4,5},{5,4},{6,7},{7,6},{8,9},{9,8},{10,11... | collective-permute-start | bytes 3342344 | tf_op jit(solution)/shard_map/ppermute | solution.py:58
  76.1 8.2 %collective-permute-start.3 = (bf16[272,1024]{1,0:T(8,128)(2,1)S(1)}, bf16[272,1024]{1,0:T(8,128)(2,1)S(1)}, u32[]{:S(2)}, u32[]{:S(2)}) collective-permute-start(bf16[272,1024]{1,0:T(8,128)(2,1)S(1)} %collective-permute-done), channel_id=1, source_target_pairs={{0,1},{1,0},{2,3},{3,2},{4,5},{5,4},{6,7},{7,6},{8,9},{9,8},{10,11... | collective-permute-start | bytes 1671176 | tf_op jit(solution)/shard_map/ppermute | solution.py:65
  82.1 4.5 %collective-permute-start.4 = (f32[256]{0:T(256)S(1)}, f32[256]{0:T(256)S(1)}, u32[]{:S(2)}, u32[]{:S(2)}) collective-permute-start(f32[256]{0:T(256)S(1)} %max.21), channel_id=1, source_target_pairs={{0,6},{1,7},{2,0},{3,1},{4,2},{5,3},{6,4},{7,5},{8,14},{9,15},{10,... | collective-permute-start | bytes 3080 | tf_op jit(solution)/shard_map/ppermute | solution.py:67

commit v23 on v22

--- a/solution.py
+++ b/solution.py
@@ -62,9 +62,10 @@
         found = [block_best(query, k, slots, rows_total) for k in keys]
         return functools.reduce(jnp.maximum, found)
 
-    sibling_below = lax.ppermute(from_below, "pair", swap)
     for_below = best_over(from_below, [from_above, sibling_above])
     from_chip_above = lax.ppermute(for_below, "pair", down)
+    later_below, _ = lax.optimization_barrier((from_below, for_below))
+    sibling_below = lax.ppermute(later_below, "pair", swap)
     late = lax.optimization_barrier(
         (block, from_below, from_above, sibling, sibling_above, sibling_below, for_below)
     )

time: 110 us -> 112 us (1.018)
  waiting for transfers between devices: 5.75 us -> 7.66 us
    ppermute x1, starting transfers between devices: 2.03 us -> 4.27 us  [pair_best(): from_chip_above = lax.ppermute(for_below, 'pair', down)]
    ppermute x1, waiting for transfers between devices: 0.01 us -> 1.91 us  [pair_best(): swapped = lax.ppermute(jnp.concatenate([block, from_above]), 'pair', swap)]
    ppermute x1, starting transfers between devices: 5.21 us -> 3.33 us  [pair_best(): sibling_below = lax.ppermute(later_below, 'pair', swap)]
  transfers between devices with their start and end apart: 5 -> 5, of which waited for: 1 -> 2; matrix products, arithmetic and copies ran while one was open for 3% -> 3% of each run, Pallas kernels for 0% -> 0%
where the time goes in v23:
time: 112 us; the launch traced here: 111 us
  blocking collectives  72.9 us (65%)
  starting transfers between devices  21.2 us (19%)
  waiting for transfers between devices  7.66 us (7%)
  other arithmetic  5.77 us (5%)
  matrix products  2.87 us (3%)
    all_to_all x1, blocking collectives, on_device(): lax.all_to_all(send_rows.reshape(groups, capacity, -1), 'dp', split_axis=...  51.3 us
    all_to_all x1, blocking collectives, on_device(): lax.all_to_all(lanes, 'dp', split_axis=0, concat_axis=0, tiled=True)  21.6 us
    ppermute x1, starting transfers between devices, pair_best(): swapped = lax.ppermute(jnp.concatenate([block, from_above]), 'pair', swap)  7.05 us
    ppermute x1, waiting for transfers between devices, pair_best(): from_above = lax.ppermute(block, 'pair', down)  5.74 us
    ppermute x1, starting transfers between devices, pair_best(): from_above = lax.ppermute(block, 'pair', down)  4.64 us
    ppermute x1, starting transfers between devices, pair_best(): from_chip_above = lax.ppermute(for_below, 'pair', down)  4.27 us
    ppermute x1, starting transfers between devices, pair_best(): sibling_below = lax.ppermute(later_below, 'pair', swap)  3.33 us
    dot_general x8, matrix products, tile_best(): scores = jnp.dot(own_rows, other_rows.T, preferred_element_type=jnp.float32)  2.87 us
  transfers between devices with their start and end apart: 5, of which 2 were waited for; matrix products, arithmetic and copies ran while one was open for 3% of the time, Pallas kernels for 0%

profile of v23, /device:TPU:1, one launch (start us, length us, event | category | flops | bytes accessed | tf_op | source)
XLA Modules:
  0.0 111.4 jit_solution(9039949601676162706)
XLA Ops:
  0.0 1.1 fusion.8
  1.1 0.7 and_select_fusion.11
  1.9 0.2 reduce_window_sum.11
  2.1 0.2 select_reduce_fusion.1
  2.2 1.1 fusion.9
  3.4 1.3 %scatter_custom_fusion = bf16[256,1152]{1,0:T(8,128)(2,1)S(1)} fusion(s32[128]{0:T(128)S(1)} %get-tuple-element.35, bf16[128,128]{1,0:T(8,128)(2,1)S(1)} %select_convert_fusion, bf16[]{:T(256)} %constant.165, bf16[128,1024]{1,0:T(8,128)(2,1)S(1)} %fusion.9, bf16[]{:T(256)} %constant.146.clone.1), kind=kCustom, calls=%fused_computation.32 | custom fusion | flops 589824 | bytes 884740 | tf_op jit(solution)/shard_map/scatter | solution.py:98
  4.9 51.3 %all_to_all.17 = bf16[64,4,1152]{2,1,0:T(4,128)(2,1)S(1)} all-to-all(bf16[64,4,1152]{2,1,0:T(4,128)(2,1)S(1)} %reshape.321), channel_id=1, replica_groups=mesh['dp'=64,'pair'=8] {'dp'}, dimensions={0} | all-to-all | bytes 1179648 | tf_op jit(solution)/shard_map/all_to_all | solution.py:99
  56.6 4.6 %collective-permute-start.1 = (bf16[272,1024]{1,0:T(8,128)(2,1)S(1)}, bf16[272,1024]{1,0:T(8,128)(2,1)S(1)}, u32[]{:S(2)}, u32[]{:S(2)}) collective-permute-start(bf16[272,1024]{1,0:T(8,128)(2,1)S(1)} %pad_maximum_fusion.1), channel_id=1, source_target_pairs={{0,6},{1,7},{2,0},{3,1},{4,2},{5,3},{6,4},{7,5},{8,14},{9,15},{10,... | collective-permute-start | bytes 1671176 | tf_op jit(solution)/shard_map/ppermute | solution.py:57
  61.2 1.9 %collective-permute-start = (bf16[272,1024]{1,0:T(8,128)(2,1)S(1)}, bf16[272,1024]{1,0:T(8,128)(2,1)S(1)}, u32[]{:S(2)}, u32[]{:S(2)}) collective-permute-start(bf16[272,1024]{1,0:T(8,128)(2,1)S(1)} %pad_maximum_fusion.1), channel_id=1, source_target_pairs={{0,2},{1,3},{2,4},{3,5},{4,6},{5,7},{6,0},{7,1},{8,10},{9,11},{10,... | collective-permute-start | bytes 1671176 | tf_op jit(solution)/shard_map/ppermute | solution.py:56
  63.2 5.7 %collective-permute-done.1 = bf16[272,1024]{1,0:T(8,128)(2,1)S(1)} collective-permute-done((bf16[272,1024]{1,0:T(8,128)(2,1)S(1)}, bf16[272,1024]{1,0:T(8,128)(2,1)S(1)}, u32[]{:S(2)}, u32[]{:S(2)}) %collective-permute-start.1) | collective-permute-done | bytes 557088 | tf_op jit(solution)/shard_map/ppermute | solution.py:57
  69.0 7.1 %collective-permute-start.2 = (bf16[544,1024]{1,0:T(8,128)(2,1)S(1)}, bf16[544,1024]{1,0:T(8,128)(2,1)S(1)}, u32[]{:S(2)}, u32[]{:S(2)}) collective-permute-start(bf16[544,1024]{1,0:T(8,128)(2,1)S(1)} %pad_maximum_fusion), channel_id=1, source_target_pairs={{0,1},{1,0},{2,3},{3,2},{4,5},{5,4},{6,7},{7,6},{8,9},{9,8},{10,11... | collective-permute-start | bytes 3342344 | tf_op jit(solution)/shard_map/ppermute | solution.py:58
  76.1 0.4 fusion
  76.5 1.9 %collective-permute-done.2 = bf16[544,1024]{1,0:T(8,128)(2,1)S(1)} collective-permute-done((bf16[544,1024]{1,0:T(8,128)(2,1)S(1)}, bf16[544,1024]{1,0:T(8,128)(2,1)S(1)}, u32[]{:S(2)}, u32[]{:S(2)}) %collective-permute-start.2) | collective-permute-done | bytes 1114144 | tf_op jit(solution)/shard_map/ppermute | solution.py:58
  78.4 0.4 fusion.1
  78.8 3.3 %collective-permute-start.3 = (bf16[272,1024]{1,0:T(8,128)(2,1)S(1)}, bf16[272,1024]{1,0:T(8,128)(2,1)S(1)}, u32[]{:S(2)}, u32[]{:S(2)}) collective-permute-start(bf16[272,1024]{1,0:T(8,128)(2,1)S(1)} %collective-permute-done), channel_id=1, source_target_pairs={{0,1},{1,0},{2,3},{3,2},{4,5},{5,4},{6,7},{7,6},{8,9},{9,8},{10,11... | collective-permute-start | bytes 1671176 | tf_op jit(solution)/shard_map/ppermute | solution.py:68
  82.1 4.3 %collective-permute-start.4 = (f32[256]{0:T(256)S(1)}, f32[256]{0:T(256)S(1)}, u32[]{:S(2)}, u32[]{:S(2)}) collective-permute-start(f32[256]{0:T(256)S(1)} %max.21), channel_id=1, source_target_pairs={{0,6},{1,7},{2,0},{3,1},{4,2},{5,3},{6,4},{7,5},{8,14},{9,15},{10,... | collective-permute-start | bytes 3080 | tf_op jit(solution)/shard_map/ppermute | solution.py:66
  86.7 0.4 fusion.3
  87.1 0.4 fusion.4
  87.5 0.4 fusion.5
  87.8 0.4 fusion.6
  88.2 0.4 fusion.7
  88.5 0.4 fusion.2
  89.0 21.6 %all_to_all.18 = f32[64,1,128]{2,1,0:T(1,128)S(1)} all-to-all(f32[64,1,128]{2,1,0:T(1,128)S(1)} %bitcast.25), channel_id=1, replica_groups=mesh['dp'=64,'pair'=8] {'dp'}, dimensions={0} | all-to-all | bytes 65536 | tf_op jit(solution)/shard_map/all_to_all | solution.py:104
  110.7 0.7 select_reduce_fusion
  (43 shorter events, 1.3 us)
Async XLA Ops:
  56.6 12.3 %collective-permute-start.1 = (bf16[272,1024]{1,0:T(8,128)(2,1)S(1)}, bf16[272,1024]{1,0:T(8,128)(2,1)S(1)}, u32[]{:S(2)}, u32[]{:S(2)}) collective-permute-start(bf16[272,1024]{1,0:T(8,128)(2,1)S(1)} %pad_maximum_fusion.1), channel_id=1, source_target_pairs={{0,6},{1,7},{2,0},{3,1},{4,2},{5,3},{6,4},{7,5},{8,14},{9,15},{10,... | collective-permute-start | bytes 1671176 | tf_op jit(solution)/shard_map/ppermute | solution.py:57
  61.2 14.8 %collective-permute-start = (bf16[272,1024]{1,0:T(8,128)(2,1)S(1)}, bf16[272,1024]{1,0:T(8,128)(2,1)S(1)}, u32[]{:S(2)}, u32[]{:S(2)}) collective-permute-start(bf16[272,1024]{1,0:T(8,128)(2,1)S(1)} %pad_maximum_fusion.1), channel_id=1, source_target_pairs={{0,2},{1,3},{2,4},{3,5},{4,6},{5,7},{6,0},{7,1},{8,10},{9,11},{10,... | collective-permute-start | bytes 1671176 | tf_op jit(solution)/shard_map/ppermute | solution.py:56
  69.0 9.4 %collective-permute-start.2 = (bf16[544,1024]{1,0:T(8,128)(2,1)S(1)}, bf16[544,1024]{1,0:T(8,128)(2,1)S(1)}, u32[]{:S(2)}, u32[]{:S(2)}) collective-permute-start(bf16[544,1024]{1,0:T(8,128)(2,1)S(1)} %pad_maximum_fusion), channel_id=1, source_target_pairs={{0,1},{1,0},{2,3},{3,2},{4,5},{5,4},{6,7},{7,6},{8,9},{9,8},{10,11... | collective-permute-start | bytes 3342344 | tf_op jit(solution)/shard_map/ppermute | solution.py:58
  78.8 7.7 %collective-permute-start.3 = (bf16[272,1024]{1,0:T(8,128)(2,1)S(1)}, bf16[272,1024]{1,0:T(8,128)(2,1)S(1)}, u32[]{:S(2)}, u32[]{:S(2)}) collective-permute-start(bf16[272,1024]{1,0:T(8,128)(2,1)S(1)} %collective-permute-done), channel_id=1, source_target_pairs={{0,1},{1,0},{2,3},{3,2},{4,5},{5,4},{6,7},{7,6},{8,9},{9,8},{10,11... | collective-permute-start | bytes 1671176 | tf_op jit(solution)/shard_map/ppermute | solution.py:68
  82.1 6.8 %collective-permute-start.4 = (f32[256]{0:T(256)S(1)}, f32[256]{0:T(256)S(1)}, u32[]{:S(2)}, u32[]{:S(2)}) collective-permute-start(f32[256]{0:T(256)S(1)} %max.21), channel_id=1, source_target_pairs={{0,6},{1,7},{2,0},{3,1},{4,2},{5,3},{6,4},{7,5},{8,14},{9,15},{10,... | collective-permute-start | bytes 3080 | tf_op jit(solution)/shard_map/ppermute | solution.py:66

commit v24 on v22

--- a/solution.py
+++ b/solution.py
@@ -55,14 +55,14 @@
     rows = block.shape[0]
     from_below = lax.ppermute(block, "pair", up)
     from_above = lax.ppermute(block, "pair", down)
-    swapped = lax.ppermute(jnp.concatenate([block, from_above]), "pair", swap)
-    sibling, sibling_above = swapped[:rows], swapped[rows:]
+    sibling_above = lax.ppermute(from_above, "pair", swap)
 
     def best_over(query, keys):
         found = [block_best(query, k, slots, rows_total) for k in keys]
         return functools.reduce(jnp.maximum, found)
 
-    sibling_below = lax.ppermute(from_below, "pair", swap)
+    swapped = lax.ppermute(jnp.concatenate([block, from_below]), "pair", swap)
+    sibling, sibling_below = swapped[:rows], swapped[rows:]
     for_below = best_over(from_below, [from_above, sibling_above])
     from_chip_above = lax.ppermute(for_below, "pair", down)
     late = lax.optimization_barrier(

time: 110 us -> 111 us (level)
  waiting for transfers between devices: 5.75 us -> 8.08 us
  starting transfers between devices: 20.9 us -> 19.6 us
    ppermute x1, waiting for transfers between devices: 0.01 us -> 6.56 us  [pair_best(): from_below = lax.ppermute(block, 'pair', up)]
    ppermute x1, waiting for transfers between devices: 5.74 us -> 0.01 us  [pair_best(): from_above = lax.ppermute(block, 'pair', down)]
    ppermute x2, starting transfers between devices: 12.3 us -> 8.9 us  [the longest x1 6.98 us: pair_best(): swapped = lax.ppermute(jnp.concatenate([block, from_below]), 'pair', swap)]
    ppermute x1, starting transfers between devices: 2.03 us -> 4.09 us  [pair_best(): from_chip_above = lax.ppermute(for_below, 'pair', down)]
    ppermute x2, waiting for transfers between devices: 0.01 us -> 1.51 us  [the longest x1 1.51 us: pair_best(): sibling_above = lax.ppermute(from_above, 'pair', swap)]
    ppermute x1, starting transfers between devices: 1.92 us -> 3.2 us  [pair_best(): from_below = lax.ppermute(block, 'pair', up)]
    ppermute x1, starting transfers between devices: 4.64 us -> 3.36 us  [pair_best(): from_above = lax.ppermute(block, 'pair', down)]
  transfers between devices with their start and end apart: 5 -> 5, of which waited for: 1 -> 2; matrix products, arithmetic and copies ran while one was open for 3% -> 3% of each run, Pallas kernels for 0% -> 0%
where the time goes in v24:
time: 111 us; the launch traced here: 110 us
  blocking collectives  72.8 us (66%)
  starting transfers between devices  19.6 us (18%)
  waiting for transfers between devices  8.08 us (7%)
  other arithmetic  5.78 us (5%)
  matrix products  2.86 us (3%)
    all_to_all x1, blocking collectives, on_device(): lax.all_to_all(send_rows.reshape(groups, capacity, -1), 'dp', split_axis=...  51.3 us
    all_to_all x1, blocking collectives, on_device(): lax.all_to_all(lanes, 'dp', split_axis=0, concat_axis=0, tiled=True)  21.6 us
    ppermute x1, starting transfers between devices, pair_best(): swapped = lax.ppermute(jnp.concatenate([block, from_below]), 'pair', swap)  6.98 us
    ppermute x1, waiting for transfers between devices, pair_best(): from_below = lax.ppermute(block, 'pair', up)  6.56 us
    ppermute x1, starting transfers between devices, pair_best(): from_chip_above = lax.ppermute(for_below, 'pair', down)  4.09 us
    ppermute x1, starting transfers between devices, pair_best(): from_above = lax.ppermute(block, 'pair', down)  3.36 us
    ppermute x1, starting transfers between devices, pair_best(): from_below = lax.ppermute(block, 'pair', up)  3.2 us
    dot_general x8, matrix products, tile_best(): scores = jnp.dot(own_rows, other_rows.T, preferred_element_type=jnp.float32)  2.86 us
  transfers between devices with their start and end apart: 5, of which 2 were waited for; matrix products, arithmetic and copies ran while one was open for 3% of the time, Pallas kernels for 0%

profile of v24, /device:TPU:1, one launch (start us, length us, event | category | flops | bytes accessed | tf_op | source)
XLA Modules:
  0.0 110.2 jit_solution(14016701384670336076)
XLA Ops:
  0.0 0.7 and_select_fusion.11
  0.8 0.2 reduce_window_sum.11
  1.0 0.2 select_reduce_fusion.1
  1.2 1.1 fusion.8
  2.2 1.1 fusion.9
  3.4 1.3 %scatter_custom_fusion = bf16[256,1152]{1,0:T(8,128)(2,1)S(1)} fusion(s32[128]{0:T(128)S(1)} %get-tuple-element.33, bf16[128,128]{1,0:T(8,128)(2,1)S(1)} %select_convert_fusion, bf16[]{:T(256)} %constant.165, bf16[128,1024]{1,0:T(8,128)(2,1)S(1)} %fusion.9, bf16[]{:T(256)} %constant.146.clone.1), kind=kCustom, calls=%fused_computation.32 | custom fusion | flops 589824 | bytes 884740 | tf_op jit(solution)/shard_map/scatter | solution.py:97
  4.9 51.3 %all_to_all.17 = bf16[64,4,1152]{2,1,0:T(4,128)(2,1)S(1)} all-to-all(bf16[64,4,1152]{2,1,0:T(4,128)(2,1)S(1)} %reshape.321), channel_id=1, replica_groups=mesh['dp'=64,'pair'=8] {'dp'}, dimensions={0} | all-to-all | bytes 1179648 | tf_op jit(solution)/shard_map/all_to_all | solution.py:98
  56.6 3.2 %collective-permute-start = (bf16[272,1024]{1,0:T(8,128)(2,1)S(1)}, bf16[272,1024]{1,0:T(8,128)(2,1)S(1)}, u32[]{:S(2)}, u32[]{:S(2)}) collective-permute-start(bf16[272,1024]{1,0:T(8,128)(2,1)S(1)} %pad_maximum_fusion.1), channel_id=1, source_target_pairs={{0,2},{1,3},{2,4},{3,5},{4,6},{5,7},{6,0},{7,1},{8,10},{9,11},{10,... | collective-permute-start | bytes 1671176 | tf_op jit(solution)/shard_map/ppermute | solution.py:56
  59.8 3.4 %collective-permute-start.1 = (bf16[272,1024]{1,0:T(8,128)(2,1)S(1)}, bf16[272,1024]{1,0:T(8,128)(2,1)S(1)}, u32[]{:S(2)}, u32[]{:S(2)}) collective-permute-start(bf16[272,1024]{1,0:T(8,128)(2,1)S(1)} %pad_maximum_fusion.1), channel_id=1, source_target_pairs={{0,6},{1,7},{2,0},{3,1},{4,2},{5,3},{6,4},{7,5},{8,14},{9,15},{10,... | collective-permute-start | bytes 1671176 | tf_op jit(solution)/shard_map/ppermute | solution.py:57
  63.2 6.6 %collective-permute-done = bf16[272,1024]{1,0:T(8,128)(2,1)S(1)} collective-permute-done((bf16[272,1024]{1,0:T(8,128)(2,1)S(1)}, bf16[272,1024]{1,0:T(8,128)(2,1)S(1)}, u32[]{:S(2)}, u32[]{:S(2)}) %collective-permute-start) | collective-permute-done | bytes 557088 | tf_op jit(solution)/shard_map/ppermute | solution.py:56
  69.8 7.0 %collective-permute-start.2 = (bf16[544,1024]{1,0:T(8,128)(2,1)S(1)}, bf16[544,1024]{1,0:T(8,128)(2,1)S(1)}, u32[]{:S(2)}, u32[]{:S(2)}) collective-permute-start(bf16[544,1024]{1,0:T(8,128)(2,1)S(1)} %pad_maximum_fusion), channel_id=1, source_target_pairs={{0,1},{1,0},{2,3},{3,2},{4,5},{5,4},{6,7},{7,6},{8,9},{9,8},{10,11... | collective-permute-start | bytes 3342344 | tf_op jit(solution)/shard_map/ppermute | solution.py:64
  76.8 1.9 %collective-permute-start.3 = (bf16[272,1024]{1,0:T(8,128)(2,1)S(1)}, bf16[272,1024]{1,0:T(8,128)(2,1)S(1)}, u32[]{:S(2)}, u32[]{:S(2)}) collective-permute-start(bf16[272,1024]{1,0:T(8,128)(2,1)S(1)} %collective-permute-done.1), channel_id=1, source_target_pairs={{0,1},{1,0},{2,3},{3,2},{4,5},{5,4},{6,7},{7,6},{8,9},{9,8},{10,11... | collective-permute-start | bytes 1671176 | tf_op jit(solution)/shard_map/ppermute | solution.py:58
  78.8 0.4 fusion
  79.2 1.5 %collective-permute-done.3 = bf16[272,1024]{1,0:T(8,128)(2,1)S(1)} collective-permute-done((bf16[272,1024]{1,0:T(8,128)(2,1)S(1)}, bf16[272,1024]{1,0:T(8,128)(2,1)S(1)}, u32[]{:S(2)}, u32[]{:S(2)}) %collective-permute-start.3) | collective-permute-done | bytes 557088 | tf_op jit(solution)/shard_map/ppermute | solution.py:58
  80.7 0.4 fusion.1
  81.1 4.1 %collective-permute-start.4 = (f32[256]{0:T(256)S(1)}, f32[256]{0:T(256)S(1)}, u32[]{:S(2)}, u32[]{:S(2)}) collective-permute-start(f32[256]{0:T(256)S(1)} %max.21), channel_id=1, source_target_pairs={{0,6},{1,7},{2,0},{3,1},{4,2},{5,3},{6,4},{7,5},{8,14},{9,15},{10,... | collective-permute-start | bytes 3080 | tf_op jit(solution)/shard_map/ppermute | solution.py:67
  85.5 0.4 fusion.3
  85.8 0.4 fusion.4
  86.2 0.4 fusion.5
  86.6 0.4 fusion.6
  86.9 0.4 fusion.7
  87.3 0.4 fusion.2
  87.8 21.6 %all_to_all.18 = f32[64,1,128]{2,1,0:T(1,128)S(1)} all-to-all(f32[64,1,128]{2,1,0:T(1,128)S(1)} %bitcast.24), channel_id=1, replica_groups=mesh['dp'=64,'pair'=8] {'dp'}, dimensions={0} | all-to-all | bytes 65536 | tf_op jit(solution)/shard_map/all_to_all | solution.py:103
  109.5 0.7 select_reduce_fusion
  (43 shorter events, 1.3 us)
Async XLA Ops:
  56.6 13.1 %collective-permute-start = (bf16[272,1024]{1,0:T(8,128)(2,1)S(1)}, bf16[272,1024]{1,0:T(8,128)(2,1)S(1)}, u32[]{:S(2)}, u32[]{:S(2)}) collective-permute-start(bf16[272,1024]{1,0:T(8,128)(2,1)S(1)} %pad_maximum_fusion.1), channel_id=1, source_target_pairs={{0,2},{1,3},{2,4},{3,5},{4,6},{5,7},{6,0},{7,1},{8,10},{9,11},{10,... | collective-permute-start | bytes 1671176 | tf_op jit(solution)/shard_map/ppermute | solution.py:56
  59.8 17.0 %collective-permute-start.1 = (bf16[272,1024]{1,0:T(8,128)(2,1)S(1)}, bf16[272,1024]{1,0:T(8,128)(2,1)S(1)}, u32[]{:S(2)}, u32[]{:S(2)}) collective-permute-start(bf16[272,1024]{1,0:T(8,128)(2,1)S(1)} %pad_maximum_fusion.1), channel_id=1, source_target_pairs={{0,6},{1,7},{2,0},{3,1},{4,2},{5,3},{6,4},{7,5},{8,14},{9,15},{10,... | collective-permute-start | bytes 1671176 | tf_op jit(solution)/shard_map/ppermute | solution.py:57
  69.8 15.4 %collective-permute-start.2 = (bf16[544,1024]{1,0:T(8,128)(2,1)S(1)}, bf16[544,1024]{1,0:T(8,128)(2,1)S(1)}, u32[]{:S(2)}, u32[]{:S(2)}) collective-permute-start(bf16[544,1024]{1,0:T(8,128)(2,1)S(1)} %pad_maximum_fusion), channel_id=1, source_target_pairs={{0,1},{1,0},{2,3},{3,2},{4,5},{5,4},{6,7},{7,6},{8,9},{9,8},{10,11... | collective-permute-start | bytes 3342344 | tf_op jit(solution)/shard_map/ppermute | solution.py:64
  76.8 3.9 %collective-permute-start.3 = (bf16[272,1024]{1,0:T(8,128)(2,1)S(1)}, bf16[272,1024]{1,0:T(8,128)(2,1)S(1)}, u32[]{:S(2)}, u32[]{:S(2)}) collective-permute-start(bf16[272,1024]{1,0:T(8,128)(2,1)S(1)} %collective-permute-done.1), channel_id=1, source_target_pairs={{0,1},{1,0},{2,3},{3,2},{4,5},{5,4},{6,7},{7,6},{8,9},{9,8},{10,11... | collective-permute-start | bytes 1671176 | tf_op jit(solution)/shard_map/ppermute | solution.py:58
  81.1 6.6 %collective-permute-start.4 = (f32[256]{0:T(256)S(1)}, f32[256]{0:T(256)S(1)}, u32[]{:S(2)}, u32[]{:S(2)}) collective-permute-start(f32[256]{0:T(256)S(1)} %max.21), channel_id=1, source_target_pairs={{0,6},{1,7},{2,0},{3,1},{4,2},{5,3},{6,4},{7,5},{8,14},{9,15},{10,... | collective-permute-start | bytes 3080 | tf_op jit(solution)/shard_map/ppermute | solution.py:67
